TPU v7x, 128 devices: a whole 4x4x4 slice. The times are simulated.
128 devices in a mesh: ex: 8 (over z, core), sh: 16 (over y, x).
Axes of the slice: x: 4, y: 4, z: 4, core: 2. Of those that a mesh axis runs over, the one named last changes fastest.
Arguments:
- hidden_in: bfloat16 [12288, 2304], P(('ex', 'sh')), may hold values from -3 to 3
- queries: bfloat16 [12288, 2304], P(('ex', 'sh')), may hold values from -2.5 to 2.5
- new_keys: bfloat16 [12288, 2304], P(('ex', 'sh')), may hold values from -2.5 to 2.5
- new_values: bfloat16 [12288, 2304], P(('ex', 'sh')), may hold values from -6 to 6
- key_pool: bfloat16 [131072, 2304], P(('ex', 'sh')), may hold values from -2.5 to 2.5
- value_pool: bfloat16 [131072, 2304], P(('ex', 'sh')), may hold values from -6 to 6
- page_order: int32 [128, 64], P(('ex', 'sh')), may hold values from 0 to 63, each once within a row
- new_lengths: int32 [128, 4], P(('ex', 'sh')), may hold values from 1 to 48, 96 in all within a row
- context_lengths: int32 [128, 4], P(('ex', 'sh')), may hold values from 1 to 256, 512 in all within a row
- route_ids: int32 [12288, 2], P(('ex', 'sh')), may hold values from 0 to 7, all different within a row; in each aligned block of 96 rows (0 to 95, 96 to 191, ...) at most 32 rows name the same one
- norm_gain: bfloat16 [2304], replicated, may hold values from 0.25 to 1.75
- router_weight: bfloat16 [2304, 8], replicated, may hold values from -0.125 to 0.125
- gate_weight: bfloat16 [8, 2304, 5760], P('ex', None, 'sh'), may hold values from -0.125 to 0.125
- up_weight: bfloat16 [8, 2304, 5760], P('ex', None, 'sh'), may hold values from -0.125 to 0.125
- down_weight: bfloat16 [8, 5760, 2304], P('ex', 'sh'), may hold values from -0.078125 to 0.078125
- out_gain: bfloat16 [2304], replicated, may hold values from 0.25 to 1.75
Outputs:
- layer_out: bfloat16 [12288, 2304], P(('ex', 'sh'))
Inputs may be any that keep to these rules, and one draw needn't show every extreme that they name: `page_order`: each row names the pages 0 to 63 of one device's pool once each; request r owns entries r * 16 to (r+1) * 16 - 1 of its row, in order. `new_lengths`: each row sums to 96; its largest entry is 48. `context_lengths`: each row sums to 512; its largest entry is 256. `route_ids`: A row names two different experts. Among the 96 rows of one device no expert is named by more than 32 rows, and in some devices' rows one expert is named by exactly 32.
All inputs are finite; a program needn't handle non-finite values.
Results may differ from a plain program's by a relative error of at most 0.015.
Values may be sent and summed in bfloat16 or wider, within the bound.
No kernel may reach another device: no remote copies, remote signals or barrier semaphores. Data moves between devices by JAX's collectives and lax.ppermute only.
A program may use at most 128 MiB of HBM per device.

v0:
```python
import jax
import jax.numpy as jnp
from jax import lax
from jax.sharding import PartitionSpec as P

HEADS = 36
HEAD_DIM = 64
EXPERTS = 8
PAGE = 16
MOST = 32


def rms_scale(values, gain):
    mean_square = jnp.mean(values * values, axis=-1, keepdims=True)
    return values * lax.rsqrt(mean_square + 1e-05) * gain.astype(jnp.float32)


def route_probs(normed, router_weight, route_ids):
    logits = jnp.dot(normed, router_weight, preferred_element_type=jnp.float32)
    expert_range = jnp.arange(router_weight.shape[1], dtype=jnp.int32)
    picked = jnp.sum(
        jnp.where(route_ids[:, :, None] == expert_range[None, None, :], logits[:, None, :], 0.0),
        axis=2,
    )
    raised = jnp.exp(picked)
    return raised / jnp.sum(raised, axis=1, keepdims=True)


def attend(
    hidden_rows,
    query_rows,
    key_rows,
    value_rows,
    key_store,
    value_store,
    page_row,
    new_row_lengths,
    context_row_lengths,
):
    row_count = query_rows.shape[0]
    store_count = key_store.shape[0]
    requests = new_row_lengths.shape[0]
    table = page_row.reshape(requests, -1)
    per_request = table.shape[1]
    ends = jnp.cumsum(new_row_lengths)
    row_index = jnp.arange(row_count, dtype=jnp.int32)
    owner = jnp.sum((row_index[:, None] >= ends[None, :]).astype(jnp.int32), axis=1)
    request_index = jnp.arange(requests, dtype=jnp.int32)
    row_owner = owner[:, None] == request_index[None, :]
    token_index = jnp.arange(store_count, dtype=jnp.int32)
    token_page = token_index // PAGE
    token_offset = token_index % PAGE
    matched = table[:, :, None] == token_page[None, None, :]
    page_slot = jnp.arange(per_request, dtype=jnp.int32) * PAGE
    position = (
        jnp.sum(jnp.where(matched, page_slot[None, :, None], 0), axis=1) + token_offset[None, :]
    )
    visible = jnp.any(matched, axis=1) & (position < context_row_lengths[:, None])
    store_mask = jnp.any(row_owner[:, :, None] & visible[None, :, :], axis=1)
    fresh_mask = (owner[:, None] == owner[None, :]) & (row_index[None, :] <= row_index[:, None])
    allowed = jnp.concatenate([store_mask, fresh_mask], axis=1)
    keys = jnp.concatenate([key_store, key_rows], axis=0).reshape(-1, HEADS, HEAD_DIM)
    values = jnp.concatenate([value_store, value_rows], axis=0).reshape(-1, HEADS, HEAD_DIM)
    query_heads = query_rows.reshape(row_count, HEADS, HEAD_DIM)
    scores = jnp.einsum(
        "rhd,khd->hrk", query_heads, keys, preferred_element_type=jnp.float32
    ) * HEAD_DIM ** (-0.5)
    raised = jnp.where(allowed[None, :, :], jnp.exp(scores), 0.0)
    weights = (raised / jnp.sum(raised, axis=2, keepdims=True)).astype(jnp.bfloat16)
    attended = jnp.einsum(
        "hrk,khd->rhd", weights, values, preferred_element_type=jnp.float32
    ).reshape(row_count, HEADS * HEAD_DIM)
    return hidden_rows.astype(jnp.float32) + attended


def per_device(
    hidden_in,
    queries,
    new_keys,
    new_values,
    key_pool,
    value_pool,
    page_order,
    new_lengths,
    context_lengths,
    route_ids,
    norm_gain,
    router_weight,
    gate_weight,
    up_weight,
    down_weight,
    out_gain,
):
    groups = lax.axis_size("ex")
    local_experts = gate_weight.shape[0]
    width = hidden_in.shape[1]
    row_count = hidden_in.shape[0]
    resid = attend(
        hidden_in,
        queries,
        new_keys,
        new_values,
        key_pool,
        value_pool,
        page_order[0],
        new_lengths[0],
        context_lengths[0],
    )
    normed = rms_scale(resid, norm_gain).astype(jnp.bfloat16)
    route_weights = route_probs(normed, router_weight, route_ids)
    top_count = route_ids.shape[1]
    entries = route_ids.reshape(-1)
    expert_range = jnp.arange(EXPERTS, dtype=jnp.int32)
    onehot = (entries[:, None] == expert_range[None, :]).astype(jnp.int32)
    before = jnp.cumsum(onehot, axis=0) - onehot
    slot_index = jnp.sum(before * onehot, axis=1)
    target = entries * MOST + slot_index
    entry_rows = jnp.arange(entries.shape[0], dtype=jnp.int32) // top_count
    source_row = jnp.zeros((EXPERTS * MOST,), jnp.int32).at[target].set(entry_rows)
    filled = jnp.zeros((EXPERTS * MOST,), jnp.bool_).at[target].set(True)
    outgoing = jnp.where(filled[:, None], normed[source_row], jnp.zeros((), jnp.bfloat16)).reshape(
        EXPERTS, MOST, width
    )
    arrived = lax.all_to_all(outgoing, "ex", split_axis=0, concat_axis=0, tiled=True).reshape(
        groups, local_experts, MOST, width
    )
    arrived_rows = lax.all_gather(arrived, "sh", axis=0, tiled=True)
    gate_value = jnp.einsum(
        "gemd,edf->gemf", arrived_rows, gate_weight, preferred_element_type=jnp.float32
    )
    up_value = jnp.einsum(
        "gemd,edf->gemf", arrived_rows, up_weight, preferred_element_type=jnp.float32
    )
    hidden = (jax.nn.silu(gate_value) * up_value).astype(jnp.bfloat16)
    summed = lax.psum_scatter(
        jnp.einsum(
            "gemf,efd->gemd", hidden, down_weight, preferred_element_type=jnp.float32
        ).astype(jnp.bfloat16),
        "sh",
        scatter_dimension=0,
        tiled=True,
    )
    returned = lax.all_to_all(
        summed.reshape(EXPERTS, MOST, width), "ex", split_axis=0, concat_axis=0, tiled=True
    )
    flat_results = returned.reshape(EXPERTS * MOST, width)
    picked = flat_results[target].reshape(row_count, top_count, width)
    mixed = resid + jnp.sum(route_weights[:, :, None] * picked.astype(jnp.float32), axis=1)
    return rms_scale(mixed, out_gain).astype(jnp.bfloat16)


def solution(mesh):
    placed = (
        P(("ex", "sh"), None),
        P(("ex", "sh"), None),
        P(("ex", "sh"), None),
        P(("ex", "sh"), None),
        P(("ex", "sh"), None),
        P(("ex", "sh"), None),
        P(("ex", "sh"), None),
        P(("ex", "sh"), None),
        P(("ex", "sh"), None),
        P(("ex", "sh"), None),
        P(),
        P(),
        P("ex", None, "sh"),
        P("ex", None, "sh"),
        P("ex", "sh", None),
        P(),
    )
    return jax.shard_map(
        per_device, mesh=mesh, in_specs=placed, out_specs=P(("ex", "sh"), None), check_vma=False
    )
```

profile of v0, /device:TPU:1, one launch (start us, length us, event | category | flops | bytes accessed | tf_op | source)
XLA Modules:
  0.0 542.8 jit_solution(4539421278832399427)
XLA Ops:
  6.5 0.0 copy-start
  6.6 0.9 reduce-window.18
  7.5 0.1 convert_reduce_fusion
  7.6 0.1 fusion.18
  7.7 0.7 broadcast_multiply_fusion
  8.4 0.8 copy.50
  9.2 0.5 broadcast.230
  9.7 1.3 reduce.5
  11.0 0.1 eq.85
  11.1 0.1 compare_reduce_fusion
  11.2 0.1 fusion.17
  11.3 0.7 convert_element_type.49
  12.0 0.1 copy.49
  12.1 0.1 mul.97
  12.3 0.1 eq.95
  12.4 0.6 reduce-window.19
  13.0 0.2 slice_reduce_fusion
  13.3 0.1 add_bitcast_fusion
  13.4 1.2 scatter_custom_fusion.1
  14.6 1.2 scatter_custom_fusion
  15.9 0.1 broadcast_in_dim.96
  16.0 1.3 copy.46
  17.3 5.1 pad_maximum_fusion.1
  22.4 8.6 %copy.45 = bf16[1120,2304]{0,1:T(8,128)(2,1)} copy(bf16[1120,2304]{1,0:T(8,128)(2,1)} %pad_maximum_fusion.1) | data formatting | bytes 10321920 | tf_op jit(solution)/shard_map/concatenate | solution.py:62
  31.0 0.0 copy-done.5
  31.0 4.9 pad_maximum_fusion
  35.9 8.5 %copy.44 = bf16[1120,2304]{0,1:T(8,128)(2,1)} copy(bf16[1120,2304]{1,0:T(8,128)(2,1)} %pad_maximum_fusion) | data formatting | bytes 10321920 | tf_op jit(solution)/shard_map/concatenate | solution.py:63
  44.5 0.1 fusion.19
  44.5 0.2 and_reduce_fusion
  44.8 11.1 %fusion.2 = f32[36,96,1120]{2,1,0:T(8,128)} fusion(bf16[1120,36,64]{0,2,1:T(8,128)(2,1)} %bitcast.94, bf16[96,36,64]{0,2,1:T(8,128)(2,1)S(1)} %bitcast.97, pred[96,1120]{1,0:T(8,128)(4,1)S(1)} %pad_add_fusion), kind=kOutput, calls=%fused_computation.8 | convolution fusion | flops 503193600 | bytes 21193728 | tf_op jit(solution)/shard_map/rhd,khd->hrk/dot_general | solution.py:65
  55.9 15.5 %fusion.9 = f32[36,64,96]{2,1,0:T(8,128)} fusion(bf16[1120,36,64]{0,2,1:T(8,128)(2,1)} %bitcast.95, f32[36,96,1120]{2,1,0:T(8,128)} %fusion.2), kind=kOutput, calls=%fused_computation.21 | convolution fusion | flops 503198176 | bytes 21528576 | tf_op jit(solution)/shard_map/hrk,khd->rhd/dot_general | solution.py:70
  71.4 1.6 copy.47
  73.0 0.2 multiply_reduce_fusion.2
  73.2 0.2 multiply_convert_fusion.1
  73.4 2.4 gather_fusion
  75.8 1.4 broadcast_select_fusion
  77.3 23.1 %all_to_all.10 = bf16[8,32,2304]{2,1,0:T(8,128)(2,1)S(1)} all-to-all(bf16[8,32,2304]{2,1,0:T(8,128)(2,1)S(1)} %broadcast_select_fusion), channel_id=1, replica_groups=mesh['ex'=8,'sh'=16] {'ex'}, dimensions={0} | all-to-all | bytes 2359296 | tf_op jit(solution)/shard_map/all_to_all | solution.py:124
  100.4 1.7 copy.51
  102.1 0.0 all-gather.3.cloned.1.call-update
  102.1 0.2 all-reduce.4.cloned.1.call-start
  102.3 121.2 %all-gather.3.cloned.1.call-done = bf16[128,32,2304]{2,0,1:T(8,128)(2,1)} async-done(((bf16[8,32,2304]{2,0,1:T(8,128)(2,1)}), bf16[128,32,2304]{2,0,1:T(8,128)(2,1)}) %all-gather.3.cloned.1.call-update) | async-done | bytes 18874384 | tf_op jit(solution)/shard_map/all_gather | solution.py:127
  223.6 12.9 %fusion.12 = f32[128,32,360]{0,2,1:T(8,128)} fusion(bf16[128,32,2304]{2,0,1:T(8,128)(2,1)} %all-gather.3.cloned.1.call-done, bf16[1,2304,360]{1,2,0:T(8,128)(2,1)} %param.29), kind=kOutput, calls=%fused_computation.25 | convolution fusion | flops 6794772480 | bytes 26431488 | tf_op jit(solution)/shard_map/gemd,edf->gemf/dot_general | solution.py:131
  236.4 0.0 copy-done
  236.4 24.0 %fusion.3 = bf16[128,1,32,2304]{3,0,2,1:T(8,128)(2,1)} fusion(bf16[1,360,2304]{2,1,0:T(8,128)(2,1)S(1)} %copy-done, f32[128,32,360]{0,2,1:T(8,128)} %fusion.12, bf16[128,32,2304]{2,0,1:T(8,128)(2,1)} %all-gather.3.cloned.1.call-done, bf16[1,2304,360]{1,2,0:T(8,128)(2,1)} %param.28), kind=kOutput, calls=%fused_computation.9 | convolution fusion | flops 13607829504 | bytes 46964736 | tf_op jit(solution)/shard_map/gemf,efd->gemd/dot_general | solution.py:136
  260.4 0.0 all-reduce.4.cloned.1.call-update
  260.5 0.0 copy-start.8
  260.5 0.0 copy-start.6
  260.5 0.0 copy-start.7
  260.5 0.6 copy-done.10
  261.1 0.6 dynamic-slice
  262.3 238.8 %all-reduce.4.cloned.1.call-done = bf16[128,1,32,2304]{3,0,2,1:T(8,128)(2,1)} async-done(((bf16[128,1,32,2304]{3,0,2,1:T(8,128)(2,1)}), bf16[128,1,32,2304]{3,0,2,1:T(8,128)(2,1)}) %all-reduce.4.cloned.1.call-update) | async-done | bytes 18874384
  501.2 1.3 dynamic-slice_bitcast_fusion
  502.5 1.2 copy.52
  503.7 5.3 all-to-all-start.1
  509.0 0.0 copy-done.8
  509.0 0.2 fusion.35
  509.2 0.1 select_reduce_fusion
  509.3 0.1 copy.48
  509.4 15.9 %all-to-all-done.1 = bf16[8,32,2304]{2,1,0:T(8,128)(2,1)S(1)} async-done(((bf16[8,32,2304]{2,1,0:T(8,128)(2,1)}), bf16[8,32,2304]{2,1,0:T(8,128)(2,1)S(1)}, u32[]{:S(2)}, u32[]{:S(2)}) %all-to-all-start.1) | async-done | bytes 1179680 | tf_op jit(solution)/shard_map/all_to_all | solution.py:143
  525.3 2.1 gather_fusion.1
  527.5 3.3 reshape.258
  530.7 4.0 multiply_reduce_fusion
  534.7 0.3 multiply_reduce_fusion.1
  535.0 1.0 multiply_convert_fusion
  (36 shorter events, 0.2 us)
Async XLA Ops:
  6.5 229.9 %copy-start = (bf16[1,360,2304]{2,1,0:T(8,128)(2,1)S(1)}, bf16[1,360,2304]{2,1,0:T(8,128)(2,1)}, u32[]{:S(2)}) copy-start(bf16[1,360,2304]{2,1,0:T(8,128)(2,1)} %param.30) | copy-start | bytes 4976644
  6.5 217.0 %all-gather.3.cloned.1.call-start = ((), (), s32[]{:S(2)}) async-start(), calls=%async_computation.2 | async-start | bytes 20054016 | tf_op jit(solution)/shard_map/all_gather | solution.py:127
  22.4 8.6 %copy-start.5 = (bf16[96,2304]{1,0:T(8,128)(2,1)S(1)}, bf16[96,2304]{1,0:T(8,128)(2,1)}, u32[]{:S(2)}) copy-start(bf16[96,2304]{1,0:T(8,128)(2,1)} %param.19) | copy-start | bytes 1327108
  35.9 8.5 %copy-start.9 = (s32[1,4]{1,0:T(1,128)S(1)}, s32[1,4]{1,0:T(1,128)}, u32[]{:S(2)}) copy-start(s32[1,4]{1,0:T(1,128)} %param.24) | copy-start | bytes 52
  55.9 17.1 %copy-start.3 = (bf16[96,2304]{1,0:T(8,128)(2,1)S(1)}, bf16[96,2304]{1,0:T(8,128)(2,1)}, u32[]{:S(2)}) copy-start(bf16[96,2304]{1,0:T(8,128)(2,1)} %param.16) | copy-start | bytes 1327108
  73.0 2.8 copy-start.1
  102.1 399.1 %all-reduce.4.cloned.1.call-start = ((), (), s32[]{:S(2)}) async-start(), calls=%async_computation.3 | async-start | bytes 37748736
  260.4 0.7 copy-start.10
  260.5 248.5 %copy-start.8 = (bf16[2304]{0:T(1024)(128)(2,1)S(1)}, bf16[2304]{0:T(1024)(128)(2,1)}, u32[]{:S(2)}) copy-start(bf16[2304]{0:T(1024)(128)(2,1)} %param.31) | copy-start | bytes 13828
  260.5 248.5 %copy-start.6 = (bf16[2304,8]{0,1:T(8,128)(2,1)S(1)}, bf16[2304,8]{0,1:T(8,128)(2,1)}, u32[]{:S(2)}) copy-start(bf16[2304,8]{0,1:T(8,128)(2,1)} %param.27) | copy-start | bytes 110596
  260.5 248.7 %copy-start.7 = (s32[96,2]{0,1:T(2,128)S(1)}, s32[96,2]{0,1:T(2,128)}, u32[]{:S(2)}) copy-start(s32[96,2]{0,1:T(2,128)} %param.25) | copy-start | bytes 2308
  503.7 21.6 %all-to-all-start.1 = ((bf16[8,32,2304]{2,1,0:T(8,128)(2,1)}), bf16[8,32,2304]{2,1,0:T(8,128)(2,1)S(1)}, u32[]{:S(2)}, u32[]{:S(2)}) async-start(bf16[8,32,2304]{2,1,0:T(8,128)(2,1)} %copy.52), calls=%async_computation.1 | async-start | bytes 2359296 | tf_op jit(solution)/shard_map/all_to_all | solution.py:143
  527.5 7.3 %copy-start.2 = (f32[96,2304]{1,0:T(8,128)S(1)}, f32[96,2304]{1,0:T(8,128)}, u32[]{:S(2)}) copy-start(f32[96,2304]{1,0:T(8,128)} %copy-done.1) | copy-start | bytes 2654212
  527.5 7.3 %copy-start.4 = (bf16[96,2304]{1,0:T(8,128)(2,1)S(1)}, bf16[96,2304]{1,0:T(8,128)(2,1)}, u32[]{:S(2)}) copy-start(bf16[96,2304]{1,0:T(8,128)(2,1)} %param.16) | copy-start | bytes 1327108
Sparse Core Ops, SparseCore 0:
  102.2 121.2 all-gather.2
  260.6 240.5 all-reduce.3
where the time goes:
time: 544 us; the launch traced here: 543 us
  waiting for transfers between devices  376 us (69%)
  matrix products  63.6 us (12%)
  local copies, waits for them, and re-layouts  37.9 us (7%)
  blocking collectives  23.1 us (4%)
  other arithmetic  22.3 us (4%)
  between operations  14.3 us (3%)
  starting transfers between devices  5.49 us (1%)
    unnamed x3, waiting for transfers between devices  239 us
    all_gather x1, waiting for transfers between devices, per_device(): arrived_rows = lax.all_gather(arrived, 'sh', axis=0, tiled=True)  121 us
    dot_general x1, matrix products, per_device(): jnp.einsum('gemf,efd->gemd', hidden, down_weight, preferred_element_type=...  24 us
    all_to_all x1, blocking collectives, per_device(): lax.all_to_all(outgoing, 'ex', split_axis=0, concat_axis=0, tiled=True)  23.1 us
    all_to_all x1, waiting for transfers between devices, per_device(): lax.all_to_all(summed.reshape(EXPERTS, MOST, width), 'ex', split_axis=0,...  15.9 us
    dot_general x1, matrix products, attend(): jnp.einsum('hrk,khd->rhd', weights, values, preferred_element_type=jnp.fl...  15.5 us
    dot_general x1, matrix products, per_device(): jnp.einsum('gemd,edf->gemf', arrived_rows, up_weight, preferred_element_t...  12.9 us
    dot_general x1, matrix products, attend(): jnp.einsum('rhd,khd->hrk', query_heads, keys, preferred_element_type=jnp....  11.1 us
  transfers between devices with their start and end apart: 3, of which 3 were waited for; matrix products, arithmetic and copies ran while one was open for 0% of the time, Pallas kernels for 0%

commit v1 on v0

--- a/solution.py
+++ b/solution.py
@@ -122,24 +122,14 @@
         EXPERTS, MOST, width
     )
     arrived = lax.all_to_all(outgoing, "ex", split_axis=0, concat_axis=0, tiled=True).reshape(
-        groups, local_experts, MOST, width
+        groups * MOST, width
     )
     arrived_rows = lax.all_gather(arrived, "sh", axis=0, tiled=True)
-    gate_value = jnp.einsum(
-        "gemd,edf->gemf", arrived_rows, gate_weight, preferred_element_type=jnp.float32
-    )
-    up_value = jnp.einsum(
-        "gemd,edf->gemf", arrived_rows, up_weight, preferred_element_type=jnp.float32
-    )
+    gate_value = jnp.dot(arrived_rows, gate_weight[0], preferred_element_type=jnp.float32)
+    up_value = jnp.dot(arrived_rows, up_weight[0], preferred_element_type=jnp.float32)
     hidden = (jax.nn.silu(gate_value) * up_value).astype(jnp.bfloat16)
-    summed = lax.psum_scatter(
-        jnp.einsum(
-            "gemf,efd->gemd", hidden, down_weight, preferred_element_type=jnp.float32
-        ).astype(jnp.bfloat16),
-        "sh",
-        scatter_dimension=0,
-        tiled=True,
-    )
+    partial = jnp.dot(hidden, down_weight[0], preferred_element_type=jnp.float32).astype(jnp.bfloat16)
+    summed = lax.psum_scatter(partial, "sh", scatter_dimension=0, tiled=True)
     returned = lax.all_to_all(
         summed.reshape(EXPERTS, MOST, width), "ex", split_axis=0, concat_axis=0, tiled=True
     )

time: 544 us -> 421 us (0.77)
  waiting for transfers between devices: 376 us -> 258 us
    unnamed x3 -> x2, waiting for transfers between devices: 239 us -> 0.03 us
    reduce_scatter x0 -> x1, waiting for transfers between devices: none -> 121 us  [per_device(): summed = lax.psum_scatter(partial, 'sh', scatter_dimension=0, tiled=True)]
where the time goes in v1:
time: 421 us; the launch traced here: 420 us
  waiting for transfers between devices  258 us (61%)
  matrix products  65 us (15%)
  local copies, waits for them, and re-layouts  32.5 us (8%)
  blocking collectives  23.2 us (6%)
  other arithmetic  22.3 us (5%)
  between operations  13.6 us (3%)
  starting transfers between devices  5.8 us (1%)
    all_gather x1, waiting for transfers between devices, per_device(): arrived_rows = lax.all_gather(arrived, 'sh', axis=0, tiled=True)  121 us
    reduce_scatter x1, waiting for transfers between devices, per_device(): summed = lax.psum_scatter(partial, 'sh', scatter_dimension=0, tiled=True)  121 us
    dot_general x1, matrix products, per_device(): jnp.dot(hidden, down_weight[0], preferred_element_type=jnp.float32)  25.2 us
    all_to_all x1, blocking collectives, per_device(): lax.all_to_all(outgoing, 'ex', split_axis=0, concat_axis=0, tiled=True)  23.2 us
    all_to_all x1, waiting for transfers between devices, per_device(): lax.all_to_all(summed.reshape(EXPERTS, MOST, width), 'ex', split_axis=0,...  15.9 us
    dot_general x1, matrix products, attend(): jnp.einsum('hrk,khd->rhd', weights, values, preferred_element_type=jnp.fl...  15.5 us
    dot_general x1, matrix products, per_device(): jnp.dot(arrived_rows, gate_weight[0], preferred_element_type=jnp.float32)  13 us
    dot_general x1, matrix products, attend(): jnp.einsum('rhd,khd->hrk', query_heads, keys, preferred_element_type=jnp....  11.1 us
  transfers between devices with their start and end apart: 3, of which 3 were waited for; matrix products, arithmetic and copies ran while one was open for 0% of the time, Pallas kernels for 0%

profile of v1, /device:TPU:1, one launch (start us, length us, event | category | flops | bytes accessed | tf_op | source)
XLA Modules:
  0.0 420.2 jit_solution(9019461184095956827)
XLA Ops:
  6.5 0.0 copy-start
  6.5 0.0 all-gather.2.cloned.1.call-start
  6.6 0.9 reduce-window.18
  7.5 0.1 convert_reduce_fusion
  7.6 0.1 fusion.14
  7.7 0.7 broadcast_multiply_fusion
  8.4 0.8 copy.37
  9.2 0.5 broadcast.230
  9.7 1.3 reduce.5
  11.0 0.1 eq.85
  11.1 0.1 compare_reduce_fusion
  11.2 0.1 fusion.13
  11.3 0.7 convert_element_type.40
  12.0 0.1 copy.36
  12.1 0.1 mul.97
  12.3 0.1 eq.95
  12.4 0.6 reduce-window.19
  13.0 0.2 slice_reduce_fusion
  13.3 0.1 add_bitcast_fusion
  13.4 1.2 scatter_custom_fusion.1
  14.6 1.2 scatter_custom_fusion
  15.9 0.1 broadcast_in_dim.96
  16.0 1.3 copy.33
  17.3 5.1 %pad_maximum_fusion.1 = bf16[1120,2304]{1,0:T(8,128)(2,1)} fusion(bf16[96,2304]{1,0:T(8,128)(2,1)} %param.18, bf16[1024,2304]{1,0:T(8,128)(2,1)} %param.20), kind=kLoop, calls=%fused_computation.14 | loop fusion | flops 10321920 | bytes 10321920 | tf_op jit(solution)/shard_map/concatenate | solution.py:62
  22.4 8.6 %copy.32 = bf16[1120,2304]{0,1:T(8,128)(2,1)} copy(bf16[1120,2304]{1,0:T(8,128)(2,1)} %pad_maximum_fusion.1) | data formatting | bytes 10321920 | tf_op jit(solution)/shard_map/concatenate | solution.py:62
  31.0 0.0 copy-done.5
  31.0 4.9 %pad_maximum_fusion = bf16[1120,2304]{1,0:T(8,128)(2,1)} fusion(bf16[96,2304]{1,0:T(8,128)(2,1)S(1)} %copy-done.5, bf16[1024,2304]{1,0:T(8,128)(2,1)} %param.21), kind=kLoop, calls=%fused_computation.13 | loop fusion | flops 10321920 | bytes 10321920 | tf_op jit(solution)/shard_map/concatenate | solution.py:63
  35.9 8.5 %copy.31 = bf16[1120,2304]{0,1:T(8,128)(2,1)} copy(bf16[1120,2304]{1,0:T(8,128)(2,1)} %pad_maximum_fusion) | data formatting | bytes 10321920 | tf_op jit(solution)/shard_map/concatenate | solution.py:63
  44.5 0.0 copy-done.9
  44.5 0.1 fusion.15
  44.5 0.2 and_reduce_fusion
  44.8 11.1 %fusion.2 = f32[36,96,1120]{2,1,0:T(8,128)} fusion(bf16[1120,36,64]{0,2,1:T(8,128)(2,1)} %bitcast.47, bf16[96,36,64]{0,2,1:T(8,128)(2,1)S(1)} %bitcast.51, pred[96,1120]{1,0:T(8,128)(4,1)S(1)} %pad_add_fusion), kind=kOutput, calls=%fused_computation.8 | convolution fusion | flops 503193600 | bytes 21193728 | tf_op jit(solution)/shard_map/rhd,khd->hrk/dot_general | solution.py:65
  55.9 15.5 %fusion.5 = f32[36,64,96]{2,1,0:T(8,128)} fusion(bf16[1120,36,64]{0,2,1:T(8,128)(2,1)} %bitcast.48, f32[36,96,1120]{2,1,0:T(8,128)} %fusion.2), kind=kOutput, calls=%fused_computation.15 | convolution fusion | flops 503198176 | bytes 21528576 | tf_op jit(solution)/shard_map/hrk,khd->rhd/dot_general | solution.py:70
  71.4 1.6 copy.34
  73.0 0.0 copy-done.3
  73.0 0.0 copy-start.1
  73.0 0.2 multiply_reduce_fusion.2
  73.2 0.2 multiply_convert_fusion.1
  73.4 2.4 gather_fusion
  75.8 0.0 copy-done.1
  75.8 1.4 broadcast_select_fusion
  77.3 23.2 %all_to_all.10 = bf16[8,32,2304]{2,1,0:T(8,128)(2,1)} all-to-all(bf16[8,32,2304]{2,1,0:T(8,128)(2,1)S(1)} %broadcast_select_fusion), channel_id=1, replica_groups=mesh['ex'=8,'sh'=16] {'ex'}, dimensions={0} | all-to-all | bytes 2359296 | tf_op jit(solution)/shard_map/all_to_all | solution.py:124
  100.5 0.0 all-gather.2.cloned.1.call-update
  100.5 0.2 reduce-scatter.2.cloned.1.call-start
  100.7 121.2 %all-gather.2.cloned.1.call-done = bf16[4096,2304]{1,0:T(8,128)(2,1)} async-done(((bf16[256,2304]{1,0:T(8,128)(2,1)}), bf16[4096,2304]{1,0:T(8,128)(2,1)}) %all-gather.2.cloned.1.call-update) | async-done | bytes 18874384 | tf_op jit(solution)/shard_map/all_gather | solution.py:127
  222.0 13.0 %fusion.10 = f32[4096,360]{0,1:T(8,128)} fusion(bf16[4096,2304]{1,0:T(8,128)(2,1)} %all-gather.2.cloned.1.call-done, bf16[1,2304,360]{1,2,0:T(8,128)(2,1)} %param.28), kind=kOutput, calls=%fused_computation.19 | convolution fusion | flops 6794772480 | bytes 26431488 | tf_op jit(solution)/shard_map/dot_general | solution.py:128
  235.0 0.0 copy-done
  235.0 25.2 %convolution_convert_fusion = bf16[4096,2304]{1,0:T(8,128)(2,1)} fusion(bf16[1,360,2304]{2,1,0:T(8,128)(2,1)S(1)} %copy-done, bf16[4096,2304]{1,0:T(8,128)(2,1)} %all-gather.2.cloned.1.call-done, f32[4096,360]{0,1:T(8,128)} %fusion.10, bf16[1,2304,360]{1,2,0:T(8,128)(2,1)} %param.29), kind=kOutput, calls=%fused_computation.4 | convolution fusion | flops 13607829504 | bytes 46964736 | tf_op jit(solution)/shard_map/dot_general | solution.py:131
  260.2 0.0 reduce-scatter.2.cloned.1.call-update
  260.2 120.5 %reduce-scatter.2.cloned.1.call-done = bf16[256,2304]{1,0:T(8,128)(2,1)} async-done(((bf16[4096,2304]{1,0:T(8,128)(2,1)}), bf16[256,2304]{1,0:T(8,128)(2,1)}) %reduce-scatter.2.cloned.1.call-update) | async-done | bytes 1179664 | tf_op jit(solution)/shard_map/reduce_scatter | solution.py:132
  380.7 5.6 %all-to-all-start.1 = ((bf16[8,32,2304]{2,1,0:T(8,128)(2,1)}), bf16[8,32,2304]{2,1,0:T(8,128)(2,1)S(1)}, u32[]{:S(2)}, u32[]{:S(2)}) async-start(bf16[8,32,2304]{2,1,0:T(8,128)(2,1)} %bitcast.52), calls=%async_computation.2 | async-start | bytes 2359296 | tf_op jit(solution)/shard_map/all_to_all | solution.py:133
  386.3 0.0 copy-done.8
  386.3 0.0 copy-done.6
  386.3 0.2 fusion.31
  386.5 0.0 copy-done.7
  386.5 0.1 select_reduce_fusion
  386.6 0.1 copy.35
  386.7 15.9 %all-to-all-done.1 = bf16[8,32,2304]{2,1,0:T(8,128)(2,1)S(1)} async-done(((bf16[8,32,2304]{2,1,0:T(8,128)(2,1)}), bf16[8,32,2304]{2,1,0:T(8,128)(2,1)S(1)}, u32[]{:S(2)}, u32[]{:S(2)}) %all-to-all-start.1) | async-done | bytes 1179680 | tf_op jit(solution)/shard_map/all_to_all | solution.py:133
  402.7 2.1 gather_fusion.1
  404.8 3.3 reshape.233
  408.0 4.0 multiply_reduce_fusion
  412.0 0.0 copy-done.2
  412.1 0.3 multiply_reduce_fusion.1
  412.3 1.0 multiply_convert_fusion
  (30 shorter events, 0.2 us)
Async XLA Ops:
  6.5 228.4 %copy-start = (bf16[1,360,2304]{2,1,0:T(8,128)(2,1)S(1)}, bf16[1,360,2304]{2,1,0:T(8,128)(2,1)}, u32[]{:S(2)}) copy-start(bf16[1,360,2304]{2,1,0:T(8,128)(2,1)} %param.30) | copy-start | bytes 4976644
  6.5 215.4 %all-gather.2.cloned.1.call-start = ((), (), s32[]{:S(2)}) async-start(), calls=%async_computation.3 | async-start | bytes 20054016 | tf_op jit(solution)/shard_map/all_gather | solution.py:127
  22.4 8.6 %copy-start.5 = (bf16[96,2304]{1,0:T(8,128)(2,1)S(1)}, bf16[96,2304]{1,0:T(8,128)(2,1)}, u32[]{:S(2)}) copy-start(bf16[96,2304]{1,0:T(8,128)(2,1)} %param.19) | copy-start | bytes 1327108
  35.9 8.5 %copy-start.9 = (s32[1,4]{1,0:T(1,128)S(1)}, s32[1,4]{1,0:T(1,128)}, u32[]{:S(2)}) copy-start(s32[1,4]{1,0:T(1,128)} %param.24) | copy-start | bytes 52
  55.9 17.1 %copy-start.3 = (bf16[96,2304]{1,0:T(8,128)(2,1)S(1)}, bf16[96,2304]{1,0:T(8,128)(2,1)}, u32[]{:S(2)}) copy-start(bf16[96,2304]{1,0:T(8,128)(2,1)} %param.16) | copy-start | bytes 1327108
  73.0 2.8 copy-start.1
  100.5 280.2 %reduce-scatter.2.cloned.1.call-start = ((), (), s32[]{:S(2)}) async-start(), calls=%async_computation.4 | async-start | bytes 20054016 | tf_op jit(solution)/shard_map/reduce_scatter | solution.py:132
  260.2 126.1 %copy-start.8 = (bf16[2304]{0:T(1024)(128)(2,1)S(1)}, bf16[2304]{0:T(1024)(128)(2,1)}, u32[]{:S(2)}) copy-start(bf16[2304]{0:T(1024)(128)(2,1)} %param.31) | copy-start | bytes 13828
  260.2 126.1 %copy-start.6 = (bf16[2304,8]{0,1:T(8,128)(2,1)S(1)}, bf16[2304,8]{0,1:T(8,128)(2,1)}, u32[]{:S(2)}) copy-start(bf16[2304,8]{0,1:T(8,128)(2,1)} %param.27) | copy-start | bytes 110596
  260.2 126.3 %copy-start.7 = (s32[96,2]{0,1:T(2,128)S(1)}, s32[96,2]{0,1:T(2,128)}, u32[]{:S(2)}) copy-start(s32[96,2]{0,1:T(2,128)} %param.25) | copy-start | bytes 2308
  380.7 21.9 %all-to-all-start.1 = ((bf16[8,32,2304]{2,1,0:T(8,128)(2,1)}), bf16[8,32,2304]{2,1,0:T(8,128)(2,1)S(1)}, u32[]{:S(2)}, u32[]{:S(2)}) async-start(bf16[8,32,2304]{2,1,0:T(8,128)(2,1)} %bitcast.52), calls=%async_computation.2 | async-start | bytes 2359296 | tf_op jit(solution)/shard_map/all_to_all | solution.py:133
  404.8 7.3 %copy-start.2 = (f32[96,2304]{1,0:T(8,128)S(1)}, f32[96,2304]{1,0:T(8,128)}, u32[]{:S(2)}) copy-start(f32[96,2304]{1,0:T(8,128)} %copy-done.1) | copy-start | bytes 2654212
  404.8 7.3 %copy-start.4 = (bf16[96,2304]{1,0:T(8,128)(2,1)S(1)}, bf16[96,2304]{1,0:T(8,128)(2,1)}, u32[]{:S(2)}) copy-start(bf16[96,2304]{1,0:T(8,128)(2,1)} %param.16) | copy-start | bytes 1327108
Sparse Core Ops, SparseCore 0:
  100.6 121.2 all-gather.1
  260.3 120.3 reduce-scatter.1

commit v2 on v1

--- a/solution.py
+++ b/solution.py
@@ -121,18 +121,36 @@
     outgoing = jnp.where(filled[:, None], normed[source_row], jnp.zeros((), jnp.bfloat16)).reshape(
         EXPERTS, MOST, width
     )
-    arrived = lax.all_to_all(outgoing, "ex", split_axis=0, concat_axis=0, tiled=True).reshape(
-        groups * MOST, width
-    )
-    arrived_rows = lax.all_gather(arrived, "sh", axis=0, tiled=True)
-    gate_value = jnp.dot(arrived_rows, gate_weight[0], preferred_element_type=jnp.float32)
-    up_value = jnp.dot(arrived_rows, up_weight[0], preferred_element_type=jnp.float32)
+    cuts = 3
+    step = width // cuts
+    gate_value = 0.0
+    up_value = 0.0
+    for cut in range(cuts):
+        columns = slice(cut * step, (cut + 1) * step)
+        arrived = lax.all_to_all(
+            outgoing[:, :, columns], "ex", split_axis=0, concat_axis=0, tiled=True
+        ).reshape(groups * MOST, step)
+        arrived_rows = lax.all_gather(arrived, "sh", axis=0, tiled=True)
+        gate_value = gate_value + jnp.dot(
+            arrived_rows, gate_weight[0, columns], preferred_element_type=jnp.float32
+        )
+        up_value = up_value + jnp.dot(
+            arrived_rows, up_weight[0, columns], preferred_element_type=jnp.float32
+        )
     hidden = (jax.nn.silu(gate_value) * up_value).astype(jnp.bfloat16)
-    partial = jnp.dot(hidden, down_weight[0], preferred_element_type=jnp.float32).astype(jnp.bfloat16)
-    summed = lax.psum_scatter(partial, "sh", scatter_dimension=0, tiled=True)
-    returned = lax.all_to_all(
-        summed.reshape(EXPERTS, MOST, width), "ex", split_axis=0, concat_axis=0, tiled=True
-    )
+    pieces = []
+    for cut in range(cuts):
+        columns = slice(cut * step, (cut + 1) * step)
+        partial = jnp.dot(
+            hidden, down_weight[0, :, columns], preferred_element_type=jnp.float32
+        ).astype(jnp.bfloat16)
+        summed = lax.psum_scatter(partial, "sh", scatter_dimension=0, tiled=True)
+        pieces.append(
+            lax.all_to_all(
+                summed.reshape(EXPERTS, MOST, step), "ex", split_axis=0, concat_axis=0, tiled=True
+            )
+        )
+    returned = jnp.concatenate(pieces, axis=2)
     flat_results = returned.reshape(EXPERTS * MOST, width)
     picked = flat_results[target].reshape(row_count, top_count, width)
     mixed = resid + jnp.sum(route_weights[:, :, None] * picked.astype(jnp.float32), axis=1)

time: 421 us -> 598 us (1.42); the launches traced: 420 us -> 589 us
  waiting for transfers between devices: 258 us -> 359 us
  matrix products: 65 us -> 99.9 us
  blocking collectives: 23.2 us -> 39.7 us
  starting transfers between devices: 5.8 us -> 21.2 us
    reduce_scatter x1 -> x3, waiting for transfers between devices: 121 us -> 218 us  [per_device(): summed = lax.psum_scatter(partial, 'sh', scatter_dimension=0, tiled=True)]
    dot_general x2 -> x9, matrix products: 38.2 us -> 74 us  [the longest x3 30.7 us: per_device(): jnp.dot(arrived_rows, up_weight[0, columns], preferred_element_type=jnp.f...]
    all_to_all x1 -> x3, blocking collectives: 23.2 us -> 39.7 us  [per_device(): lax.all_to_all(outgoing[:, :, columns], 'ex', split_axis=0, concat_axis=0...]
    all_to_all x1 -> x3, starting transfers between devices: 5.58 us -> 20.9 us  [per_device(): lax.all_to_all(summed.reshape(EXPERTS, MOST, step), 'ex', split_axis=0, c...]
    all_gather x1 -> x3, waiting for transfers between devices: 121 us -> 133 us  [per_device(): arrived_rows = lax.all_gather(arrived, 'sh', axis=0, tiled=True)]
    all_to_all x1 -> x3, waiting for transfers between devices: 15.9 us -> 6.96 us  [per_device(): lax.all_to_all(summed.reshape(EXPERTS, MOST, step), 'ex', split_axis=0, c...]
  transfers between devices with their start and end apart: 3 -> 9, of which waited for: 3 -> 7; matrix products, arithmetic and copies ran while one was open for 0% -> 8% of each run, Pallas kernels for 0% -> 0%
where the time goes in v2:
time: 598 us; the launch traced here: 589 us
  waiting for transfers between devices  359 us (60%)
  matrix products  99.9 us (17%)
  blocking collectives  39.7 us (7%)
  local copies, waits for them, and re-layouts  33.4 us (6%)
  other arithmetic  21.8 us (4%)
  starting transfers between devices  21.2 us (4%)
  between operations  14.2 us (2%)
    reduce_scatter x3, waiting for transfers between devices, per_device(): summed = lax.psum_scatter(partial, 'sh', scatter_dimension=0, tiled=True)  218 us
    all_gather x3, waiting for transfers between devices, per_device(): arrived_rows = lax.all_gather(arrived, 'sh', axis=0, tiled=True)  133 us
    all_to_all x3, blocking collectives, per_device(): lax.all_to_all(outgoing[:, :, columns], 'ex', split_axis=0, concat_axis=0...  39.7 us
    dot_general x3, matrix products, per_device(): jnp.dot(arrived_rows, up_weight[0, columns], preferred_element_type=jnp.f...  30.7 us
    dot_general x3, matrix products, per_device(): jnp.dot(hidden, down_weight[0, :, columns], preferred_element_type=jnp.fl...  23.2 us
    all_to_all x3, starting transfers between devices, per_device(): lax.all_to_all(summed.reshape(EXPERTS, MOST, step), 'ex', split_axis=0, c...  20.9 us
    dot_general x3, matrix products, per_device(): jnp.dot(arrived_rows, gate_weight[0, columns], preferred_element_type=jnp...  20.1 us
    dot_general x1, matrix products, attend(): jnp.einsum('hrk,khd->rhd', weights, values, preferred_element_type=jnp.fl...  14.7 us
  transfers between devices with their start and end apart: 9, of which 7 were waited for; matrix products, arithmetic and copies ran while one was open for 8% of the time, Pallas kernels for 0%

profile of v2, /device:TPU:1, one launch (start us, length us, event | category | flops | bytes accessed | tf_op | source)
XLA Modules:
  0.0 588.8 jit_solution(9405374475156152643)
XLA Ops:
  6.6 0.8 reduce-window.18
  7.4 0.1 convert_reduce_fusion
  7.6 0.7 broadcast_multiply_fusion
  8.3 0.8 copy.37
  9.0 0.5 broadcast.230
  9.6 1.3 reduce.5
  10.9 0.1 eq.85
  11.0 0.1 compare_reduce_fusion
  11.1 0.1 fusion.29
  11.2 0.7 convert_element_type.46
  11.9 0.1 copy.36
  12.0 0.1 mul.97
  12.2 0.1 eq.95
  12.3 0.6 reduce-window.19
  12.9 0.2 slice_reduce_fusion
  13.3 1.2 scatter_custom_fusion.1
  14.5 1.2 scatter_custom_fusion
  15.8 0.1 broadcast_in_dim.96
  15.9 1.3 copy.33
  17.2 5.1 pad_maximum_fusion.1
  22.3 8.6 %copy.32 = bf16[1120,2304]{0,1:T(8,128)(2,1)} copy(bf16[1120,2304]{1,0:T(8,128)(2,1)} %pad_maximum_fusion.1) | data formatting | bytes 10321920 | tf_op jit(solution)/shard_map/concatenate | solution.py:62
  30.9 4.9 pad_maximum_fusion
  35.8 8.5 %copy.31 = bf16[1120,2304]{0,1:T(8,128)(2,1)} copy(bf16[1120,2304]{1,0:T(8,128)(2,1)} %pad_maximum_fusion) | data formatting | bytes 10321920 | tf_op jit(solution)/shard_map/concatenate | solution.py:63
  44.4 0.2 and_reduce_fusion
  44.7 11.1 %fusion.2 = f32[36,96,1120]{2,1,0:T(8,128)} fusion(bf16[1120,36,64]{0,2,1:T(8,128)(2,1)} %bitcast.74, bf16[96,36,64]{0,2,1:T(8,128)(2,1)S(1)} %bitcast.77, pred[96,1120]{1,0:T(8,128)(4,1)S(1)} %pad_add_fusion), kind=kOutput, calls=%fused_computation.7 | convolution fusion | flops 503193600 | bytes 21193728 | tf_op jit(solution)/shard_map/rhd,khd->hrk/dot_general | solution.py:65
  55.8 14.7 %fusion.4 = f32[36,64,96]{2,1,0:T(8,128)S(1)} fusion(bf16[1120,36,64]{0,2,1:T(8,128)(2,1)} %bitcast.75, f32[36,96,1120]{2,1,0:T(8,128)} %fusion.2), kind=kOutput, calls=%fused_computation.16 | convolution fusion | flops 503198176 | bytes 21528576 | tf_op jit(solution)/shard_map/hrk,khd->rhd/dot_general | solution.py:70
  70.4 0.4 copy.34
  70.8 0.2 multiply_reduce_fusion.2
  71.0 0.2 multiply_convert_fusion.2
  71.2 2.4 gather_fusion
  73.6 1.4 broadcast_select_fusion
  75.1 0.9 fusion.46
  76.0 14.7 %all_to_all.30 = bf16[8,32,768]{2,1,0:T(8,128)(2,1)} all-to-all(bf16[8,32,768]{2,1,0:T(8,128)(2,1)S(1)} %get-tuple-element.7), channel_id=1, replica_groups=mesh['ex'=8,'sh'=16] {'ex'}, dimensions={0} | all-to-all | bytes 786432 | tf_op jit(solution)/shard_map/all_to_all | solution.py:130
  90.8 13.0 %all_to_all.31 = bf16[8,32,768]{2,1,0:T(8,128)(2,1)} all-to-all(bf16[8,32,768]{2,1,0:T(8,128)(2,1)} %get-tuple-element.6), channel_id=1, replica_groups=mesh['ex'=8,'sh'=16] {'ex'}, dimensions={0} | all-to-all | bytes 786432 | tf_op jit(solution)/shard_map/all_to_all | solution.py:130
  103.8 12.0 %all_to_all.32 = bf16[8,32,768]{2,1,0:T(8,128)(2,1)} all-to-all(bf16[8,32,768]{2,1,0:T(8,128)(2,1)S(1)} %get-tuple-element.5), channel_id=1, replica_groups=mesh['ex'=8,'sh'=16] {'ex'}, dimensions={0} | all-to-all | bytes 786432 | tf_op jit(solution)/shard_map/all_to_all | solution.py:130
  115.8 0.2 reduce-scatter.8.cloned.1.call-start
  116.1 35.5 %all-gather.4.cloned.1.call-done = bf16[4096,768]{1,0:T(8,128)(2,1)} async-done(((bf16[256,768]{1,0:T(8,128)(2,1)}), bf16[4096,768]{1,0:T(8,128)(2,1)}) %all-gather.4.cloned.1.call-update) | async-done | bytes 6291472 | tf_op jit(solution)/shard_map/all_gather | solution.py:133
  151.5 8.0 %fusion.11 = f32[4096,360]{0,1:T(8,128)} fusion(bf16[4096,768]{1,0:T(8,128)(2,1)} %all-gather.4.cloned.1.call-done, bf16[1,2304,360]{1,2,0:T(8,128)(2,1)} %param.29), kind=kOutput, calls=%fused_computation.32 | convolution fusion | flops 2264924160 | bytes 12742656 | tf_op jit(solution)/shard_map/dot_general | solution.py:137
  159.5 6.1 %fusion.17 = f32[4096,360]{0,1:T(8,128)} fusion(bf16[4096,768]{1,0:T(8,128)(2,1)S(1)} %copy-done.7, bf16[1,2304,360]{1,2,0:T(8,128)(2,1)} %param.28), kind=kOutput, calls=%fused_computation.38 | convolution fusion | flops 2264924160 | bytes 12742656 | tf_op jit(solution)/shard_map/dot_general | solution.py:134
  165.6 49.0 %all-gather.6.cloned.1.call-done = bf16[4096,768]{1,0:T(8,128)(2,1)} async-done(((bf16[256,768]{1,0:T(8,128)(2,1)}), bf16[4096,768]{1,0:T(8,128)(2,1)}) %all-gather.6.cloned.1.call-update) | async-done | bytes 6291472 | tf_op jit(solution)/shard_map/all_gather | solution.py:133
  214.6 8.1 %fusion.9 = f32[4096,360]{0,1:T(8,128)} fusion(bf16[4096,768]{1,0:T(8,128)(2,1)} %all-gather.6.cloned.1.call-done, bf16[1,2304,360]{1,2,0:T(8,128)(2,1)} %param.29), kind=kOutput, calls=%fused_computation.30 | convolution fusion | flops 2264924160 | bytes 12742656 | tf_op jit(solution)/shard_map/dot_general | solution.py:137
  222.7 6.2 %fusion.15 = f32[4096,360]{0,1:T(8,128)} fusion(bf16[4096,768]{1,0:T(8,128)(2,1)S(1)} %copy-done.8, bf16[1,2304,360]{1,2,0:T(8,128)(2,1)} %param.28), kind=kOutput, calls=%fused_computation.36 | convolution fusion | flops 2264924160 | bytes 12742656 | tf_op jit(solution)/shard_map/dot_general | solution.py:134
  228.8 48.8 %all-gather.8.cloned.1.call-done = bf16[4096,768]{1,0:T(8,128)(2,1)} async-done(((bf16[256,768]{1,0:T(8,128)(2,1)}), bf16[4096,768]{1,0:T(8,128)(2,1)}) %all-gather.8.cloned.1.call-update) | async-done | bytes 6291472 | tf_op jit(solution)/shard_map/all_gather | solution.py:133
  277.6 7.9 %fusion.13 = f32[4096,360]{0,1:T(8,128)} fusion(bf16[4096,768]{1,0:T(8,128)(2,1)} %all-gather.8.cloned.1.call-done, bf16[1,2304,360]{1,2,0:T(8,128)(2,1)} %param.28), kind=kOutput, calls=%fused_computation.34 | convolution fusion | flops 2264924160 | bytes 12742656 | tf_op jit(solution)/shard_map/dot_general | solution.py:134
  285.4 14.6 %multiply_convert_fusion = bf16[4096,360]{0,1:T(8,128)(2,1)S(1)} fusion(f32[4096,360]{0,1:T(8,128)} %fusion.11, f32[4096,360]{0,1:T(8,128)} %fusion.9, f32[4096,360]{0,1:T(8,128)} %fusion.13, f32[4096,360]{0,1:T(8,128)} %fusion.17, f32[4096,360]{0,1:T(8,128)} %fusion.15, bf16[4096,768]{1,0:T(8,128)(2,1)} %all-gather.8.cloned.1.call-done, ...), kind=kOutput, calls=%fused_computation.13 | convolution fusion | flops 2279669760 | bytes 39284736 | tf_op jit(solution)/shard_map/dot_general | solution.py:137
  300.1 1.6 copy-done.9
  301.7 6.7 %convolution_convert_fusion = bf16[4096,768]{1,0:T(8,128)(2,1)} fusion(bf16[4096,360]{0,1:T(8,128)(2,1)S(1)} %multiply_convert_fusion, bf16[1,360,2304]{2,1,0:T(8,128)(2,1)} %param.30), kind=kOutput, calls=%fused_computation.10 | convolution fusion | flops 2268069888 | bytes 9793536 | tf_op jit(solution)/shard_map/dot_general | solution.py:144
  308.5 8.1 %convolution_convert_fusion.1 = bf16[4096,768]{1,0:T(8,128)(2,1)} fusion(bf16[4096,360]{0,1:T(8,128)(2,1)} %copy-done.9, bf16[1,360,2304]{2,1,0:T(8,128)(2,1)} %param.30), kind=kOutput, calls=%fused_computation.11 | convolution fusion | flops 2268069888 | bytes 9793536 | tf_op jit(solution)/shard_map/dot_general | solution.py:144
  316.7 8.3 %convolution_convert_fusion.2 = bf16[4096,768]{1,0:T(8,128)(2,1)} fusion(bf16[4096,360]{0,1:T(8,128)(2,1)} %copy-done.9, bf16[1,360,2304]{2,1,0:T(8,128)(2,1)} %param.30), kind=kOutput, calls=%fused_computation.12 | convolution fusion | flops 2268069888 | bytes 9793536 | tf_op jit(solution)/shard_map/dot_general | solution.py:144
  325.0 63.3 %reduce-scatter.8.cloned.1.call-done = bf16[256,768]{1,0:T(8,128)(2,1)} async-done(((bf16[4096,768]{1,0:T(8,128)(2,1)}), bf16[256,768]{1,0:T(8,128)(2,1)}) %reduce-scatter.8.cloned.1.call-update) | async-done | bytes 393232 | tf_op jit(solution)/shard_map/reduce_scatter | solution.py:147
  388.3 6.9 %all-to-all-start.5 = ((bf16[8,32,768]{2,1,0:T(8,128)(2,1)}), bf16[8,32,768]{2,1,0:T(8,128)(2,1)S(1)}, u32[]{:S(2)}, u32[]{:S(2)}) async-start(bf16[8,32,768]{2,1,0:T(8,128)(2,1)} %bitcast.84), calls=%async_computation.8 | async-start | bytes 786432 | tf_op jit(solution)/shard_map/all_to_all | solution.py:149
  395.2 77.5 %reduce-scatter.6.cloned.1.call-done = bf16[256,768]{1,0:T(8,128)(2,1)} async-done(((bf16[4096,768]{1,0:T(8,128)(2,1)}), bf16[256,768]{1,0:T(8,128)(2,1)}) %reduce-scatter.6.cloned.1.call-update) | async-done | bytes 393232 | tf_op jit(solution)/shard_map/reduce_scatter | solution.py:147
  472.7 6.9 %all-to-all-start.4 = ((bf16[8,32,768]{2,1,0:T(8,128)(2,1)}), bf16[8,32,768]{2,1,0:T(8,128)(2,1)S(1)}, u32[]{:S(2)}, u32[]{:S(2)}) async-start(bf16[8,32,768]{2,1,0:T(8,128)(2,1)} %bitcast.83), calls=%async_computation.6 | async-start | bytes 786432 | tf_op jit(solution)/shard_map/all_to_all | solution.py:149
  479.6 0.2 fusion.47
  479.8 77.5 %reduce-scatter.4.cloned.1.call-done = bf16[256,768]{1,0:T(8,128)(2,1)} async-done(((bf16[4096,768]{1,0:T(8,128)(2,1)}), bf16[256,768]{1,0:T(8,128)(2,1)}) %reduce-scatter.4.cloned.1.call-update) | async-done | bytes 393232 | tf_op jit(solution)/shard_map/reduce_scatter | solution.py:147
  557.3 7.2 %all-to-all-start.3 = ((bf16[8,32,768]{2,1,0:T(8,128)(2,1)}), bf16[8,32,768]{2,1,0:T(8,128)(2,1)}, u32[]{:S(2)}, u32[]{:S(2)}) async-start(bf16[8,32,768]{2,1,0:T(8,128)(2,1)} %bitcast.82), calls=%async_computation.4 | async-start | bytes 786432 | tf_op jit(solution)/shard_map/all_to_all | solution.py:149
  564.5 0.7 copy.35
  565.2 7.0 %all-to-all-done.3 = bf16[8,32,768]{2,1,0:T(8,128)(2,1)} async-done(((bf16[8,32,768]{2,1,0:T(8,128)(2,1)}), bf16[8,32,768]{2,1,0:T(8,128)(2,1)}, u32[]{:S(2)}, u32[]{:S(2)}) %all-to-all-start.3) | async-done | bytes 393248 | tf_op jit(solution)/shard_map/all_to_all | solution.py:149
  572.2 1.1 pad_maximum_fusion.2
  573.3 2.1 gather_fusion.1
  575.4 2.3 reshape.249
  577.7 2.5 multiply_reduce_fusion
  580.2 0.3 multiply_reduce_fusion.1
  580.5 1.0 multiply_convert_fusion.1
  (57 shorter events, 0.8 us)
Async XLA Ops:
  6.5 473.0 %copy-start = (bf16[2304,8]{0,1:T(8,128)(2,1)S(1)}, bf16[2304,8]{0,1:T(8,128)(2,1)}, u32[]{:S(2)}) copy-start(bf16[2304,8]{0,1:T(8,128)(2,1)} %param.27) | copy-start | bytes 110596
  6.5 145.0 %all-gather.4.cloned.1.call-start = ((), (), s32[]{:S(2)}) async-start(), calls=%async_computation.9 | async-start | bytes 6684672 | tf_op jit(solution)/shard_map/all_gather | solution.py:133
  22.3 8.6 %copy-start.2 = (bf16[96,2304]{1,0:T(8,128)(2,1)S(1)}, bf16[96,2304]{1,0:T(8,128)(2,1)}, u32[]{:S(2)}) copy-start(bf16[96,2304]{1,0:T(8,128)(2,1)} %param.19) | copy-start | bytes 1327108
  35.8 8.5 %copy-start.6 = (s32[1,4]{1,0:T(1,128)S(1)}, s32[1,4]{1,0:T(1,128)}, u32[]{:S(2)}) copy-start(s32[1,4]{1,0:T(1,128)} %param.24) | copy-start | bytes 52
  55.8 15.0 %copy-start.1 = (bf16[96,2304]{1,0:T(8,128)(2,1)S(1)}, bf16[96,2304]{1,0:T(8,128)(2,1)}, u32[]{:S(2)}) copy-start(bf16[96,2304]{1,0:T(8,128)(2,1)} %param.16) | copy-start | bytes 1327108
  90.7 123.9 %all-gather.6.cloned.1.call-start = ((), (), s32[]{:S(2)}) async-start(), calls=%async_computation.10 | async-start | bytes 6684672 | tf_op jit(solution)/shard_map/all_gather | solution.py:133
  103.8 173.8 %all-gather.8.cloned.1.call-start = ((), (), s32[]{:S(2)}) async-start(), calls=%async_computation.11 | async-start | bytes 6684672 | tf_op jit(solution)/shard_map/all_gather | solution.py:133
  115.8 272.5 %reduce-scatter.8.cloned.1.call-start = ((), (), s32[]{:S(2)}) async-start(), calls=%async_computation.14 | async-start | bytes 6684672 | tf_op jit(solution)/shard_map/reduce_scatter | solution.py:147
  151.5 8.0 %copy-start.7 = (bf16[4096,768]{1,0:T(8,128)(2,1)S(1)}, bf16[4096,768]{1,0:T(8,128)(2,1)}, u32[]{:S(2)}) copy-start(bf16[4096,768]{1,0:T(8,128)(2,1)} %all-gather.4.cloned.1.call-done) | copy-start | bytes 18874372
  214.6 8.1 %copy-start.8 = (bf16[4096,768]{1,0:T(8,128)(2,1)S(1)}, bf16[4096,768]{1,0:T(8,128)(2,1)}, u32[]{:S(2)}) copy-start(bf16[4096,768]{1,0:T(8,128)(2,1)} %all-gather.6.cloned.1.call-done) | copy-start | bytes 18874372
  300.1 1.6 copy-start.9
  308.4 164.3 %reduce-scatter.6.cloned.1.call-start = ((), (), s32[]{:S(2)}) async-start(), calls=%async_computation.13 | async-start | bytes 6684672 | tf_op jit(solution)/shard_map/reduce_scatter | solution.py:147
  316.6 240.6 %reduce-scatter.4.cloned.1.call-start = ((), (), s32[]{:S(2)}) async-start(), calls=%async_computation.12 | async-start | bytes 6684672 | tf_op jit(solution)/shard_map/reduce_scatter | solution.py:147
  325.0 154.7 %copy-start.4 = (s32[96,2]{0,1:T(2,128)S(1)}, s32[96,2]{0,1:T(2,128)}, u32[]{:S(2)}) copy-start(s32[96,2]{0,1:T(2,128)} %param.25) | copy-start | bytes 2308
  325.0 239.4 %copy-start.5 = (bf16[2304]{0:T(1024)(128)(2,1)S(1)}, bf16[2304]{0:T(1024)(128)(2,1)}, u32[]{:S(2)}) copy-start(bf16[2304]{0:T(1024)(128)(2,1)} %param.31) | copy-start | bytes 13828
  388.3 84.4 %all-to-all-start.5 = ((bf16[8,32,768]{2,1,0:T(8,128)(2,1)}), bf16[8,32,768]{2,1,0:T(8,128)(2,1)S(1)}, u32[]{:S(2)}, u32[]{:S(2)}) async-start(bf16[8,32,768]{2,1,0:T(8,128)(2,1)} %bitcast.84), calls=%async_computation.8 | async-start | bytes 786432 | tf_op jit(solution)/shard_map/all_to_all | solution.py:149
  472.7 84.6 %all-to-all-start.4 = ((bf16[8,32,768]{2,1,0:T(8,128)(2,1)}), bf16[8,32,768]{2,1,0:T(8,128)(2,1)S(1)}, u32[]{:S(2)}, u32[]{:S(2)}) async-start(bf16[8,32,768]{2,1,0:T(8,128)(2,1)} %bitcast.83), calls=%async_computation.6 | async-start | bytes 786432 | tf_op jit(solution)/shard_map/all_to_all | solution.py:149
  557.3 14.9 %all-to-all-start.3 = ((bf16[8,32,768]{2,1,0:T(8,128)(2,1)}), bf16[8,32,768]{2,1,0:T(8,128)(2,1)}, u32[]{:S(2)}, u32[]{:S(2)}) async-start(bf16[8,32,768]{2,1,0:T(8,128)(2,1)} %bitcast.82), calls=%async_computation.4 | async-start | bytes 786432 | tf_op jit(solution)/shard_map/all_to_all | solution.py:149
  573.3 4.4 copy-start.3
Sparse Core Ops, SparseCore 0:
  90.8 60.6 all-gather.3
  153.7 60.8 all-gather.5
  216.7 60.8 all-gather.7
  308.6 79.7 reduce-scatter.7
  391.6 81.0 reduce-scatter.5
  476.0 81.2 reduce-scatter.3

commit v3 on v1

--- a/solution.py
+++ b/solution.py
@@ -8,6 +8,7 @@
 EXPERTS = 8
 PAGE = 16
 MOST = 32
+CTX_TOTAL = 512
 
 
 def rms_scale(values, gain):
@@ -38,25 +39,19 @@
     context_row_lengths,
 ):
     row_count = query_rows.shape[0]
-    store_count = key_store.shape[0]
     requests = new_row_lengths.shape[0]
     table = page_row.reshape(requests, -1)
-    per_request = table.shape[1]
     ends = jnp.cumsum(new_row_lengths)
     row_index = jnp.arange(row_count, dtype=jnp.int32)
     owner = jnp.sum((row_index[:, None] >= ends[None, :]).astype(jnp.int32), axis=1)
-    request_index = jnp.arange(requests, dtype=jnp.int32)
-    row_owner = owner[:, None] == request_index[None, :]
-    token_index = jnp.arange(store_count, dtype=jnp.int32)
-    token_page = token_index // PAGE
-    token_offset = token_index % PAGE
-    matched = table[:, :, None] == token_page[None, None, :]
-    page_slot = jnp.arange(per_request, dtype=jnp.int32) * PAGE
-    position = (
-        jnp.sum(jnp.where(matched, page_slot[None, :, None], 0), axis=1) + token_offset[None, :]
-    )
-    visible = jnp.any(matched, axis=1) & (position < context_row_lengths[:, None])
-    store_mask = jnp.any(row_owner[:, :, None] & visible[None, :, :], axis=1)
+    context_ends = jnp.cumsum(context_row_lengths)
+    slot = jnp.arange(CTX_TOTAL, dtype=jnp.int32)
+    slot_owner = jnp.sum((slot[:, None] >= context_ends[None, :]).astype(jnp.int32), axis=1)
+    position = slot - (context_ends - context_row_lengths)[slot_owner]
+    token = table[slot_owner, position // PAGE] * PAGE + position % PAGE
+    key_store = key_store[token]
+    value_store = value_store[token]
+    store_mask = owner[:, None] == slot_owner[None, :]
     fresh_mask = (owner[:, None] == owner[None, :]) & (row_index[None, :] <= row_index[:, None])
     allowed = jnp.concatenate([store_mask, fresh_mask], axis=1)
     keys = jnp.concatenate([key_store, key_rows], axis=0).reshape(-1, HEADS, HEAD_DIM)

time: 421 us -> 418 us (level)
  matrix products: 65 us -> 46.1 us
  local copies, waits for them, and re-layouts: 32.5 us -> 48.4 us
    gather x0 -> x4, local copies, waits for them, and re-layouts: none -> 22.9 us  [the longest x1 8.78 us: attend(): key_store = key_store[token]]
    dot_general x1, matrix products: 15.5 us -> 3.49 us  [attend(): jnp.einsum('hrk,khd->rhd', weights, values, preferred_element_type=jnp.fl...]
    dot_general x1, matrix products: 11.1 us -> 4.22 us  [attend(): jnp.einsum('rhd,khd->hrk', query_heads, keys, preferred_element_type=jnp....]
where the time goes in v3:
time: 418 us
  waiting for transfers between devices  258 us (62%)
  local copies, waits for them, and re-layouts  48.4 us (12%)
  matrix products  46.1 us (11%)
  blocking collectives  23.2 us (6%)
  other arithmetic  22.9 us (5%)
  between operations  13.7 us (3%)
  starting transfers between devices  5.84 us (1%)
    all_gather x1, waiting for transfers between devices, per_device(): arrived_rows = lax.all_gather(arrived, 'sh', axis=0, tiled=True)  121 us
    reduce_scatter x1, waiting for transfers between devices, per_device(): summed = lax.psum_scatter(partial, 'sh', scatter_dimension=0, tiled=True)  121 us
    dot_general x1, matrix products, per_device(): jnp.dot(hidden, down_weight[0], preferred_element_type=jnp.float32)  25.2 us
    all_to_all x1, blocking collectives, per_device(): lax.all_to_all(outgoing, 'ex', split_axis=0, concat_axis=0, tiled=True)  23.2 us
    all_to_all x1, waiting for transfers between devices, per_device(): lax.all_to_all(summed.reshape(EXPERTS, MOST, width), 'ex', split_axis=0,...  15.9 us
    dot_general x1, matrix products, per_device(): jnp.dot(arrived_rows, gate_weight[0], preferred_element_type=jnp.float32)  13 us
    gather x1, local copies, waits for them, and re-layouts, attend(): key_store = key_store[token]  8.78 us
    gather x1, local copies, waits for them, and re-layouts, attend(): value_store = value_store[token]  8.74 us
  transfers between devices with their start and end apart: 3, of which 3 were waited for; matrix products, arithmetic and copies ran while one was open for 0% of the time, Pallas kernels for 0%

profile of v3, /device:TPU:1, one launch (start us, length us, event | category | flops | bytes accessed | tf_op | source)
XLA Modules:
  0.0 417.8 jit_solution(15909731302938036896)
XLA Ops:
  6.5 0.0 copy-start
  6.5 0.0 all-gather.2.cloned.1.call-start
  6.5 0.8 broadcast_multiply_fusion.1
  7.4 0.8 copy.37
  8.2 0.8 reduce-window.26
  9.0 0.7 bitcast_subtract_fusion
  9.6 0.8 reduce-window.27
  10.5 0.1 convert_reduce_fusion.1
  10.6 0.5 broadcast.363
  11.1 1.3 reduce.5
  12.4 0.1 reshape_squeeze.3
  12.5 0.7 fusion.26
  13.1 0.1 convert_reduce_fusion
  13.2 0.1 fusion.10
  13.3 0.1 broadcast_compare_fusion
  13.4 2.6 fusion.17
  16.0 4.8 %gather_fusion = s32[512]{0:T(512)S(1)} fusion(s32[4,16]{1,0:T(4,128)S(1)} %reshape_squeeze.3, s32[512]{0:T(512)S(1)} %bitcast.61), kind=kCustom, calls=%fused_computation | custom fusion | bytes 8192 | tf_op jit(solution)/shard_map/gather | solution.py:51
  20.8 0.7 convert_element_type.44
  21.5 0.1 copy.36
  21.6 0.1 mul.104
  21.7 0.1 eq.72
  21.9 0.6 reduce-window.28
  22.5 0.2 slice_reduce_fusion
  22.7 0.1 add_bitcast_fusion
  22.9 1.2 scatter_custom_fusion.1
  24.1 1.4 scatter_custom_fusion
  25.5 0.1 broadcast_in_dim.46
  25.6 0.3 copy.33
  25.9 0.0 copy-start.7
  26.0 8.8 %gather_fusion.2 = bf16[512,2304]{1,0:T(8,128)(2,1)} fusion(bf16[1024,2304]{1,0:T(8,128)(2,1)} %param.20, s32[1024]{0:T(1024)S(1)} %pad_clamp_fusion.2), kind=kCustom, calls=%fused_computation.2 | custom fusion | bytes 4720640 | tf_op jit(solution)/shard_map/gather | solution.py:52
  34.7 3.4 pad_maximum_fusion.1
  38.2 5.4 %copy.32 = bf16[608,2304]{0,1:T(8,128)(2,1)} copy(bf16[608,2304]{1,0:T(8,128)(2,1)} %pad_maximum_fusion.1) | data formatting | bytes 5603328 | tf_op jit(solution)/shard_map/concatenate | solution.py:57
  43.6 8.7 %gather_fusion.1 = bf16[512,2304]{1,0:T(8,128)(2,1)} fusion(bf16[1024,2304]{1,0:T(8,128)(2,1)} %param.21, s32[1024]{0:T(1024)S(1)} %pad_clamp_fusion.2), kind=kCustom, calls=%fused_computation.1 | custom fusion | bytes 4720640 | tf_op jit(solution)/shard_map/gather | solution.py:53
  52.3 0.0 copy-done.8
  52.3 3.4 pad_maximum_fusion
  55.7 5.4 %copy.31 = bf16[608,2304]{0,1:T(8,128)(2,1)} copy(bf16[608,2304]{1,0:T(8,128)(2,1)} %pad_maximum_fusion) | data formatting | bytes 5603328 | tf_op jit(solution)/shard_map/concatenate | solution.py:58
  61.2 0.0 copy-start.5
  61.2 4.2 %fusion = (f32[36,96]{1,0:T(8,128)S(1)}, f32[36,608,96]{1,2,0:T(8,128)S(1)}) fusion(pred[96,608]{1,0:T(8,128)(4,1)S(1)} %pad_add_fusion, bf16[608,36,64]{0,2,1:T(8,128)(2,1)} %bitcast.64, bf16[96,36,64]{0,2,1:T(8,128)(2,1)S(1)} %bitcast.68), kind=kOutput, calls=%fused_computation.10 | convolution fusion | flops 275260032 | bytes 11721216 | tf_op jit(solution)/shard_map/rhd,khd->hrk/dot_general | solution.py:60
  65.4 0.0 copy-start.3
  65.4 3.5 fusion.2
  68.9 1.6 copy.34
  70.6 0.2 multiply_reduce_fusion.2
  70.8 0.2 multiply_convert_fusion.1
  71.0 2.4 gather_fusion.3
  73.4 1.4 broadcast_select_fusion
  74.8 23.2 %all_to_all.10 = bf16[8,32,2304]{2,1,0:T(8,128)(2,1)} all-to-all(bf16[8,32,2304]{2,1,0:T(8,128)(2,1)S(1)} %broadcast_select_fusion), channel_id=1, replica_groups=mesh['ex'=8,'sh'=16] {'ex'}, dimensions={0} | all-to-all | bytes 2359296 | tf_op jit(solution)/shard_map/all_to_all | solution.py:119
  98.1 0.0 all-gather.2.cloned.1.call-update
  98.1 0.3 reduce-scatter.2.cloned.1.call-start
  98.4 121.2 %all-gather.2.cloned.1.call-done = bf16[4096,2304]{1,0:T(8,128)(2,1)} async-done(((bf16[256,2304]{1,0:T(8,128)(2,1)}), bf16[4096,2304]{1,0:T(8,128)(2,1)}) %all-gather.2.cloned.1.call-update) | async-done | bytes 18874384 | tf_op jit(solution)/shard_map/all_gather | solution.py:122
  219.6 13.0 %fusion.7 = f32[4096,360]{0,1:T(8,128)} fusion(bf16[4096,2304]{1,0:T(8,128)(2,1)} %all-gather.2.cloned.1.call-done, bf16[1,2304,360]{1,2,0:T(8,128)(2,1)} %param.28), kind=kOutput, calls=%fused_computation.19 | convolution fusion | flops 6794772480 | bytes 26431488 | tf_op jit(solution)/shard_map/dot_general | solution.py:123
  232.6 0.0 copy-done
  232.6 25.2 %convolution_convert_fusion = bf16[4096,2304]{1,0:T(8,128)(2,1)} fusion(bf16[1,360,2304]{2,1,0:T(8,128)(2,1)S(1)} %copy-done, bf16[4096,2304]{1,0:T(8,128)(2,1)} %all-gather.2.cloned.1.call-done, f32[4096,360]{0,1:T(8,128)} %fusion.7, bf16[1,2304,360]{1,2,0:T(8,128)(2,1)} %param.29), kind=kOutput, calls=%fused_computation.7 | convolution fusion | flops 13607829504 | bytes 46964736 | tf_op jit(solution)/shard_map/dot_general | solution.py:126
  257.8 0.0 reduce-scatter.2.cloned.1.call-update
  257.8 120.5 %reduce-scatter.2.cloned.1.call-done = bf16[256,2304]{1,0:T(8,128)(2,1)} async-done(((bf16[4096,2304]{1,0:T(8,128)(2,1)}), bf16[256,2304]{1,0:T(8,128)(2,1)}) %reduce-scatter.2.cloned.1.call-update) | async-done | bytes 1179664 | tf_op jit(solution)/shard_map/reduce_scatter | solution.py:127
  378.3 5.6 %all-to-all-start.1 = ((bf16[8,32,2304]{2,1,0:T(8,128)(2,1)}), bf16[8,32,2304]{2,1,0:T(8,128)(2,1)S(1)}, u32[]{:S(2)}, u32[]{:S(2)}) async-start(bf16[8,32,2304]{2,1,0:T(8,128)(2,1)} %bitcast.66), calls=%async_computation.2 | async-start | bytes 2359296 | tf_op jit(solution)/shard_map/all_to_all | solution.py:128
  383.9 0.2 fusion.27
  384.1 0.1 select_reduce_fusion
  384.2 0.1 copy.35
  384.3 15.9 %all-to-all-done.1 = bf16[8,32,2304]{2,1,0:T(8,128)(2,1)S(1)} async-done(((bf16[8,32,2304]{2,1,0:T(8,128)(2,1)}), bf16[8,32,2304]{2,1,0:T(8,128)(2,1)S(1)}, u32[]{:S(2)}, u32[]{:S(2)}) %all-to-all-start.1) | async-done | bytes 1179680 | tf_op jit(solution)/shard_map/all_to_all | solution.py:128
  400.3 2.1 gather_fusion.4
  402.4 3.3 reshape.302
  405.6 4.0 multiply_reduce_fusion
  409.7 0.3 multiply_reduce_fusion.1
  409.9 1.0 multiply_convert_fusion
  (38 shorter events, 0.2 us)
Async XLA Ops:
  6.5 226.0 %copy-start = (bf16[1,360,2304]{2,1,0:T(8,128)(2,1)S(1)}, bf16[1,360,2304]{2,1,0:T(8,128)(2,1)}, u32[]{:S(2)}) copy-start(bf16[1,360,2304]{2,1,0:T(8,128)(2,1)} %param.30) | copy-start | bytes 4976644
  6.5 19.1 %copy-start.6 = (bf16[96,2304]{1,0:T(8,128)(2,1)S(1)}, bf16[96,2304]{1,0:T(8,128)(2,1)}, u32[]{:S(2)}) copy-start(bf16[96,2304]{1,0:T(8,128)(2,1)} %param.17) | copy-start | bytes 1327108
  6.5 213.0 %all-gather.2.cloned.1.call-start = ((), (), s32[]{:S(2)}) async-start(), calls=%async_computation.3 | async-start | bytes 20054016 | tf_op jit(solution)/shard_map/all_gather | solution.py:122
  25.9 8.8 %copy-start.7 = (bf16[96,2304]{1,0:T(8,128)(2,1)S(1)}, bf16[96,2304]{1,0:T(8,128)(2,1)}, u32[]{:S(2)}) copy-start(bf16[96,2304]{1,0:T(8,128)(2,1)} %param.18) | copy-start | bytes 1327108
  43.6 8.7 %copy-start.8 = (bf16[96,2304]{1,0:T(8,128)(2,1)S(1)}, bf16[96,2304]{1,0:T(8,128)(2,1)}, u32[]{:S(2)}) copy-start(bf16[96,2304]{1,0:T(8,128)(2,1)} %param.19) | copy-start | bytes 1327108
  61.2 4.2 %copy-start.5 = (bf16[608,2304]{0,1:T(8,128)(2,1)S(1)}, bf16[608,2304]{0,1:T(8,128)(2,1)}, u32[]{:S(2)}) copy-start(bf16[608,2304]{0,1:T(8,128)(2,1)} %copy.31) | copy-start | bytes 8404996
  65.4 5.1 %copy-start.3 = (bf16[96,2304]{1,0:T(8,128)(2,1)S(1)}, bf16[96,2304]{1,0:T(8,128)(2,1)}, u32[]{:S(2)}) copy-start(bf16[96,2304]{1,0:T(8,128)(2,1)} %param.16) | copy-start | bytes 1327108
  70.6 2.8 copy-start.1
  98.1 280.2 %reduce-scatter.2.cloned.1.call-start = ((), (), s32[]{:S(2)}) async-start(), calls=%async_computation.4 | async-start | bytes 20054016 | tf_op jit(solution)/shard_map/reduce_scatter | solution.py:127
  257.8 126.1 %copy-start.11 = (bf16[2304]{0:T(1024)(128)(2,1)S(1)}, bf16[2304]{0:T(1024)(128)(2,1)}, u32[]{:S(2)}) copy-start(bf16[2304]{0:T(1024)(128)(2,1)} %param.31) | copy-start | bytes 13828
  257.8 126.1 %copy-start.9 = (bf16[2304,8]{0,1:T(8,128)(2,1)S(1)}, bf16[2304,8]{0,1:T(8,128)(2,1)}, u32[]{:S(2)}) copy-start(bf16[2304,8]{0,1:T(8,128)(2,1)} %param.27) | copy-start | bytes 110596
  257.8 126.3 %copy-start.10 = (s32[96,2]{0,1:T(2,128)S(1)}, s32[96,2]{0,1:T(2,128)}, u32[]{:S(2)}) copy-start(s32[96,2]{0,1:T(2,128)} %param.25) | copy-start | bytes 2308
  378.3 21.9 %all-to-all-start.1 = ((bf16[8,32,2304]{2,1,0:T(8,128)(2,1)}), bf16[8,32,2304]{2,1,0:T(8,128)(2,1)S(1)}, u32[]{:S(2)}, u32[]{:S(2)}) async-start(bf16[8,32,2304]{2,1,0:T(8,128)(2,1)} %bitcast.66), calls=%async_computation.2 | async-start | bytes 2359296 | tf_op jit(solution)/shard_map/all_to_all | solution.py:128
  402.4 7.3 %copy-start.2 = (f32[96,2304]{1,0:T(8,128)S(1)}, f32[96,2304]{1,0:T(8,128)}, u32[]{:S(2)}) copy-start(f32[96,2304]{1,0:T(8,128)} %copy-done.1) | copy-start | bytes 2654212
  402.4 7.3 %copy-start.4 = (bf16[96,2304]{1,0:T(8,128)(2,1)S(1)}, bf16[96,2304]{1,0:T(8,128)(2,1)}, u32[]{:S(2)}) copy-start(bf16[96,2304]{1,0:T(8,128)(2,1)} %param.16) | copy-start | bytes 1327108
Sparse Core Ops, SparseCore 0:
  98.2 121.3 all-gather.1
  257.9 120.3 reduce-scatter.1

commit v4 on v1

--- a/solution.py
+++ b/solution.py
@@ -2,12 +2,14 @@
 import jax.numpy as jnp
 from jax import lax
 from jax.sharding import PartitionSpec as P
+from jax.experimental import pallas as pl
 
 HEADS = 36
 HEAD_DIM = 64
 EXPERTS = 8
 PAGE = 16
 MOST = 32
+INTERPRET = False
 
 
 def rms_scale(values, gain):
@@ -24,6 +26,43 @@
     )
     raised = jnp.exp(picked)
     return raised / jnp.sum(raised, axis=1, keepdims=True)
+
+
+def attention_kernel(
+    query_ref, pool_key_ref, new_key_ref, pool_value_ref, new_value_ref, hidden_ref,
+    token_owner_ref, owner_ref, owner_row_ref, out_ref
+):
+    query = query_ref[...]
+    rows = query.shape[0]
+    owner = owner_ref[...]
+    pool_ok = owner == token_owner_ref[...]
+    row_at = lax.broadcasted_iota(jnp.int32, (rows, rows), 0)
+    col_at = lax.broadcasted_iota(jnp.int32, (rows, rows), 1)
+    new_ok = (owner == owner_row_ref[...]) & (col_at <= row_at)
+    lane = lax.broadcasted_iota(jnp.int32, (1, query.shape[1]), 1)
+    contract = (((1,), (1,)), ((), ()))
+    total = hidden_ref[...].astype(jnp.float32)
+    for head in range(query.shape[1] // HEAD_DIM):
+        in_head = (lane >= head * HEAD_DIM) & (lane < (head + 1) * HEAD_DIM)
+        head_query = jnp.where(in_head, query, jnp.zeros((), query.dtype))
+        pool_score = lax.dot_general(
+            head_query, pool_key_ref[...], contract, preferred_element_type=jnp.float32
+        ) * HEAD_DIM ** (-0.5)
+        new_score = lax.dot_general(
+            head_query, new_key_ref[...], contract, preferred_element_type=jnp.float32
+        ) * HEAD_DIM ** (-0.5)
+        pool_raised = jnp.where(pool_ok, jnp.exp(pool_score), 0.0)
+        new_raised = jnp.where(new_ok, jnp.exp(new_score), 0.0)
+        denom = jnp.sum(pool_raised, axis=1, keepdims=True) + jnp.sum(
+            new_raised, axis=1, keepdims=True
+        )
+        pool_weight = (pool_raised / denom).astype(jnp.bfloat16)
+        new_weight = (new_raised / denom).astype(jnp.bfloat16)
+        mixed = jnp.dot(
+            pool_weight, pool_value_ref[...], preferred_element_type=jnp.float32
+        ) + jnp.dot(new_weight, new_value_ref[...], preferred_element_type=jnp.float32)
+        total = total + jnp.where(in_head, mixed, 0.0)
+    out_ref[...] = total
 
 
 def attend(
@@ -37,40 +76,57 @@
     new_row_lengths,
     context_row_lengths,
 ):
-    row_count = query_rows.shape[0]
+    row_count, width = query_rows.shape
     store_count = key_store.shape[0]
     requests = new_row_lengths.shape[0]
-    table = page_row.reshape(requests, -1)
-    per_request = table.shape[1]
+    per_request = page_row.shape[0] // requests
     ends = jnp.cumsum(new_row_lengths)
     row_index = jnp.arange(row_count, dtype=jnp.int32)
     owner = jnp.sum((row_index[:, None] >= ends[None, :]).astype(jnp.int32), axis=1)
-    request_index = jnp.arange(requests, dtype=jnp.int32)
-    row_owner = owner[:, None] == request_index[None, :]
+    pages = store_count // PAGE
+    entry = jnp.arange(page_row.shape[0], dtype=jnp.int32)
+    page_entry = jnp.sum(
+        jnp.where(page_row[None, :] == jnp.arange(pages, dtype=jnp.int32)[:, None], entry[None, :], 0),
+        axis=1,
+    )
     token_index = jnp.arange(store_count, dtype=jnp.int32)
-    token_page = token_index // PAGE
-    token_offset = token_index % PAGE
-    matched = table[:, :, None] == token_page[None, None, :]
-    page_slot = jnp.arange(per_request, dtype=jnp.int32) * PAGE
-    position = (
-        jnp.sum(jnp.where(matched, page_slot[None, :, None], 0), axis=1) + token_offset[None, :]
-    )
-    visible = jnp.any(matched, axis=1) & (position < context_row_lengths[:, None])
-    store_mask = jnp.any(row_owner[:, :, None] & visible[None, :, :], axis=1)
-    fresh_mask = (owner[:, None] == owner[None, :]) & (row_index[None, :] <= row_index[:, None])
-    allowed = jnp.concatenate([store_mask, fresh_mask], axis=1)
-    keys = jnp.concatenate([key_store, key_rows], axis=0).reshape(-1, HEADS, HEAD_DIM)
-    values = jnp.concatenate([value_store, value_rows], axis=0).reshape(-1, HEADS, HEAD_DIM)
-    query_heads = query_rows.reshape(row_count, HEADS, HEAD_DIM)
-    scores = jnp.einsum(
-        "rhd,khd->hrk", query_heads, keys, preferred_element_type=jnp.float32
-    ) * HEAD_DIM ** (-0.5)
-    raised = jnp.where(allowed[None, :, :], jnp.exp(scores), 0.0)
-    weights = (raised / jnp.sum(raised, axis=2, keepdims=True)).astype(jnp.bfloat16)
-    attended = jnp.einsum(
-        "hrk,khd->rhd", weights, values, preferred_element_type=jnp.float32
-    ).reshape(row_count, HEADS * HEAD_DIM)
-    return hidden_rows.astype(jnp.float32) + attended
+    token_entry = page_entry[token_index // PAGE]
+    token_request = token_entry // per_request
+    position = (token_entry % per_request) * PAGE + token_index % PAGE
+    token_owner = jnp.where(
+        position < context_row_lengths[token_request], token_request, -1
+    ).astype(jnp.int32)
+    block = 2 * HEAD_DIM
+    column = lambda count: pl.BlockSpec((count, block), lambda j: (0, j))
+    whole = lambda shape: pl.BlockSpec(shape, lambda j: (0, 0))
+    return pl.pallas_call(
+        attention_kernel,
+        grid=(width // block,),
+        in_specs=[
+            column(row_count),
+            column(store_count),
+            column(row_count),
+            column(store_count),
+            column(row_count),
+            column(row_count),
+            whole((1, store_count)),
+            whole((row_count, 1)),
+            whole((1, row_count)),
+        ],
+        out_specs=column(row_count),
+        out_shape=jax.ShapeDtypeStruct((row_count, width), jnp.float32),
+        interpret=INTERPRET,
+    )(
+        query_rows,
+        key_store,
+        key_rows,
+        value_store,
+        value_rows,
+        hidden_rows,
+        token_owner.reshape(1, store_count),
+        owner.reshape(row_count, 1),
+        owner.reshape(1, row_count),
+    )
 
 
 def per_device(

time: 421 us -> 430 us (1.021)
  other arithmetic: 22.3 us -> 55.3 us
  matrix products: 65 us -> 38.4 us
  Pallas kernels: 0 us -> 19.4 us
  local copies, waits for them, and re-layouts: 32.5 us -> 15 us
    gather x0 -> x59, other arithmetic: none -> 41.8 us  [attend(): token_entry = page_entry[token_index // PAGE]]
    dot_general x2 -> x0, matrix products: 26.6 us -> none  [the longest x1 15.5 us: attend(): jnp.einsum('hrk,khd->rhd', weights, values, preferred_element_type=jnp.fl...]
    pallas_call x0 -> x1, Pallas kernels: none -> 19.4 us  [attend(): pl.pallas_call(attention_kernel, grid=(width // block,), in_specs=[column...]
    concatenate x2 -> x0, local copies, waits for them, and re-layouts: 17.1 us -> none  [the longest x1 8.56 us: attend(): jnp.concatenate([key_store, key_rows], axis=0).reshape(-1, HEADS, HEAD_DIM)]
    concatenate x3 -> x0, other arithmetic: 10.1 us -> none  [the longest x1 5.1 us: attend(): jnp.concatenate([key_store, key_rows], axis=0).reshape(-1, HEADS, HEAD_DIM)]
    gather x0 -> x5, local copies, waits for them, and re-layouts: none -> 4.34 us  [the longest x4 2.86 us: attend(): token_entry = page_entry[token_index // PAGE]]
where the time goes in v4:
time: 430 us; the launch traced here: 428 us
  waiting for transfers between devices  258 us (60%)
  other arithmetic  55.3 us (13%)
  matrix products  38.4 us (9%)
  blocking collectives  23.2 us (5%)
  Pallas kernels  19.4 us (5%)
  local copies, waits for them, and re-layouts  15 us (3%)
  between operations  13.7 us (3%)
  starting transfers between devices  5.73 us (1%)
    all_gather x1, waiting for transfers between devices, per_device(): arrived_rows = lax.all_gather(arrived, 'sh', axis=0, tiled=True)  121 us
    reduce_scatter x1, waiting for transfers between devices, per_device(): summed = lax.psum_scatter(partial, 'sh', scatter_dimension=0, tiled=True)  121 us
    gather x59, other arithmetic, attend(): token_entry = page_entry[token_index // PAGE]  41.8 us
    dot_general x1, matrix products, per_device(): jnp.dot(hidden, down_weight[0], preferred_element_type=jnp.float32)  25.2 us
    all_to_all x1, blocking collectives, per_device(): lax.all_to_all(outgoing, 'ex', split_axis=0, concat_axis=0, tiled=True)  23.2 us
    pallas_call x1, Pallas kernels, attend(): pl.pallas_call(attention_kernel, grid=(width // block,), in_specs=[column...  19.4 us
    all_to_all x1, waiting for transfers between devices, per_device(): lax.all_to_all(summed.reshape(EXPERTS, MOST, width), 'ex', split_axis=0,...  15.9 us
    dot_general x1, matrix products, per_device(): jnp.dot(arrived_rows, gate_weight[0], preferred_element_type=jnp.float32)  13 us
  transfers between devices with their start and end apart: 3, of which 3 were waited for; matrix products, arithmetic and copies ran while one was open for 0% of the time, Pallas kernels for 0%

profile of v4, /device:TPU:1, one launch (start us, length us, event | category | flops | bytes accessed | tf_op | source)
XLA Modules:
  0.0 428.4 jit_solution(11411634228982721445)
XLA Ops:
  6.5 0.0 copy-start
  6.5 0.0 all-gather.2.cloned.1.call-start
  8.5 0.8 select_reduce_fusion
  9.3 0.7 fusion.21
  10.0 0.7 fusion.18
  10.7 0.7 fusion.19
  11.4 0.7 fusion.20
  12.2 0.7 broadcast_multiply_fusion
  12.8 0.8 copy.28
  13.6 0.8 reduce-window.18
  14.4 0.1 convert_reduce_fusion
  14.5 0.0 copy-start.6
  14.5 1.5 fusion.17
  16.0 0.7 convert_element_type.32
  16.7 0.1 copy.27
  16.8 0.1 mul.92
  16.9 0.7 copy.25.owner_ref
  17.7 0.1 eq.60
  17.8 0.6 reduce-window.19
  18.4 0.2 slice_reduce_fusion
  18.7 0.1 add_bitcast_fusion
  18.8 1.2 scatter_custom_fusion.1
  20.0 1.2 scatter_custom_fusion
  21.3 0.1 broadcast_in_dim.75
  21.4 4.2 compare_select_fusion.5
  25.6 35.6 %select_select_fusion = s32[1024]{0:T(1024)S(1)} fusion(pred[1024]{0:T(1024)(128)(4,1)S(1)} %compare_reduce_fusion, pred[1024]{0:T(1024)(128)(4,1)S(1)} %compare_reduce_fusion.1, pred[1024]{0:T(1024)(128)(4,1)S(1)} %compare_reduce_fusion.2, pred[1024]{0:T(1024)(128)(4,1)S(1)} %compare_reduce_fusion.3, pred[1024]{0:T(1024)(128)(4,1)S(1)} %compare_reduce_fusion.4, ...), kind=kLoop, calls=%fused_computation.118 | loop fusion | flops 58368 | bytes 66788 | tf_op jit(solution)/shard_map/gather | solution.py:93
  61.3 3.2 compare_select_fusion.11.token_owner_ref
  64.5 0.0 copy-done.6
  64.5 19.4 %shard_map.154 = f32[96,2304]{1,0:T(8,128)} custom-call(bf16[96,2304]{1,0:T(8,128)(2,1)} %query_ref.1, bf16[1024,2304]{1,0:T(8,128)(2,1)} %pool_key_ref.1, bf16[96,2304]{1,0:T(8,128)(2,1)} %new_key_ref.1, bf16[1024,2304]{1,0:T(8,128)(2,1)} %pool_value_ref.1, bf16[96,2304]{1,0:T(8,128)(2,1)} %new_value_ref.1, bf16[96,2304]{1,0:T(8,128)(2,1)} %hidden_ref.1, ...), custom_call_target="tpu_custom_call" | custom-call | tf_op jit(solution)/shard_map/pallas_call | solution.py:102
  83.9 1.3 multiply_reduce_fusion.2
  85.2 1.3 multiply_convert_fusion.1
  86.5 1.4 gather_fusion
  88.0 0.1 broadcast_select_fusion
  88.1 23.2 %all_to_all.10 = bf16[8,32,2304]{2,1,0:T(8,128)(2,1)} all-to-all(bf16[8,32,2304]{2,1,0:T(8,128)(2,1)S(1)} %broadcast_select_fusion), channel_id=1, replica_groups=mesh['ex'=8,'sh'=16] {'ex'}, dimensions={0} | all-to-all | bytes 2359296 | tf_op jit(solution)/shard_map/all_to_all | solution.py:180
  111.3 0.0 all-gather.2.cloned.1.call-update
  111.4 0.2 reduce-scatter.2.cloned.1.call-start
  111.6 121.2 %all-gather.2.cloned.1.call-done = bf16[4096,2304]{1,0:T(8,128)(2,1)} async-done(((bf16[256,2304]{1,0:T(8,128)(2,1)}), bf16[4096,2304]{1,0:T(8,128)(2,1)}) %all-gather.2.cloned.1.call-update) | async-done | bytes 18874384 | tf_op jit(solution)/shard_map/all_gather | solution.py:183
  232.8 13.0 %fusion.5 = f32[4096,360]{0,1:T(8,128)} fusion(bf16[4096,2304]{1,0:T(8,128)(2,1)} %all-gather.2.cloned.1.call-done, bf16[1,2304,360]{1,2,0:T(8,128)(2,1)} %param.28), kind=kOutput, calls=%fused_computation.10 | convolution fusion | flops 6794772480 | bytes 26431488 | tf_op jit(solution)/shard_map/dot_general | solution.py:184
  245.8 0.0 copy-done
  245.8 25.2 %convolution_convert_fusion = bf16[4096,2304]{1,0:T(8,128)(2,1)} fusion(bf16[1,360,2304]{2,1,0:T(8,128)(2,1)S(1)} %copy-done, bf16[4096,2304]{1,0:T(8,128)(2,1)} %all-gather.2.cloned.1.call-done, f32[4096,360]{0,1:T(8,128)} %fusion.5, bf16[1,2304,360]{1,2,0:T(8,128)(2,1)} %param.29), kind=kOutput, calls=%fused_computation.4 | convolution fusion | flops 13607829504 | bytes 46964736 | tf_op jit(solution)/shard_map/dot_general | solution.py:187
  271.0 0.0 reduce-scatter.2.cloned.1.call-update
  271.1 0.0 copy-start.5
  271.1 0.0 copy-start.3
  271.1 0.0 copy-start.4
  271.1 120.5 %reduce-scatter.2.cloned.1.call-done = bf16[256,2304]{1,0:T(8,128)(2,1)} async-done(((bf16[4096,2304]{1,0:T(8,128)(2,1)}), bf16[256,2304]{1,0:T(8,128)(2,1)}) %reduce-scatter.2.cloned.1.call-update) | async-done | bytes 1179664 | tf_op jit(solution)/shard_map/reduce_scatter | solution.py:188
  391.6 5.5 %all-to-all-start.1 = ((bf16[8,32,2304]{2,1,0:T(8,128)(2,1)}), bf16[8,32,2304]{2,1,0:T(8,128)(2,1)S(1)}, u32[]{:S(2)}, u32[]{:S(2)}) async-start(bf16[8,32,2304]{2,1,0:T(8,128)(2,1)} %bitcast.112), calls=%async_computation.2 | async-start | bytes 2359296 | tf_op jit(solution)/shard_map/all_to_all | solution.py:189
  397.1 0.0 copy-done.5
  397.1 0.0 copy-done.3
  397.2 0.2 fusion.22
  397.3 0.0 copy-done.4
  397.3 0.1 select_reduce_fusion.1
  397.4 0.1 copy.26
  397.6 15.9 %all-to-all-done.1 = bf16[8,32,2304]{2,1,0:T(8,128)(2,1)S(1)} async-done(((bf16[8,32,2304]{2,1,0:T(8,128)(2,1)}), bf16[8,32,2304]{2,1,0:T(8,128)(2,1)S(1)}, u32[]{:S(2)}, u32[]{:S(2)}) %all-to-all-start.1) | async-done | bytes 1179680 | tf_op jit(solution)/shard_map/all_to_all | solution.py:189
  413.5 2.1 gather_fusion.1
  415.6 2.3 reshape.348
  417.9 0.0 copy-start.2
  417.9 0.0 copy-start.1
  418.0 2.5 multiply_reduce_fusion
  420.4 0.0 copy-done.2
  420.4 0.2 multiply_reduce_fusion.1
  420.6 0.9 multiply_convert_fusion
  421.6 0.0 copy-done.1
  (73 shorter events, 2.1 us)
Async XLA Ops:
  6.5 239.3 %copy-start = (bf16[1,360,2304]{2,1,0:T(8,128)(2,1)S(1)}, bf16[1,360,2304]{2,1,0:T(8,128)(2,1)}, u32[]{:S(2)}) copy-start(bf16[1,360,2304]{2,1,0:T(8,128)(2,1)} %param.30) | copy-start | bytes 4976644
  6.5 226.3 %all-gather.2.cloned.1.call-start = ((), (), s32[]{:S(2)}) async-start(), calls=%async_computation.3 | async-start | bytes 20054016 | tf_op jit(solution)/shard_map/all_gather | solution.py:183
  14.5 50.0 %copy-start.6 = (s32[96]{0:T(128)}, s32[96]{0:T(128)S(1)}, u32[]{:S(2)}) copy-start(s32[96]{0:T(128)S(1)} %convert_reduce_fusion) | copy-start | bytes 1156
  111.4 280.3 %reduce-scatter.2.cloned.1.call-start = ((), (), s32[]{:S(2)}) async-start(), calls=%async_computation.4 | async-start | bytes 20054016 | tf_op jit(solution)/shard_map/reduce_scatter | solution.py:188
  271.1 126.1 %copy-start.5 = (bf16[2304]{0:T(1024)(128)(2,1)S(1)}, bf16[2304]{0:T(1024)(128)(2,1)}, u32[]{:S(2)}) copy-start(bf16[2304]{0:T(1024)(128)(2,1)} %param.31) | copy-start | bytes 13828
  271.1 126.1 %copy-start.3 = (bf16[2304,8]{0,1:T(8,128)(2,1)S(1)}, bf16[2304,8]{0,1:T(8,128)(2,1)}, u32[]{:S(2)}) copy-start(bf16[2304,8]{0,1:T(8,128)(2,1)} %param.27) | copy-start | bytes 110596
  271.1 126.3 %copy-start.4 = (s32[96,2]{0,1:T(2,128)S(1)}, s32[96,2]{0,1:T(2,128)}, u32[]{:S(2)}) copy-start(s32[96,2]{0,1:T(2,128)} %param.25) | copy-start | bytes 2308
  391.6 21.9 %all-to-all-start.1 = ((bf16[8,32,2304]{2,1,0:T(8,128)(2,1)}), bf16[8,32,2304]{2,1,0:T(8,128)(2,1)S(1)}, u32[]{:S(2)}, u32[]{:S(2)}) async-start(bf16[8,32,2304]{2,1,0:T(8,128)(2,1)} %bitcast.112), calls=%async_computation.2 | async-start | bytes 2359296 | tf_op jit(solution)/shard_map/all_to_all | solution.py:189
  417.9 2.5 copy-start.2
  417.9 3.6 copy-start.1
Sparse Core Ops, SparseCore 0:
  111.5 121.3 all-gather.1
  271.2 120.4 reduce-scatter.1

commit v5 on v4

--- a/solution.py
+++ b/solution.py
@@ -83,19 +83,20 @@
     ends = jnp.cumsum(new_row_lengths)
     row_index = jnp.arange(row_count, dtype=jnp.int32)
     owner = jnp.sum((row_index[:, None] >= ends[None, :]).astype(jnp.int32), axis=1)
-    pages = store_count // PAGE
     entry = jnp.arange(page_row.shape[0], dtype=jnp.int32)
-    page_entry = jnp.sum(
-        jnp.where(page_row[None, :] == jnp.arange(pages, dtype=jnp.int32)[:, None], entry[None, :], 0),
-        axis=1,
-    )
     token_index = jnp.arange(store_count, dtype=jnp.int32)
-    token_entry = page_entry[token_index // PAGE]
+    hit = page_row[:, None] == (token_index // PAGE)[None, :]
+    token_entry = jnp.sum(jnp.where(hit, entry[:, None], 0), axis=0)
     token_request = token_entry // per_request
     position = (token_entry % per_request) * PAGE + token_index % PAGE
-    token_owner = jnp.where(
-        position < context_row_lengths[token_request], token_request, -1
-    ).astype(jnp.int32)
+    request_index = jnp.arange(requests, dtype=jnp.int32)
+    limit = jnp.sum(
+        jnp.where(
+            token_request[None, :] == request_index[:, None], context_row_lengths[:, None], 0
+        ),
+        axis=0,
+    )
+    token_owner = jnp.where(position < limit, token_request, -1).astype(jnp.int32)
     block = 2 * HEAD_DIM
     column = lambda count: pl.BlockSpec((count, block), lambda j: (0, j))
     whole = lambda shape: pl.BlockSpec(shape, lambda j: (0, 0))

time: 430 us -> 382 us (0.89)
  other arithmetic: 55.3 us -> 13.5 us
  local copies, waits for them, and re-layouts: 15 us -> 9.47 us
    gather x59 -> x0, other arithmetic: 41.8 us -> none  [attend(): token_entry = page_entry[token_index // PAGE]]
    gather x5 -> x0, local copies, waits for them, and re-layouts: 4.34 us -> none  [the longest x4 2.86 us: attend(): token_entry = page_entry[token_index // PAGE]]
where the time goes in v5:
time: 382 us; the launch traced here: 381 us
  waiting for transfers between devices  258 us (68%)
  matrix products  38.4 us (10%)
  blocking collectives  23.2 us (6%)
  Pallas kernels  19.4 us (5%)
  between operations  13.6 us (4%)
  other arithmetic  13.5 us (4%)
  local copies, waits for them, and re-layouts  9.47 us (2%)
  starting transfers between devices  5.76 us (2%)
    all_gather x1, waiting for transfers between devices, per_device(): arrived_rows = lax.all_gather(arrived, 'sh', axis=0, tiled=True)  121 us
    reduce_scatter x1, waiting for transfers between devices, per_device(): summed = lax.psum_scatter(partial, 'sh', scatter_dimension=0, tiled=True)  121 us
    dot_general x1, matrix products, per_device(): jnp.dot(hidden, down_weight[0], preferred_element_type=jnp.float32)  25.2 us
    all_to_all x1, blocking collectives, per_device(): lax.all_to_all(outgoing, 'ex', split_axis=0, concat_axis=0, tiled=True)  23.2 us
    pallas_call x1, Pallas kernels, attend(): pl.pallas_call(attention_kernel, grid=(width // block,), in_specs=[column...  19.4 us
    all_to_all x1, waiting for transfers between devices, per_device(): lax.all_to_all(summed.reshape(EXPERTS, MOST, width), 'ex', split_axis=0,...  15.9 us
    dot_general x1, matrix products, per_device(): jnp.dot(arrived_rows, gate_weight[0], preferred_element_type=jnp.float32)  13 us
  transfers between devices with their start and end apart: 3, of which 3 were waited for; matrix products, arithmetic and copies ran while one was open for 0% of the time, Pallas kernels for 0%

profile of v5, /device:TPU:1, one launch (start us, length us, event | category | flops | bytes accessed | tf_op | source)
XLA Modules:
  0.0 381.0 jit_solution(18381532362854523878)
XLA Ops:
  6.5 0.0 copy-start
  6.5 0.0 all-gather.2.cloned.1.call-start
  6.5 0.8 broadcast_multiply_fusion
  7.4 0.8 copy.28
  8.1 0.8 reduce-window.18
  9.0 0.1 convert_reduce_fusion
  9.0 0.0 copy-start.6
  9.0 0.8 select_reduce_fusion
  9.8 0.7 convert_element_type.32
  10.5 0.1 copy.27
  10.6 0.1 mul.92
  10.8 0.7 copy.25.owner_ref
  11.5 0.1 eq.76
  11.7 0.6 reduce-window.19
  12.2 0.2 slice_reduce_fusion
  12.5 0.1 add_bitcast_fusion
  12.6 1.2 scatter_custom_fusion.1
  13.8 1.2 scatter_custom_fusion
  15.1 0.1 broadcast_in_dim.92
  15.2 0.7 select_reduce_fusion.1
  15.9 0.6 compare_select_fusion.token_owner_ref
  16.6 0.0 copy-done.6
  16.6 19.4 %shard_map.154 = f32[96,2304]{1,0:T(8,128)} custom-call(bf16[96,2304]{1,0:T(8,128)(2,1)} %query_ref.1, bf16[1024,2304]{1,0:T(8,128)(2,1)} %pool_key_ref.1, bf16[96,2304]{1,0:T(8,128)(2,1)} %new_key_ref.1, bf16[1024,2304]{1,0:T(8,128)(2,1)} %pool_value_ref.1, bf16[96,2304]{1,0:T(8,128)(2,1)} %new_value_ref.1, bf16[96,2304]{1,0:T(8,128)(2,1)} %hidden_ref.1, ...), custom_call_target="tpu_custom_call" | custom-call | tf_op jit(solution)/shard_map/pallas_call | solution.py:103
  35.9 1.3 multiply_reduce_fusion.2
  37.3 1.3 multiply_convert_fusion.1
  38.6 1.4 gather_fusion
  40.0 0.1 broadcast_select_fusion
  40.2 23.2 %all_to_all.10 = bf16[8,32,2304]{2,1,0:T(8,128)(2,1)} all-to-all(bf16[8,32,2304]{2,1,0:T(8,128)(2,1)S(1)} %broadcast_select_fusion), channel_id=1, replica_groups=mesh['ex'=8,'sh'=16] {'ex'}, dimensions={0} | all-to-all | bytes 2359296 | tf_op jit(solution)/shard_map/all_to_all | solution.py:181
  63.4 0.0 all-gather.2.cloned.1.call-update
  63.4 0.2 reduce-scatter.2.cloned.1.call-start
  63.7 121.2 %all-gather.2.cloned.1.call-done = bf16[4096,2304]{1,0:T(8,128)(2,1)} async-done(((bf16[256,2304]{1,0:T(8,128)(2,1)}), bf16[4096,2304]{1,0:T(8,128)(2,1)}) %all-gather.2.cloned.1.call-update) | async-done | bytes 18874384 | tf_op jit(solution)/shard_map/all_gather | solution.py:184
  184.9 13.0 %fusion.5 = f32[4096,360]{0,1:T(8,128)} fusion(bf16[4096,2304]{1,0:T(8,128)(2,1)} %all-gather.2.cloned.1.call-done, bf16[1,2304,360]{1,2,0:T(8,128)(2,1)} %param.28), kind=kOutput, calls=%fused_computation.10 | convolution fusion | flops 6794772480 | bytes 26431488 | tf_op jit(solution)/shard_map/dot_general | solution.py:185
  197.9 0.0 copy-done
  197.9 25.2 %convolution_convert_fusion = bf16[4096,2304]{1,0:T(8,128)(2,1)} fusion(bf16[1,360,2304]{2,1,0:T(8,128)(2,1)S(1)} %copy-done, bf16[4096,2304]{1,0:T(8,128)(2,1)} %all-gather.2.cloned.1.call-done, f32[4096,360]{0,1:T(8,128)} %fusion.5, bf16[1,2304,360]{1,2,0:T(8,128)(2,1)} %param.29), kind=kOutput, calls=%fused_computation.4 | convolution fusion | flops 13607829504 | bytes 46964736 | tf_op jit(solution)/shard_map/dot_general | solution.py:188
  223.1 0.0 reduce-scatter.2.cloned.1.call-update
  223.1 0.0 copy-start.5
  223.1 0.0 copy-start.3
  223.1 0.0 copy-start.4
  223.2 120.5 %reduce-scatter.2.cloned.1.call-done = bf16[256,2304]{1,0:T(8,128)(2,1)} async-done(((bf16[4096,2304]{1,0:T(8,128)(2,1)}), bf16[256,2304]{1,0:T(8,128)(2,1)}) %reduce-scatter.2.cloned.1.call-update) | async-done | bytes 1179664 | tf_op jit(solution)/shard_map/reduce_scatter | solution.py:189
  343.7 5.5 %all-to-all-start.1 = ((bf16[8,32,2304]{2,1,0:T(8,128)(2,1)}), bf16[8,32,2304]{2,1,0:T(8,128)(2,1)S(1)}, u32[]{:S(2)}, u32[]{:S(2)}) async-start(bf16[8,32,2304]{2,1,0:T(8,128)(2,1)} %bitcast.40), calls=%async_computation.2 | async-start | bytes 2359296 | tf_op jit(solution)/shard_map/all_to_all | solution.py:190
  349.2 0.0 copy-done.5
  349.2 0.0 copy-done.3
  349.2 0.2 fusion.21
  349.4 0.0 copy-done.4
  349.4 0.1 select_reduce_fusion.2
  349.5 0.1 copy.26
  349.7 15.9 %all-to-all-done.1 = bf16[8,32,2304]{2,1,0:T(8,128)(2,1)S(1)} async-done(((bf16[8,32,2304]{2,1,0:T(8,128)(2,1)}), bf16[8,32,2304]{2,1,0:T(8,128)(2,1)S(1)}, u32[]{:S(2)}, u32[]{:S(2)}) %all-to-all-start.1) | async-done | bytes 1179680 | tf_op jit(solution)/shard_map/all_to_all | solution.py:190
  365.6 1.2 gather_fusion.1
  366.8 2.1 reshape.264
  368.9 0.0 copy-start.2
  368.9 0.0 copy-start.1
  368.9 4.1 %multiply_reduce_fusion = f32[96,2304]{1,0:T(8,128)S(1)} fusion(f32[96,2,2304]{2,1,0:T(2,128)} %reshape.264, f32[96,2]{1,0:T(8,128)S(1)} %copy.26), kind=kLoop, calls=%fused_computation.7 | loop fusion | flops 663552 | bytes 2654976 | tf_op jit(solution)/shard_map/reduce_sum | solution.py:195
  373.0 0.0 copy-done.2
  373.0 0.2 multiply_reduce_fusion.1
  373.2 0.9 multiply_convert_fusion
  374.2 0.0 copy-done.1
  (18 shorter events, 0.2 us)
Async XLA Ops:
  6.5 191.4 %copy-start = (bf16[1,360,2304]{2,1,0:T(8,128)(2,1)S(1)}, bf16[1,360,2304]{2,1,0:T(8,128)(2,1)}, u32[]{:S(2)}) copy-start(bf16[1,360,2304]{2,1,0:T(8,128)(2,1)} %param.30) | copy-start | bytes 4976644
  6.5 178.4 %all-gather.2.cloned.1.call-start = ((), (), s32[]{:S(2)}) async-start(), calls=%async_computation.3 | async-start | bytes 20054016 | tf_op jit(solution)/shard_map/all_gather | solution.py:184
  9.0 7.5 %copy-start.6 = (s32[96]{0:T(128)}, s32[96]{0:T(128)S(1)}, u32[]{:S(2)}) copy-start(s32[96]{0:T(128)S(1)} %convert_reduce_fusion) | copy-start | bytes 1156
  63.4 280.3 %reduce-scatter.2.cloned.1.call-start = ((), (), s32[]{:S(2)}) async-start(), calls=%async_computation.4 | async-start | bytes 20054016 | tf_op jit(solution)/shard_map/reduce_scatter | solution.py:189
  223.1 126.1 %copy-start.5 = (bf16[2304]{0:T(1024)(128)(2,1)S(1)}, bf16[2304]{0:T(1024)(128)(2,1)}, u32[]{:S(2)}) copy-start(bf16[2304]{0:T(1024)(128)(2,1)} %param.31) | copy-start | bytes 13828
  223.1 126.1 %copy-start.3 = (bf16[2304,8]{0,1:T(8,128)(2,1)S(1)}, bf16[2304,8]{0,1:T(8,128)(2,1)}, u32[]{:S(2)}) copy-start(bf16[2304,8]{0,1:T(8,128)(2,1)} %param.27) | copy-start | bytes 110596
  223.1 126.3 %copy-start.4 = (s32[96,2]{0,1:T(2,128)S(1)}, s32[96,2]{0,1:T(2,128)}, u32[]{:S(2)}) copy-start(s32[96,2]{0,1:T(2,128)} %param.25) | copy-start | bytes 2308
  343.7 21.9 %all-to-all-start.1 = ((bf16[8,32,2304]{2,1,0:T(8,128)(2,1)}), bf16[8,32,2304]{2,1,0:T(8,128)(2,1)S(1)}, u32[]{:S(2)}, u32[]{:S(2)}) async-start(bf16[8,32,2304]{2,1,0:T(8,128)(2,1)} %bitcast.40), calls=%async_computation.2 | async-start | bytes 2359296 | tf_op jit(solution)/shard_map/all_to_all | solution.py:190
  368.9 4.2 %copy-start.2 = (f32[96,2304]{1,0:T(8,128)S(1)}, f32[96,2304]{1,0:T(8,128)}, u32[]{:S(2)}) copy-start(f32[96,2304]{1,0:T(8,128)} %shard_map.154) | copy-start | bytes 2654212
  368.9 5.3 %copy-start.1 = (bf16[1,360,2304]{2,1,0:T(8,128)(2,1)S(1)}, bf16[1,360,2304]{2,1,0:T(8,128)(2,1)}, u32[]{:S(2)}) copy-start(bf16[1,360,2304]{2,1,0:T(8,128)(2,1)} %param.30) | copy-start | bytes 4976644
Sparse Core Ops, SparseCore 0:
  63.6 121.3 all-gather.1
  223.2 120.4 reduce-scatter.1

commit v6 on v5

--- a/solution.py
+++ b/solution.py
@@ -130,6 +130,36 @@
     )
 
 
+def ffn_kernel(rows_ref, gate_ref, up_ref, down_ref, out_ref):
+    rows = rows_ref[...]
+    gate_value = jnp.dot(rows, gate_ref[...], preferred_element_type=jnp.float32)
+    up_value = jnp.dot(rows, up_ref[...], preferred_element_type=jnp.float32)
+    hidden = (gate_value / (1.0 + jnp.exp(-gate_value)) * up_value).astype(jnp.bfloat16)
+    out_ref[...] = jnp.dot(hidden, down_ref[...], preferred_element_type=jnp.float32).astype(
+        out_ref.dtype
+    )
+
+
+def expert_ffn(rows, gate, up, down):
+    count, width = rows.shape
+    units = gate.shape[1]
+    tile = 512
+    fixed = lambda shape: pl.BlockSpec(shape, lambda i: (0, 0))
+    return pl.pallas_call(
+        ffn_kernel,
+        grid=(count // tile,),
+        in_specs=[
+            pl.BlockSpec((tile, width), lambda i: (i, 0)),
+            fixed((width, units)),
+            fixed((width, units)),
+            fixed((units, width)),
+        ],
+        out_specs=pl.BlockSpec((tile, width), lambda i: (i, 0)),
+        out_shape=jax.ShapeDtypeStruct((count, width), jnp.bfloat16),
+        interpret=INTERPRET,
+    )(rows, gate, up, down)
+
+
 def per_device(
     hidden_in,
     queries,
@@ -182,10 +212,7 @@
         groups * MOST, width
     )
     arrived_rows = lax.all_gather(arrived, "sh", axis=0, tiled=True)
-    gate_value = jnp.dot(arrived_rows, gate_weight[0], preferred_element_type=jnp.float32)
-    up_value = jnp.dot(arrived_rows, up_weight[0], preferred_element_type=jnp.float32)
-    hidden = (jax.nn.silu(gate_value) * up_value).astype(jnp.bfloat16)
-    partial = jnp.dot(hidden, down_weight[0], preferred_element_type=jnp.float32).astype(jnp.bfloat16)
+    partial = expert_ffn(arrived_rows, gate_weight[0], up_weight[0], down_weight[0])
     summed = lax.psum_scatter(partial, "sh", scatter_dimension=0, tiled=True)
     returned = lax.all_to_all(
         summed.reshape(EXPERTS, MOST, width), "ex", split_axis=0, concat_axis=0, tiled=True

time: 382 us -> 377 us (0.987)
  matrix products: 38.4 us -> 0.19 us
  Pallas kernels: 19.4 us -> 55.8 us
  waiting for transfers between devices: 258 us -> 252 us
  local copies, waits for them, and re-layouts: 9.47 us -> 14.2 us
    dot_general x2 -> x0, matrix products: 38.2 us -> none  [the longest x1 25.2 us: per_device(): jnp.dot(hidden, down_weight[0], preferred_element_type=jnp.float32)]
    pallas_call x0 -> x1, Pallas kernels: none -> 36.5 us  [expert_ffn(): pl.pallas_call(ffn_kernel, grid=(count // tile,), in_specs=[pl.BlockSpec(...]
    unnamed x15, local copies, waits for them, and re-layouts: 0.81 us -> 6.8 us
    all_gather x1, waiting for transfers between devices: 121 us -> 115 us  [per_device(): arrived_rows = lax.all_gather(arrived, 'sh', axis=0, tiled=True)]
  transfers between devices with their start and end apart: 3 -> 3, of which waited for: 3 -> 3; matrix products, arithmetic and copies ran while one was open for 0% -> 2% of each run, Pallas kernels for 0% -> 0%
where the time goes in v6:
time: 377 us; the launch traced here: 376 us
  waiting for transfers between devices  252 us (67%)
  Pallas kernels  55.8 us (15%)
  blocking collectives  23.3 us (6%)
  local copies, waits for them, and re-layouts  14.2 us (4%)
  between operations  13.6 us (4%)
  other arithmetic  11.7 us (3%)
  starting transfers between devices  5.61 us (1%)
    reduce_scatter x1, waiting for transfers between devices, per_device(): summed = lax.psum_scatter(partial, 'sh', scatter_dimension=0, tiled=True)  120 us
    all_gather x1, waiting for transfers between devices, per_device(): arrived_rows = lax.all_gather(arrived, 'sh', axis=0, tiled=True)  115 us
    pallas_call x1, Pallas kernels, expert_ffn(): pl.pallas_call(ffn_kernel, grid=(count // tile,), in_specs=[pl.BlockSpec(...  36.5 us
    all_to_all x1, blocking collectives, per_device(): lax.all_to_all(outgoing, 'ex', split_axis=0, concat_axis=0, tiled=True)  23.3 us
    pallas_call x1, Pallas kernels, attend(): pl.pallas_call(attention_kernel, grid=(width // block,), in_specs=[column...  19.4 us
    all_to_all x1, waiting for transfers between devices, per_device(): lax.all_to_all(summed.reshape(EXPERTS, MOST, width), 'ex', split_axis=0,...  15.9 us
  transfers between devices with their start and end apart: 3, of which 3 were waited for; matrix products, arithmetic and copies ran while one was open for 2% of the time, Pallas kernels for 0%

profile of v6, /device:TPU:1, one launch (start us, length us, event | category | flops | bytes accessed | tf_op | source)
XLA Modules:
  0.0 376.4 jit_solution(11081540197142924257)
XLA Ops:
  6.5 0.0 copy-start
  6.5 0.0 all-gather.2.cloned.1.call-start
  6.5 0.7 broadcast_multiply_fusion
  7.2 0.8 copy.32
  8.0 0.8 reduce-window.18
  8.8 0.1 convert_reduce_fusion
  8.9 0.0 copy-start.5
  8.9 0.8 select_reduce_fusion
  9.7 0.7 convert_element_type.26
  10.4 0.1 copy.31
  10.5 0.1 mul.85
  10.6 0.7 copy.29.owner_ref
  11.4 0.1 eq.76
  11.5 0.6 reduce-window.19
  12.1 0.2 slice_reduce_fusion
  12.4 0.1 add_bitcast_fusion
  12.5 1.2 scatter_custom_fusion.1
  13.7 1.2 scatter_custom_fusion
  15.0 0.1 broadcast_in_dim.92
  15.1 0.7 select_reduce_fusion.1
  15.8 0.6 compare_select_fusion.token_owner_ref
  16.4 0.0 copy-done.5
  16.4 19.4 %shard_map.154 = f32[96,2304]{1,0:T(8,128)} custom-call(bf16[96,2304]{1,0:T(8,128)(2,1)} %query_ref.1, bf16[1024,2304]{1,0:T(8,128)(2,1)} %pool_key_ref.1, bf16[96,2304]{1,0:T(8,128)(2,1)} %new_key_ref.1, bf16[1024,2304]{1,0:T(8,128)(2,1)} %pool_value_ref.1, bf16[96,2304]{1,0:T(8,128)(2,1)} %new_value_ref.1, bf16[96,2304]{1,0:T(8,128)(2,1)} %hidden_ref.1, ...), custom_call_target="tpu_custom_call" | custom-call | tf_op jit(solution)/shard_map/pallas_call | solution.py:103
  35.8 1.3 multiply_reduce_fusion.2
  37.1 1.3 multiply_convert_fusion.1
  38.5 1.4 gather_fusion
  39.9 0.1 broadcast_select_fusion
  40.1 0.0 copy-start.2
  40.1 23.3 %all_to_all.10 = bf16[8,32,2304]{2,1,0:T(8,128)(2,1)} all-to-all(bf16[8,32,2304]{2,1,0:T(8,128)(2,1)S(1)} %broadcast_select_fusion), channel_id=1, replica_groups=mesh['ex'=8,'sh'=16] {'ex'}, dimensions={0} | all-to-all | bytes 2359296 | tf_op jit(solution)/shard_map/all_to_all | solution.py:211
  63.4 0.0 all-gather.2.cloned.1.call-update
  63.4 0.0 reduce-scatter.2.cloned.1.call-start
  63.5 0.0 copy-done.2
  63.5 2.2 copy.33
  65.7 3.8 %copy.34 = bf16[1,2304,360]{2,1,0:T(8,128)(2,1)} copy(bf16[1,2304,360]{1,2,0:T(8,128)(2,1)} %param.29) | data formatting | bytes 3317760 | tf_op args[13]
  69.5 115.4 %all-gather.2.cloned.1.call-done.rows_ref = bf16[4096,2304]{1,0:T(8,128)(2,1)} async-done(((bf16[256,2304]{1,0:T(8,128)(2,1)}), bf16[4096,2304]{1,0:T(8,128)(2,1)}) %all-gather.2.cloned.1.call-update) | async-done | bytes 18874384 | tf_op jit(solution)/shard_map/all_gather | solution.py:214
  184.9 36.5 %shard_map.155 = bf16[4096,2304]{1,0:T(8,128)(2,1)} custom-call(bf16[4096,2304]{1,0:T(8,128)(2,1)} %all-gather.2.cloned.1.call-done.rows_ref, bf16[2304,360]{1,0:T(8,128)(2,1)} %bitcast.28, bf16[2304,360]{1,0:T(8,128)(2,1)} %bitcast.29, bf16[360,2304]{1,0:T(8,128)(2,1)} %bitcast.32), custom_call_target="tpu_custom_call" | custom-call | tf_op jit(solution)/shard_map/pallas_call | solution.py:148
  221.4 0.0 reduce-scatter.2.cloned.1.call-update
  221.4 0.0 copy-start.4
  221.4 0.0 copy-start.3
  221.4 120.5 %reduce-scatter.2.cloned.1.call-done = bf16[256,2304]{1,0:T(8,128)(2,1)} async-done(((bf16[4096,2304]{1,0:T(8,128)(2,1)}), bf16[256,2304]{1,0:T(8,128)(2,1)}) %reduce-scatter.2.cloned.1.call-update) | async-done | bytes 1179664 | tf_op jit(solution)/shard_map/reduce_scatter | solution.py:216
  341.9 5.6 %all-to-all-start.1 = ((bf16[8,32,2304]{2,1,0:T(8,128)(2,1)}), bf16[8,32,2304]{2,1,0:T(8,128)(2,1)S(1)}, u32[]{:S(2)}, u32[]{:S(2)}) async-start(bf16[8,32,2304]{2,1,0:T(8,128)(2,1)} %bitcast.33), calls=%async_computation.2 | async-start | bytes 2359296 | tf_op jit(solution)/shard_map/all_to_all | solution.py:217
  347.5 0.0 copy-done.4
  347.5 0.0 copy-done
  347.5 0.2 fusion.13
  347.7 0.0 copy-done.3
  347.7 0.1 select_reduce_fusion.2
  347.8 0.1 copy.30
  347.9 15.9 %all-to-all-done.1 = bf16[8,32,2304]{2,1,0:T(8,128)(2,1)S(1)} async-done(((bf16[8,32,2304]{2,1,0:T(8,128)(2,1)}), bf16[8,32,2304]{2,1,0:T(8,128)(2,1)S(1)}, u32[]{:S(2)}, u32[]{:S(2)}) %all-to-all-start.1) | async-done | bytes 1179680 | tf_op jit(solution)/shard_map/all_to_all | solution.py:217
  363.9 1.2 gather_fusion.1
  365.1 0.9 reshape.264
  365.9 0.0 copy-start.1
  365.9 2.5 multiply_reduce_fusion
  368.5 0.0 copy-done.1
  368.5 0.2 multiply_reduce_fusion.1
  368.7 0.9 multiply_convert_fusion
  (18 shorter events, 0.2 us)
Async XLA Ops:
  6.5 341.0 %copy-start = (bf16[2304,8]{0,1:T(8,128)(2,1)S(1)}, bf16[2304,8]{0,1:T(8,128)(2,1)}, u32[]{:S(2)}) copy-start(bf16[2304,8]{0,1:T(8,128)(2,1)} %param.27) | copy-start | bytes 110596
  6.5 178.4 %all-gather.2.cloned.1.call-start = ((), (), s32[]{:S(2)}) async-start(), calls=%async_computation.3 | async-start | bytes 20054016 | tf_op jit(solution)/shard_map/all_gather | solution.py:214
  8.9 7.5 %copy-start.5 = (s32[96]{0:T(128)}, s32[96]{0:T(128)S(1)}, u32[]{:S(2)}) copy-start(s32[96]{0:T(128)S(1)} %convert_reduce_fusion) | copy-start | bytes 1156
  40.1 23.4 %copy-start.2 = (bf16[1,2304,360]{1,2,0:T(8,128)(2,1)S(1)}, bf16[1,2304,360]{1,2,0:T(8,128)(2,1)}, u32[]{:S(2)}) copy-start(bf16[1,2304,360]{1,2,0:T(8,128)(2,1)} %param.28) | copy-start | bytes 4976644
  63.4 278.5 %reduce-scatter.2.cloned.1.call-start = ((), (), s32[]{:S(2)}) async-start(), calls=%async_computation.4 | async-start | bytes 20054016 | tf_op jit(solution)/shard_map/reduce_scatter | solution.py:216
  221.4 126.1 %copy-start.4 = (bf16[2304]{0:T(1024)(128)(2,1)S(1)}, bf16[2304]{0:T(1024)(128)(2,1)}, u32[]{:S(2)}) copy-start(bf16[2304]{0:T(1024)(128)(2,1)} %param.31) | copy-start | bytes 13828
  221.4 126.3 %copy-start.3 = (s32[96,2]{0,1:T(2,128)S(1)}, s32[96,2]{0,1:T(2,128)}, u32[]{:S(2)}) copy-start(s32[96,2]{0,1:T(2,128)} %param.25) | copy-start | bytes 2308
  341.9 21.9 %all-to-all-start.1 = ((bf16[8,32,2304]{2,1,0:T(8,128)(2,1)}), bf16[8,32,2304]{2,1,0:T(8,128)(2,1)S(1)}, u32[]{:S(2)}, u32[]{:S(2)}) async-start(bf16[8,32,2304]{2,1,0:T(8,128)(2,1)} %bitcast.33), calls=%async_computation.2 | async-start | bytes 2359296 | tf_op jit(solution)/shard_map/all_to_all | solution.py:217
  365.9 2.5 copy-start.1
Sparse Core Ops, SparseCore 0:
  63.6 121.3 all-gather.1
  221.5 120.3 reduce-scatter.1

commit v7 on v6

--- a/solution.py
+++ b/solution.py
@@ -160,6 +160,14 @@
     )(rows, gate, up, down)
 
 
+def shift_exchange(pieces, groups, sign):
+    moved = [pieces[0]]
+    for shift in range(1, groups):
+        pairs = [(i, (i + sign * shift) % groups) for i in range(groups)]
+        moved.append(lax.ppermute(pieces[shift], "ex", pairs))
+    return jnp.stack(moved)
+
+
 def per_device(
     hidden_in,
     queries,
@@ -201,22 +209,19 @@
     onehot = (entries[:, None] == expert_range[None, :]).astype(jnp.int32)
     before = jnp.cumsum(onehot, axis=0) - onehot
     slot_index = jnp.sum(before * onehot, axis=1)
-    target = entries * MOST + slot_index
+    me = lax.axis_index("ex")
+    target = ((entries - me) % groups) * MOST + slot_index
     entry_rows = jnp.arange(entries.shape[0], dtype=jnp.int32) // top_count
     source_row = jnp.zeros((EXPERTS * MOST,), jnp.int32).at[target].set(entry_rows)
     filled = jnp.zeros((EXPERTS * MOST,), jnp.bool_).at[target].set(True)
     outgoing = jnp.where(filled[:, None], normed[source_row], jnp.zeros((), jnp.bfloat16)).reshape(
         EXPERTS, MOST, width
     )
-    arrived = lax.all_to_all(outgoing, "ex", split_axis=0, concat_axis=0, tiled=True).reshape(
-        groups * MOST, width
-    )
+    arrived = shift_exchange(outgoing, groups, 1).reshape(groups * MOST, width)
     arrived_rows = lax.all_gather(arrived, "sh", axis=0, tiled=True)
     partial = expert_ffn(arrived_rows, gate_weight[0], up_weight[0], down_weight[0])
     summed = lax.psum_scatter(partial, "sh", scatter_dimension=0, tiled=True)
-    returned = lax.all_to_all(
-        summed.reshape(EXPERTS, MOST, width), "ex", split_axis=0, concat_axis=0, tiled=True
-    )
+    returned = shift_exchange(summed.reshape(groups, MOST, width), groups, -1)
     flat_results = returned.reshape(EXPERTS * MOST, width)
     picked = flat_results[target].reshape(row_count, top_count, width)
     mixed = resid + jnp.sum(route_weights[:, :, None] * picked.astype(jnp.float32), axis=1)

time: 377 us -> 390 us (1.034)
  blocking collectives: 23.3 us -> 0 us
  starting transfers between devices: 5.61 us -> 22.1 us
  local copies, waits for them, and re-layouts: 14.2 us -> 24.9 us
  waiting for transfers between devices: 252 us -> 262 us
    ppermute x0 -> x14, waiting for transfers between devices: none -> 24.1 us  [shift_exchange(): moved.append(lax.ppermute(pieces[shift], 'ex', pairs))]
    all_to_all x1 -> x0, blocking collectives: 23.3 us -> none  [per_device(): lax.all_to_all(outgoing, 'ex', split_axis=0, concat_axis=0, tiled=True)]
    ppermute x0 -> x14, starting transfers between devices: none -> 22.1 us  [shift_exchange(): moved.append(lax.ppermute(pieces[shift], 'ex', pairs))]
    all_to_all x1 -> x0, waiting for transfers between devices: 15.9 us -> none  [per_device(): lax.all_to_all(summed.reshape(EXPERTS, MOST, width), 'ex', split_axis=0,...]
    unnamed x15 -> x29, local copies, waits for them, and re-layouts: 6.8 us -> 13.1 us
    all_to_all x1 -> x0, starting transfers between devices: 5.57 us -> none  [per_device(): lax.all_to_all(summed.reshape(EXPERTS, MOST, width), 'ex', split_axis=0,...]
  transfers between devices with their start and end apart: 3 -> 16, of which waited for: 3 -> 8; matrix products, arithmetic and copies ran while one was open for 2% -> 3% of each run, Pallas kernels for 0% -> 0%
where the time goes in v7:
time: 390 us; the launch traced here: 389 us
  waiting for transfers between devices  262 us (67%)
  Pallas kernels  55.8 us (14%)
  local copies, waits for them, and re-layouts  24.9 us (6%)
  starting transfers between devices  22.1 us (6%)
  between operations  13.7 us (4%)
  other arithmetic  10.6 us (3%)
    reduce_scatter x1, waiting for transfers between devices, per_device(): summed = lax.psum_scatter(partial, 'sh', scatter_dimension=0, tiled=True)  119 us
    all_gather x1, waiting for transfers between devices, per_device(): arrived_rows = lax.all_gather(arrived, 'sh', axis=0, tiled=True)  118 us
    pallas_call x1, Pallas kernels, expert_ffn(): pl.pallas_call(ffn_kernel, grid=(count // tile,), in_specs=[pl.BlockSpec(...  36.5 us
    ppermute x14, waiting for transfers between devices, shift_exchange(): moved.append(lax.ppermute(pieces[shift], 'ex', pairs))  24.1 us
    ppermute x14, starting transfers between devices, shift_exchange(): moved.append(lax.ppermute(pieces[shift], 'ex', pairs))  22.1 us
    pallas_call x1, Pallas kernels, attend(): pl.pallas_call(attention_kernel, grid=(width // block,), in_specs=[column...  19.4 us
    unnamed x29, local copies, waits for them, and re-layouts  13.1 us
  transfers between devices with their start and end apart: 16, of which 8 were waited for; matrix products, arithmetic and copies ran while one was open for 3% of the time, Pallas kernels for 0%

profile of v7, /device:TPU:1, one launch (start us, length us, event | category | flops | bytes accessed | tf_op | source)
XLA Modules:
  0.0 389.0 jit_solution(17711782184908403830)
XLA Ops:
  6.6 0.8 reduce-window.18
  7.4 0.1 convert_reduce_fusion
  7.5 0.8 copy.32
  8.2 0.7 broadcast_subtract_fusion
  8.9 0.8 select_reduce_fusion
  9.7 0.7 convert_element_type.26
  10.4 0.1 copy.31
  10.5 0.1 sub.42
  10.6 0.7 copy.29.owner_ref
  11.4 0.1 eq.78
  11.5 0.6 reduce-window.19
  12.1 0.2 slice_reduce_fusion
  12.4 0.1 add_bitcast_fusion
  12.5 1.2 scatter_custom_fusion.1
  13.7 0.7 select_reduce_fusion.1
  14.5 0.6 compare_select_fusion.token_owner_ref
  15.1 19.4 %shard_map.154 = f32[96,2304]{1,0:T(8,128)} custom-call(bf16[96,2304]{1,0:T(8,128)(2,1)} %query_ref.1, bf16[1024,2304]{1,0:T(8,128)(2,1)} %pool_key_ref.1, bf16[96,2304]{1,0:T(8,128)(2,1)} %new_key_ref.1, bf16[1024,2304]{1,0:T(8,128)(2,1)} %pool_value_ref.1, bf16[96,2304]{1,0:T(8,128)(2,1)} %new_value_ref.1, bf16[96,2304]{1,0:T(8,128)(2,1)} %hidden_ref.1, ...), custom_call_target="tpu_custom_call" | custom-call | tf_op jit(solution)/shard_map/pallas_call | solution.py:103
  34.5 1.4 multiply_reduce_fusion.2
  35.9 1.3 scatter_custom_fusion
  37.2 0.1 multiply_convert_fusion.1
  37.3 1.4 gather_fusion
  38.7 0.1 broadcast_select_fusion
  38.9 0.1 fusion.19
  39.0 1.4 collective-permute-start.6
  40.4 3.9 collective-permute-start.5
  44.3 0.4 collective-permute-start.4
  44.6 2.8 collective-permute-start.3
  47.4 0.7 fusion.1
  48.1 4.6 %collective-permute-done = bf16[32,2304]{1,0:T(8,128)(2,1)S(1)} collective-permute-done((bf16[32,2304]{1,0:T(8,128)(2,1)S(1)}, bf16[32,2304]{1,0:T(8,128)(2,1)S(1)}, u32[]{:S(2)}, u32[]{:S(2)}) %collective-permute-start) | collective-permute-done | bytes 147488 | tf_op jit(solution)/shard_map/ppermute | solution.py:167
  52.7 0.7 bitcast_dynamic-update-slice_fusion.13
  53.4 4.5 %collective-permute-done.1 = bf16[32,2304]{1,0:T(8,128)(2,1)S(1)} collective-permute-done((bf16[32,2304]{1,0:T(8,128)(2,1)S(1)}, bf16[32,2304]{1,0:T(8,128)(2,1)S(1)}, u32[]{:S(2)}, u32[]{:S(2)}) %collective-permute-start.1) | collective-permute-done | bytes 147488 | tf_op jit(solution)/shard_map/ppermute | solution.py:167
  57.9 2.7 collective-permute-start.2
  60.6 0.7 bitcast_dynamic-update-slice_fusion.12
  61.3 2.4 collective-permute-done.2
  63.7 0.7 bitcast_dynamic-update-slice_fusion.11
  64.3 0.7 bitcast_dynamic-update-slice_fusion.10
  65.0 0.7 bitcast_dynamic-update-slice_fusion.9
  65.7 0.7 bitcast_dynamic-update-slice_fusion.8
  66.4 0.7 bitcast_dynamic-update-slice_fusion.7
  67.1 2.2 copy.33
  69.3 3.8 copy.34
  73.1 118.0 %all-gather.2.cloned.1.call-done.rows_ref = bf16[4096,2304]{1,0:T(8,128)(2,1)} async-done(((bf16[256,2304]{1,0:T(8,128)(2,1)}), bf16[4096,2304]{1,0:T(8,128)(2,1)}) %all-gather.2.cloned.1.call-update) | async-done | bytes 18874384 | tf_op jit(solution)/shard_map/all_gather | solution.py:221
  191.2 36.5 %shard_map.155 = bf16[4096,2304]{1,0:T(8,128)(2,1)} custom-call(bf16[4096,2304]{1,0:T(8,128)(2,1)} %all-gather.2.cloned.1.call-done.rows_ref, bf16[2304,360]{1,0:T(8,128)(2,1)} %bitcast.62, bf16[2304,360]{1,0:T(8,128)(2,1)} %bitcast.63, bf16[360,2304]{1,0:T(8,128)(2,1)} %bitcast.64), custom_call_target="tpu_custom_call" | custom-call | tf_op jit(solution)/shard_map/pallas_call | solution.py:148
  227.6 0.7 copy-done.4
  228.3 0.2 fusion.20
  228.6 0.1 copy.30
  228.7 119.5 %reduce-scatter.2.cloned.1.call-done = bf16[256,2304]{1,0:T(8,128)(2,1)} async-done(((bf16[4096,2304]{1,0:T(8,128)(2,1)}), bf16[256,2304]{1,0:T(8,128)(2,1)}) %reduce-scatter.2.cloned.1.call-update) | async-done | bytes 1179664 | tf_op jit(solution)/shard_map/reduce_scatter | solution.py:223
  348.2 1.4 fusion.18
  349.6 2.3 collective-permute-start.13
  351.8 1.3 collective-permute-start.12
  353.1 1.7 collective-permute-start.11
  354.8 0.4 collective-permute-start.10
  355.2 1.2 collective-permute-start.7
  356.4 0.9 fusion
  357.3 5.2 %collective-permute-done.7 = bf16[32,2304]{1,0:T(8,128)(2,1)S(1)} collective-permute-done((bf16[32,2304]{1,0:T(8,128)(2,1)S(1)}, bf16[32,2304]{1,0:T(8,128)(2,1)S(1)}, u32[]{:S(2)}, u32[]{:S(2)}) %collective-permute-start.7) | collective-permute-done | bytes 147488 | tf_op jit(solution)/shard_map/ppermute | solution.py:167
  362.5 2.1 collective-permute-start.8
  364.5 3.4 collective-permute-done.8
  367.9 2.1 collective-permute-start.9
  370.0 4.0 %collective-permute-done.9 = bf16[32,2304]{1,0:T(8,128)(2,1)S(1)} collective-permute-done((bf16[32,2304]{1,0:T(8,128)(2,1)S(1)}, bf16[32,2304]{1,0:T(8,128)(2,1)S(1)}, u32[]{:S(2)}, u32[]{:S(2)}) %collective-permute-start.9) | collective-permute-done | bytes 147488 | tf_op jit(solution)/shard_map/ppermute | solution.py:167
  374.1 2.1 gather_fusion.1
  376.3 2.3 reshape.321
  378.6 2.5 multiply_reduce_fusion
  381.1 0.2 multiply_reduce_fusion.1
  381.3 0.9 multiply_convert_fusion
  (51 shorter events, 0.5 us)
Async XLA Ops:
  6.5 221.8 %copy-start = (bf16[2304,8]{0,1:T(8,128)(2,1)S(1)}, bf16[2304,8]{0,1:T(8,128)(2,1)}, u32[]{:S(2)}) copy-start(bf16[2304,8]{0,1:T(8,128)(2,1)} %param.27) | copy-start | bytes 110596
  6.5 184.6 %all-gather.2.cloned.1.call-start = ((), (), s32[]{:S(2)}) async-start(), calls=%async_computation.1 | async-start | bytes 20054016 | tf_op jit(solution)/shard_map/all_gather | solution.py:221
  7.5 7.6 %copy-start.5 = (s32[96]{0:T(128)}, s32[96]{0:T(128)S(1)}, u32[]{:S(2)}) copy-start(s32[96]{0:T(128)S(1)} %convert_reduce_fusion) | copy-start | bytes 1156
  34.5 2.7 copy-start.1
  39.0 27.4 %collective-permute-start.6 = (bf16[32,2304]{1,0:T(8,128)(2,1)S(1)}, bf16[32,2304]{1,0:T(8,128)(2,1)S(1)}, u32[]{:S(2)}, u32[]{:S(2)}) collective-permute-start(bf16[32,2304]{1,0:T(8,128)(2,1)S(1)} %get-tuple-element.14), channel_id=1, source_target_pairs={{0,112},{16,0},{32,16},{48,32},{64,48},{80,64},{96,80},{112,96},{1... | collective-permute-start | bytes 442376 | tf_op jit(solution)/shard_map/ppermute | solution.py:167
  40.4 25.3 %collective-permute-start.5 = (bf16[32,2304]{1,0:T(8,128)(2,1)S(1)}, bf16[32,2304]{1,0:T(8,128)(2,1)S(1)}, u32[]{:S(2)}, u32[]{:S(2)}) collective-permute-start(bf16[32,2304]{1,0:T(8,128)(2,1)S(1)} %get-tuple-element.15), channel_id=1, source_target_pairs={{0,96},{16,112},{32,0},{48,16},{64,32},{80,48},{96,64},{112,80},{1... | collective-permute-start | bytes 442376 | tf_op jit(solution)/shard_map/ppermute | solution.py:167
  44.3 20.8 %collective-permute-start.4 = (bf16[32,2304]{1,0:T(8,128)(2,1)S(1)}, bf16[32,2304]{1,0:T(8,128)(2,1)S(1)}, u32[]{:S(2)}, u32[]{:S(2)}) collective-permute-start(bf16[32,2304]{1,0:T(8,128)(2,1)S(1)} %get-tuple-element.16), channel_id=1, source_target_pairs={{0,80},{16,96},{32,112},{48,0},{64,16},{80,32},{96,48},{112,64},{1... | collective-permute-start | bytes 442376 | tf_op jit(solution)/shard_map/ppermute | solution.py:167
  44.6 19.7 %collective-permute-start.3 = (bf16[32,2304]{1,0:T(8,128)(2,1)S(1)}, bf16[32,2304]{1,0:T(8,128)(2,1)S(1)}, u32[]{:S(2)}, u32[]{:S(2)}) collective-permute-start(bf16[32,2304]{1,0:T(8,128)(2,1)S(1)} %get-tuple-element.17), channel_id=1, source_target_pairs={{0,64},{16,80},{32,96},{48,112},{64,0},{80,16},{96,32},{112,48},{1... | collective-permute-start | bytes 442376 | tf_op jit(solution)/shard_map/ppermute | solution.py:167
  47.4 5.3 %collective-permute-start = (bf16[32,2304]{1,0:T(8,128)(2,1)S(1)}, bf16[32,2304]{1,0:T(8,128)(2,1)S(1)}, u32[]{:S(2)}, u32[]{:S(2)}) collective-permute-start(bf16[32,2304]{1,0:T(8,128)(2,1)S(1)} %get-tuple-element.20), channel_id=1, source_target_pairs={{0,16},{16,32},{32,48},{48,64},{64,80},{80,96},{96,112},{112,0},{1... | collective-permute-start | bytes 442376 | tf_op jit(solution)/shard_map/ppermute | solution.py:167
  52.7 5.2 %collective-permute-start.1 = (bf16[32,2304]{1,0:T(8,128)(2,1)S(1)}, bf16[32,2304]{1,0:T(8,128)(2,1)S(1)}, u32[]{:S(2)}, u32[]{:S(2)}) collective-permute-start(bf16[32,2304]{1,0:T(8,128)(2,1)S(1)} %get-tuple-element.19), channel_id=1, source_target_pairs={{0,32},{16,48},{32,64},{48,80},{64,96},{80,112},{96,0},{112,16},{1... | collective-permute-start | bytes 442376 | tf_op jit(solution)/shard_map/ppermute | solution.py:167
  57.9 5.8 %collective-permute-start.2 = (bf16[32,2304]{1,0:T(8,128)(2,1)S(1)}, bf16[32,2304]{1,0:T(8,128)(2,1)S(1)}, u32[]{:S(2)}, u32[]{:S(2)}) collective-permute-start(bf16[32,2304]{1,0:T(8,128)(2,1)S(1)} %get-tuple-element.18), channel_id=1, source_target_pairs={{0,48},{16,64},{32,80},{48,96},{64,112},{80,0},{96,16},{112,32},{1... | collective-permute-start | bytes 442376 | tf_op jit(solution)/shard_map/ppermute | solution.py:167
  64.3 2.8 copy-start.2
  67.1 281.2 %reduce-scatter.2.cloned.1.call-start = ((), (), s32[]{:S(2)}) async-start(), calls=%async_computation.2 | async-start | bytes 20054016 | tf_op jit(solution)/shard_map/reduce_scatter | solution.py:223
  227.6 0.7 copy-start.4
  227.6 0.9 copy-start.3
  349.6 24.5 %collective-permute-start.13 = (bf16[32,2304]{1,0:T(8,128)(2,1)S(1)}, bf16[32,2304]{1,0:T(8,128)(2,1)S(1)}, u32[]{:S(2)}, u32[]{:S(2)}) collective-permute-start(bf16[32,2304]{1,0:T(8,128)(2,1)S(1)} %get-tuple-element.7), channel_id=1, source_target_pairs={{0,16},{16,32},{32,48},{48,64},{64,80},{80,96},{96,112},{112,0},{1... | collective-permute-start | bytes 442376 | tf_op jit(solution)/shard_map/ppermute | solution.py:167
  351.8 22.2 %collective-permute-start.12 = (bf16[32,2304]{1,0:T(8,128)(2,1)S(1)}, bf16[32,2304]{1,0:T(8,128)(2,1)S(1)}, u32[]{:S(2)}, u32[]{:S(2)}) collective-permute-start(bf16[32,2304]{1,0:T(8,128)(2,1)S(1)} %get-tuple-element.8), channel_id=1, source_target_pairs={{0,32},{16,48},{32,64},{48,80},{64,96},{80,112},{96,0},{112,16},{1... | collective-permute-start | bytes 442376 | tf_op jit(solution)/shard_map/ppermute | solution.py:167
  353.1 20.9 %collective-permute-start.11 = (bf16[32,2304]{1,0:T(8,128)(2,1)S(1)}, bf16[32,2304]{1,0:T(8,128)(2,1)S(1)}, u32[]{:S(2)}, u32[]{:S(2)}) collective-permute-start(bf16[32,2304]{1,0:T(8,128)(2,1)S(1)} %get-tuple-element.9), channel_id=1, source_target_pairs={{0,48},{16,64},{32,80},{48,96},{64,112},{80,0},{96,16},{112,32},{1... | collective-permute-start | bytes 442376 | tf_op jit(solution)/shard_map/ppermute | solution.py:167
  354.8 19.2 %collective-permute-start.10 = (bf16[32,2304]{1,0:T(8,128)(2,1)S(1)}, bf16[32,2304]{1,0:T(8,128)(2,1)S(1)}, u32[]{:S(2)}, u32[]{:S(2)}) collective-permute-start(bf16[32,2304]{1,0:T(8,128)(2,1)S(1)} %get-tuple-element.10), channel_id=1, source_target_pairs={{0,64},{16,80},{32,96},{48,112},{64,0},{80,16},{96,32},{112,48},{1... | collective-permute-start | bytes 442376 | tf_op jit(solution)/shard_map/ppermute | solution.py:167
  355.2 7.3 %collective-permute-start.7 = (bf16[32,2304]{1,0:T(8,128)(2,1)S(1)}, bf16[32,2304]{1,0:T(8,128)(2,1)S(1)}, u32[]{:S(2)}, u32[]{:S(2)}) collective-permute-start(bf16[32,2304]{1,0:T(8,128)(2,1)S(1)} %get-tuple-element.13), channel_id=1, source_target_pairs={{0,112},{16,0},{32,16},{48,32},{64,48},{80,64},{96,80},{112,96},{1... | collective-permute-start | bytes 442376 | tf_op jit(solution)/shard_map/ppermute | solution.py:167
  362.5 5.5 %collective-permute-start.8 = (bf16[32,2304]{1,0:T(8,128)(2,1)S(1)}, bf16[32,2304]{1,0:T(8,128)(2,1)S(1)}, u32[]{:S(2)}, u32[]{:S(2)}) collective-permute-start(bf16[32,2304]{1,0:T(8,128)(2,1)S(1)} %get-tuple-element.12), channel_id=1, source_target_pairs={{0,96},{16,112},{32,0},{48,16},{64,32},{80,48},{96,64},{112,80},{1... | collective-permute-start | bytes 442376 | tf_op jit(solution)/shard_map/ppermute | solution.py:167
  367.9 6.1 %collective-permute-start.9 = (bf16[32,2304]{1,0:T(8,128)(2,1)S(1)}, bf16[32,2304]{1,0:T(8,128)(2,1)S(1)}, u32[]{:S(2)}, u32[]{:S(2)}) collective-permute-start(bf16[32,2304]{1,0:T(8,128)(2,1)S(1)} %get-tuple-element.11), channel_id=1, source_target_pairs={{0,80},{16,96},{32,112},{48,0},{64,16},{80,32},{96,48},{112,64},{1... | collective-permute-start | bytes 442376 | tf_op jit(solution)/shard_map/ppermute | solution.py:167
Sparse Core Ops, SparseCore 0:
  67.2 123.9 all-gather.1
  227.8 120.3 reduce-scatter.1

commit v8 on v6

--- a/solution.py
+++ b/solution.py
@@ -132,8 +132,9 @@
 
 def ffn_kernel(rows_ref, gate_ref, up_ref, down_ref, out_ref):
     rows = rows_ref[...]
-    gate_value = jnp.dot(rows, gate_ref[...], preferred_element_type=jnp.float32)
-    up_value = jnp.dot(rows, up_ref[...], preferred_element_type=jnp.float32)
+    contract = (((1,), (1,)), ((), ()))
+    gate_value = lax.dot_general(rows, gate_ref[...], contract, preferred_element_type=jnp.float32)
+    up_value = lax.dot_general(rows, up_ref[...], contract, preferred_element_type=jnp.float32)
     hidden = (gate_value / (1.0 + jnp.exp(-gate_value)) * up_value).astype(jnp.bfloat16)
     out_ref[...] = jnp.dot(hidden, down_ref[...], preferred_element_type=jnp.float32).astype(
         out_ref.dtype
@@ -142,7 +143,7 @@
 
 def expert_ffn(rows, gate, up, down):
     count, width = rows.shape
-    units = gate.shape[1]
+    units = gate.shape[0]
     tile = 512
     fixed = lambda shape: pl.BlockSpec(shape, lambda i: (0, 0))
     return pl.pallas_call(
@@ -150,8 +151,8 @@
         grid=(count // tile,),
         in_specs=[
             pl.BlockSpec((tile, width), lambda i: (i, 0)),
-            fixed((width, units)),
-            fixed((width, units)),
+            fixed((units, width)),
+            fixed((units, width)),
             fixed((units, width)),
         ],
         out_specs=pl.BlockSpec((tile, width), lambda i: (i, 0)),
@@ -212,7 +213,7 @@
         groups * MOST, width
     )
     arrived_rows = lax.all_gather(arrived, "sh", axis=0, tiled=True)
-    partial = expert_ffn(arrived_rows, gate_weight[0], up_weight[0], down_weight[0])
+    partial = expert_ffn(arrived_rows, gate_weight[0].T, up_weight[0].T, down_weight[0])
     summed = lax.psum_scatter(partial, "sh", scatter_dimension=0, tiled=True)
     returned = lax.all_to_all(
         summed.reshape(EXPERTS, MOST, width), "ex", split_axis=0, concat_axis=0, tiled=True

time: 377 us -> 378 us (level)
  waiting for transfers between devices: 252 us -> 258 us
    all_gather x1, waiting for transfers between devices: 115 us -> 121 us  [per_device(): arrived_rows = lax.all_gather(arrived, 'sh', axis=0, tiled=True)]
    unnamed x15 -> x11, local copies, waits for them, and re-layouts: 6.8 us -> 0.8 us
  transfers between devices with their start and end apart: 3 -> 3, of which waited for: 3 -> 3; matrix products, arithmetic and copies ran while one was open for 2% -> 0% of each run, Pallas kernels for 0% -> 0%
where the time goes in v8:
time: 378 us; the launch traced here: 377 us
  waiting for transfers between devices  258 us (68%)
  Pallas kernels  55.5 us (15%)
  blocking collectives  23.2 us (6%)
  between operations  13.6 us (4%)
  local copies, waits for them, and re-layouts  10.6 us (3%)
  other arithmetic  10.6 us (3%)
  starting transfers between devices  5.69 us (2%)
    all_gather x1, waiting for transfers between devices, per_device(): arrived_rows = lax.all_gather(arrived, 'sh', axis=0, tiled=True)  121 us
    reduce_scatter x1, waiting for transfers between devices, per_device(): summed = lax.psum_scatter(partial, 'sh', scatter_dimension=0, tiled=True)  121 us
    pallas_call x1, Pallas kernels, expert_ffn(): pl.pallas_call(ffn_kernel, grid=(count // tile,), in_specs=[pl.BlockSpec(...  36.2 us
    all_to_all x1, blocking collectives, per_device(): lax.all_to_all(outgoing, 'ex', split_axis=0, concat_axis=0, tiled=True)  23.2 us
    pallas_call x1, Pallas kernels, attend(): pl.pallas_call(attention_kernel, grid=(width // block,), in_specs=[column...  19.3 us
    all_to_all x1, waiting for transfers between devices, per_device(): lax.all_to_all(summed.reshape(EXPERTS, MOST, width), 'ex', split_axis=0,...  15.9 us
  transfers between devices with their start and end apart: 3, of which 3 were waited for; matrix products, arithmetic and copies ran while one was open for 0% of the time, Pallas kernels for 0%

profile of v8, /device:TPU:1, one launch (start us, length us, event | category | flops | bytes accessed | tf_op | source)
XLA Modules:
  0.0 377.4 jit_solution(7004220694243943027)
XLA Ops:
  6.5 0.0 copy-start
  6.5 0.0 all-gather.2.cloned.1.call-start
  6.5 0.7 broadcast_multiply_fusion
  7.2 0.8 copy.28
  8.0 0.8 reduce-window.18
  8.8 0.1 convert_reduce_fusion
  8.9 0.0 copy-start.4
  8.9 0.8 select_reduce_fusion
  9.7 0.7 convert_element_type.26
  10.4 0.1 copy.27
  10.5 0.1 mul.85
  10.6 0.7 copy.25.owner_ref
  11.4 0.1 eq.76
  11.5 0.6 reduce-window.19
  12.1 0.2 slice_reduce_fusion
  12.4 0.1 add_bitcast_fusion
  12.5 1.2 scatter_custom_fusion.1
  13.7 1.2 scatter_custom_fusion
  15.0 0.1 broadcast_in_dim.92
  15.1 0.7 select_reduce_fusion.1
  15.8 0.6 compare_select_fusion.token_owner_ref
  16.4 0.0 copy-done.4
  16.4 19.3 %shard_map.154 = f32[96,2304]{1,0:T(8,128)} custom-call(bf16[96,2304]{1,0:T(8,128)(2,1)} %query_ref.1, bf16[1024,2304]{1,0:T(8,128)(2,1)} %pool_key_ref.1, bf16[96,2304]{1,0:T(8,128)(2,1)} %new_key_ref.1, bf16[1024,2304]{1,0:T(8,128)(2,1)} %pool_value_ref.1, bf16[96,2304]{1,0:T(8,128)(2,1)} %new_value_ref.1, bf16[96,2304]{1,0:T(8,128)(2,1)} %hidden_ref.1, ...), custom_call_target="tpu_custom_call" | custom-call | tf_op jit(solution)/shard_map/pallas_call | solution.py:103
  35.8 0.0 copy-start.1
  35.8 1.4 multiply_reduce_fusion.2
  37.2 0.0 copy-done.1
  37.2 0.1 multiply_convert_fusion.1
  37.4 1.4 gather_fusion
  38.8 0.1 broadcast_select_fusion
  39.0 23.2 %all_to_all.10 = bf16[8,32,2304]{2,1,0:T(8,128)(2,1)} all-to-all(bf16[8,32,2304]{2,1,0:T(8,128)(2,1)S(1)} %broadcast_select_fusion), channel_id=1, replica_groups=mesh['ex'=8,'sh'=16] {'ex'}, dimensions={0} | all-to-all | bytes 2359296 | tf_op jit(solution)/shard_map/all_to_all | solution.py:212
  62.2 0.0 all-gather.2.cloned.1.call-update
  62.2 0.0 reduce-scatter.2.cloned.1.call-start
  62.3 121.4 %all-gather.2.cloned.1.call-done.rows_ref = bf16[4096,2304]{1,0:T(8,128)(2,1)} async-done(((bf16[256,2304]{1,0:T(8,128)(2,1)}), bf16[4096,2304]{1,0:T(8,128)(2,1)}) %all-gather.2.cloned.1.call-update) | async-done | bytes 18874384 | tf_op jit(solution)/shard_map/all_gather | solution.py:215
  183.7 36.2 %shard_map.155 = bf16[4096,2304]{1,0:T(8,128)(2,1)} custom-call(bf16[4096,2304]{1,0:T(8,128)(2,1)} %all-gather.2.cloned.1.call-done.rows_ref, bf16[360,2304]{1,0:T(8,128)(2,1)} %bitcast.34, bf16[360,2304]{1,0:T(8,128)(2,1)} %bitcast.35, bf16[360,2304]{1,0:T(8,128)(2,1)} %bitcast.36), custom_call_target="tpu_custom_call" | custom-call | tf_op jit(solution)/shard_map/pallas_call | solution.py:149
  219.8 0.0 reduce-scatter.2.cloned.1.call-update
  219.9 120.6 %reduce-scatter.2.cloned.1.call-done = bf16[256,2304]{1,0:T(8,128)(2,1)} async-done(((bf16[4096,2304]{1,0:T(8,128)(2,1)}), bf16[256,2304]{1,0:T(8,128)(2,1)}) %reduce-scatter.2.cloned.1.call-update) | async-done | bytes 1179664 | tf_op jit(solution)/shard_map/reduce_scatter | solution.py:217
  340.4 0.0 copy-start.3
  340.4 0.0 copy-start.2
  340.4 5.6 %all-to-all-start.1 = ((bf16[8,32,2304]{2,1,0:T(8,128)(2,1)}), bf16[8,32,2304]{2,1,0:T(8,128)(2,1)S(1)}, u32[]{:S(2)}, u32[]{:S(2)}) async-start(bf16[8,32,2304]{2,1,0:T(8,128)(2,1)} %bitcast.37), calls=%async_computation.2 | async-start | bytes 2359296 | tf_op jit(solution)/shard_map/all_to_all | solution.py:218
  346.1 0.0 copy-done.3
  346.1 0.0 copy-done
  346.1 0.2 fusion.13
  346.3 0.0 copy-done.2
  346.3 0.1 select_reduce_fusion.2
  346.4 0.1 copy.26
  346.5 15.9 %all-to-all-done.1 = bf16[8,32,2304]{2,1,0:T(8,128)(2,1)S(1)} async-done(((bf16[8,32,2304]{2,1,0:T(8,128)(2,1)}), bf16[8,32,2304]{2,1,0:T(8,128)(2,1)S(1)}, u32[]{:S(2)}, u32[]{:S(2)}) %all-to-all-start.1) | async-done | bytes 1179680 | tf_op jit(solution)/shard_map/all_to_all | solution.py:218
  362.5 2.1 gather_fusion.1
  364.6 2.3 reshape.264
  366.9 2.5 multiply_reduce_fusion
  369.4 0.2 multiply_reduce_fusion.1
  369.6 0.9 multiply_convert_fusion
  (18 shorter events, 0.2 us)
Async XLA Ops:
  6.5 339.6 %copy-start = (bf16[2304,8]{0,1:T(8,128)(2,1)S(1)}, bf16[2304,8]{0,1:T(8,128)(2,1)}, u32[]{:S(2)}) copy-start(bf16[2304,8]{0,1:T(8,128)(2,1)} %param.27) | copy-start | bytes 110596
  6.5 177.2 %all-gather.2.cloned.1.call-start = ((), (), s32[]{:S(2)}) async-start(), calls=%async_computation.3 | async-start | bytes 20054016 | tf_op jit(solution)/shard_map/all_gather | solution.py:215
  8.9 7.5 %copy-start.4 = (s32[96]{0:T(128)}, s32[96]{0:T(128)S(1)}, u32[]{:S(2)}) copy-start(s32[96]{0:T(128)S(1)} %convert_reduce_fusion) | copy-start | bytes 1156
  35.8 1.4 copy-start.1
  62.2 278.2 %reduce-scatter.2.cloned.1.call-start = ((), (), s32[]{:S(2)}) async-start(), calls=%async_computation.4 | async-start | bytes 20054016 | tf_op jit(solution)/shard_map/reduce_scatter | solution.py:217
  340.4 5.7 %copy-start.3 = (bf16[2304]{0:T(1024)(128)(2,1)S(1)}, bf16[2304]{0:T(1024)(128)(2,1)}, u32[]{:S(2)}) copy-start(bf16[2304]{0:T(1024)(128)(2,1)} %param.31) | copy-start | bytes 13828
  340.4 5.9 %copy-start.2 = (s32[96,2]{0,1:T(2,128)S(1)}, s32[96,2]{0,1:T(2,128)}, u32[]{:S(2)}) copy-start(s32[96,2]{0,1:T(2,128)} %param.25) | copy-start | bytes 2308
  340.4 22.0 %all-to-all-start.1 = ((bf16[8,32,2304]{2,1,0:T(8,128)(2,1)}), bf16[8,32,2304]{2,1,0:T(8,128)(2,1)S(1)}, u32[]{:S(2)}, u32[]{:S(2)}) async-start(bf16[8,32,2304]{2,1,0:T(8,128)(2,1)} %bitcast.37), calls=%async_computation.2 | async-start | bytes 2359296 | tf_op jit(solution)/shard_map/all_to_all | solution.py:218
Sparse Core Ops, SparseCore 0:
  62.3 121.3 all-gather.1
  220.0 120.4 reduce-scatter.1

commit v9 on v8

--- a/solution.py
+++ b/solution.py
@@ -97,7 +97,7 @@
         axis=0,
     )
     token_owner = jnp.where(position < limit, token_request, -1).astype(jnp.int32)
-    block = 2 * HEAD_DIM
+    block = 4 * HEAD_DIM
     column = lambda count: pl.BlockSpec((count, block), lambda j: (0, j))
     whole = lambda shape: pl.BlockSpec(shape, lambda j: (0, 0))
     return pl.pallas_call(
@@ -144,7 +144,7 @@
 def expert_ffn(rows, gate, up, down):
     count, width = rows.shape
     units = gate.shape[0]
-    tile = 512
+    tile = 1024
     fixed = lambda shape: pl.BlockSpec(shape, lambda i: (0, 0))
     return pl.pallas_call(
         ffn_kernel,

time: 378 us -> 380 us (level)
  no operation moved by 1% of the time
where the time goes in v9:
time: 380 us; the launch traced here: 379 us
  waiting for transfers between devices  258 us (68%)
  Pallas kernels  57.4 us (15%)
  blocking collectives  23.2 us (6%)
  between operations  13.6 us (4%)
  local copies, waits for them, and re-layouts  10.6 us (3%)
  other arithmetic  10.6 us (3%)
  starting transfers between devices  5.74 us (2%)
    all_gather x1, waiting for transfers between devices, per_device(): arrived_rows = lax.all_gather(arrived, 'sh', axis=0, tiled=True)  121 us
    reduce_scatter x1, waiting for transfers between devices, per_device(): summed = lax.psum_scatter(partial, 'sh', scatter_dimension=0, tiled=True)  121 us
    pallas_call x1, Pallas kernels, expert_ffn(): pl.pallas_call(ffn_kernel, grid=(count // tile,), in_specs=[pl.BlockSpec(...  36.5 us
    all_to_all x1, blocking collectives, per_device(): lax.all_to_all(outgoing, 'ex', split_axis=0, concat_axis=0, tiled=True)  23.2 us
    pallas_call x1, Pallas kernels, attend(): pl.pallas_call(attention_kernel, grid=(width // block,), in_specs=[column...  20.9 us
    all_to_all x1, waiting for transfers between devices, per_device(): lax.all_to_all(summed.reshape(EXPERTS, MOST, width), 'ex', split_axis=0,...  15.9 us
  transfers between devices with their start and end apart: 3, of which 3 were waited for; matrix products, arithmetic and copies ran while one was open for 0% of the time, Pallas kernels for 0%

profile of v9, /device:TPU:1, one launch (start us, length us, event | category | flops | bytes accessed | tf_op | source)
XLA Modules:
  0.0 379.3 jit_solution(15197895404241202616)
XLA Ops:
  6.5 0.0 copy-start
  6.5 0.0 all-gather.2.cloned.1.call-start
  6.5 0.7 broadcast_multiply_fusion
  7.2 0.8 copy.28
  8.0 0.8 reduce-window.18
  8.8 0.1 convert_reduce_fusion
  8.9 0.0 copy-start.4
  8.9 0.8 select_reduce_fusion
  9.7 0.7 convert_element_type.26
  10.4 0.1 copy.27
  10.5 0.1 mul.85
  10.6 0.7 copy.25.owner_ref
  11.4 0.1 eq.76
  11.5 0.6 reduce-window.19
  12.1 0.2 slice_reduce_fusion
  12.4 0.1 add_bitcast_fusion
  12.5 1.2 scatter_custom_fusion.1
  13.7 1.2 scatter_custom_fusion
  15.0 0.1 broadcast_in_dim.92
  15.1 0.7 select_reduce_fusion.1
  15.8 0.6 compare_select_fusion.token_owner_ref
  16.4 0.0 copy-done.4
  16.4 20.9 %shard_map.154 = f32[96,2304]{1,0:T(8,128)} custom-call(bf16[96,2304]{1,0:T(8,128)(2,1)} %query_ref.1, bf16[1024,2304]{1,0:T(8,128)(2,1)} %pool_key_ref.1, bf16[96,2304]{1,0:T(8,128)(2,1)} %new_key_ref.1, bf16[1024,2304]{1,0:T(8,128)(2,1)} %pool_value_ref.1, bf16[96,2304]{1,0:T(8,128)(2,1)} %new_value_ref.1, bf16[96,2304]{1,0:T(8,128)(2,1)} %hidden_ref.1, ...), custom_call_target="tpu_custom_call" | custom-call | tf_op jit(solution)/shard_map/pallas_call | solution.py:103
  37.3 0.0 copy-start.1
  37.3 1.4 multiply_reduce_fusion.2
  38.7 0.0 copy-done.1
  38.8 0.1 multiply_convert_fusion.1
  38.9 1.4 gather_fusion
  40.3 0.1 broadcast_select_fusion
  40.5 23.2 %all_to_all.10 = bf16[8,32,2304]{2,1,0:T(8,128)(2,1)} all-to-all(bf16[8,32,2304]{2,1,0:T(8,128)(2,1)S(1)} %broadcast_select_fusion), channel_id=1, replica_groups=mesh['ex'=8,'sh'=16] {'ex'}, dimensions={0} | all-to-all | bytes 2359296 | tf_op jit(solution)/shard_map/all_to_all | solution.py:212
  63.7 0.0 all-gather.2.cloned.1.call-update
  63.7 0.0 reduce-scatter.2.cloned.1.call-start
  63.8 121.4 %all-gather.2.cloned.1.call-done.rows_ref = bf16[4096,2304]{1,0:T(8,128)(2,1)} async-done(((bf16[256,2304]{1,0:T(8,128)(2,1)}), bf16[4096,2304]{1,0:T(8,128)(2,1)}) %all-gather.2.cloned.1.call-update) | async-done | bytes 18874384 | tf_op jit(solution)/shard_map/all_gather | solution.py:215
  185.2 36.5 %shard_map.155 = bf16[4096,2304]{1,0:T(8,128)(2,1)} custom-call(bf16[4096,2304]{1,0:T(8,128)(2,1)} %all-gather.2.cloned.1.call-done.rows_ref, bf16[360,2304]{1,0:T(8,128)(2,1)} %bitcast.34, bf16[360,2304]{1,0:T(8,128)(2,1)} %bitcast.35, bf16[360,2304]{1,0:T(8,128)(2,1)} %bitcast.36), custom_call_target="tpu_custom_call" | custom-call | tf_op jit(solution)/shard_map/pallas_call | solution.py:149
  221.7 0.0 reduce-scatter.2.cloned.1.call-update
  221.8 120.5 %reduce-scatter.2.cloned.1.call-done = bf16[256,2304]{1,0:T(8,128)(2,1)} async-done(((bf16[4096,2304]{1,0:T(8,128)(2,1)}), bf16[256,2304]{1,0:T(8,128)(2,1)}) %reduce-scatter.2.cloned.1.call-update) | async-done | bytes 1179664 | tf_op jit(solution)/shard_map/reduce_scatter | solution.py:217
  342.3 0.0 copy-start.3
  342.3 0.0 copy-start.2
  342.3 5.7 %all-to-all-start.1 = ((bf16[8,32,2304]{2,1,0:T(8,128)(2,1)}), bf16[8,32,2304]{2,1,0:T(8,128)(2,1)S(1)}, u32[]{:S(2)}, u32[]{:S(2)}) async-start(bf16[8,32,2304]{2,1,0:T(8,128)(2,1)} %bitcast.37), calls=%async_computation.2 | async-start | bytes 2359296 | tf_op jit(solution)/shard_map/all_to_all | solution.py:218
  348.0 0.0 copy-done.3
  348.0 0.0 copy-done
  348.0 0.2 fusion.13
  348.2 0.0 copy-done.2
  348.2 0.1 select_reduce_fusion.2
  348.3 0.1 copy.26
  348.4 15.9 %all-to-all-done.1 = bf16[8,32,2304]{2,1,0:T(8,128)(2,1)S(1)} async-done(((bf16[8,32,2304]{2,1,0:T(8,128)(2,1)}), bf16[8,32,2304]{2,1,0:T(8,128)(2,1)S(1)}, u32[]{:S(2)}, u32[]{:S(2)}) %all-to-all-start.1) | async-done | bytes 1179680 | tf_op jit(solution)/shard_map/all_to_all | solution.py:218
  364.3 2.1 gather_fusion.1
  366.5 2.3 reshape.264
  368.8 2.5 multiply_reduce_fusion
  371.3 0.2 multiply_reduce_fusion.1
  371.5 0.9 multiply_convert_fusion
  (18 shorter events, 0.2 us)
Async XLA Ops:
  6.5 341.4 %copy-start = (bf16[2304,8]{0,1:T(8,128)(2,1)S(1)}, bf16[2304,8]{0,1:T(8,128)(2,1)}, u32[]{:S(2)}) copy-start(bf16[2304,8]{0,1:T(8,128)(2,1)} %param.27) | copy-start | bytes 110596
  6.5 178.7 %all-gather.2.cloned.1.call-start = ((), (), s32[]{:S(2)}) async-start(), calls=%async_computation.3 | async-start | bytes 20054016 | tf_op jit(solution)/shard_map/all_gather | solution.py:215
  8.9 7.5 %copy-start.4 = (s32[96]{0:T(128)}, s32[96]{0:T(128)S(1)}, u32[]{:S(2)}) copy-start(s32[96]{0:T(128)S(1)} %convert_reduce_fusion) | copy-start | bytes 1156
  37.3 1.4 copy-start.1
  63.7 278.5 %reduce-scatter.2.cloned.1.call-start = ((), (), s32[]{:S(2)}) async-start(), calls=%async_computation.4 | async-start | bytes 20054016 | tf_op jit(solution)/shard_map/reduce_scatter | solution.py:217
  342.3 5.7 %copy-start.3 = (bf16[2304]{0:T(1024)(128)(2,1)S(1)}, bf16[2304]{0:T(1024)(128)(2,1)}, u32[]{:S(2)}) copy-start(bf16[2304]{0:T(1024)(128)(2,1)} %param.31) | copy-start | bytes 13828
  342.3 5.9 %copy-start.2 = (s32[96,2]{0,1:T(2,128)S(1)}, s32[96,2]{0,1:T(2,128)}, u32[]{:S(2)}) copy-start(s32[96,2]{0,1:T(2,128)} %param.25) | copy-start | bytes 2308
  342.3 22.1 %all-to-all-start.1 = ((bf16[8,32,2304]{2,1,0:T(8,128)(2,1)}), bf16[8,32,2304]{2,1,0:T(8,128)(2,1)S(1)}, u32[]{:S(2)}, u32[]{:S(2)}) async-start(bf16[8,32,2304]{2,1,0:T(8,128)(2,1)} %bitcast.37), calls=%async_computation.2 | async-start | bytes 2359296 | tf_op jit(solution)/shard_map/all_to_all | solution.py:218
Sparse Core Ops, SparseCore 0:
  63.9 121.3 all-gather.1
  221.9 120.3 reduce-scatter.1

commit v10 on v8

--- a/solution.py
+++ b/solution.py
@@ -203,12 +203,12 @@
     before = jnp.cumsum(onehot, axis=0) - onehot
     slot_index = jnp.sum(before * onehot, axis=1)
     target = entries * MOST + slot_index
-    entry_rows = jnp.arange(entries.shape[0], dtype=jnp.int32) // top_count
-    source_row = jnp.zeros((EXPERTS * MOST,), jnp.int32).at[target].set(entry_rows)
-    filled = jnp.zeros((EXPERTS * MOST,), jnp.bool_).at[target].set(True)
-    outgoing = jnp.where(filled[:, None], normed[source_row], jnp.zeros((), jnp.bfloat16)).reshape(
-        EXPERTS, MOST, width
-    )
+    slots = jnp.arange(EXPERTS * MOST, dtype=jnp.int32)
+    pick = target.reshape(row_count, top_count)[:, :, None] == slots[None, None, :]
+    chosen = jnp.any(pick, axis=1).astype(jnp.bfloat16)
+    outgoing = lax.dot_general(
+        chosen, normed, (((0,), (0,)), ((), ())), preferred_element_type=jnp.float32
+    ).astype(jnp.bfloat16).reshape(EXPERTS, MOST, width)
     arrived = lax.all_to_all(outgoing, "ex", split_axis=0, concat_axis=0, tiled=True).reshape(
         groups * MOST, width
     )
@@ -219,8 +219,12 @@
         summed.reshape(EXPERTS, MOST, width), "ex", split_axis=0, concat_axis=0, tiled=True
     )
     flat_results = returned.reshape(EXPERTS * MOST, width)
-    picked = flat_results[target].reshape(row_count, top_count, width)
-    mixed = resid + jnp.sum(route_weights[:, :, None] * picked.astype(jnp.float32), axis=1)
+    terms = [
+        route_weights[:, k : k + 1]
+        * jnp.dot(pick[:, k, :].astype(jnp.bfloat16), flat_results, preferred_element_type=jnp.float32)
+        for k in range(top_count)
+    ]
+    mixed = resid + sum(terms[1:], terms[0])
     return rms_scale(mixed, out_gain).astype(jnp.bfloat16)
 
 

time: 378 us -> 366 us (0.968)
  local copies, waits for them, and re-layouts: 10.6 us -> 1.41 us
  other arithmetic: 10.6 us -> 6.36 us
where the time goes in v10:
time: 366 us; the launch traced here: 365 us
  waiting for transfers between devices  258 us (70%)
  Pallas kernels  55.5 us (15%)
  blocking collectives  23.2 us (6%)
  between operations  13.6 us (4%)
  other arithmetic  6.36 us (2%)
  starting transfers between devices  5.74 us (2%)
    all_gather x1, waiting for transfers between devices, per_device(): arrived_rows = lax.all_gather(arrived, 'sh', axis=0, tiled=True)  121 us
    reduce_scatter x1, waiting for transfers between devices, per_device(): summed = lax.psum_scatter(partial, 'sh', scatter_dimension=0, tiled=True)  121 us
    pallas_call x1, Pallas kernels, expert_ffn(): pl.pallas_call(ffn_kernel, grid=(count // tile,), in_specs=[pl.BlockSpec(...  36.1 us
    all_to_all x1, blocking collectives, per_device(): lax.all_to_all(outgoing, 'ex', split_axis=0, concat_axis=0, tiled=True)  23.2 us
    pallas_call x1, Pallas kernels, attend(): pl.pallas_call(attention_kernel, grid=(width // block,), in_specs=[column...  19.4 us
    all_to_all x1, waiting for transfers between devices, per_device(): lax.all_to_all(summed.reshape(EXPERTS, MOST, width), 'ex', split_axis=0,...  16 us
  transfers between devices with their start and end apart: 3, of which 3 were waited for; matrix products, arithmetic and copies ran while one was open for 0% of the time, Pallas kernels for 0%

profile of v10, /device:TPU:1, one launch (start us, length us, event | category | flops | bytes accessed | tf_op | source)
XLA Modules:
  0.0 365.3 jit_solution(5801828421944266039)
XLA Ops:
  6.5 0.0 copy-start
  6.5 0.0 all-gather.2.cloned.1.call-start
  6.5 0.8 select_reduce_fusion
  7.3 0.8 reduce-window.18
  8.2 0.1 convert_reduce_fusion
  8.2 0.0 copy-start.5
  8.2 0.7 copy.33.owner_ref
  9.0 0.7 select_reduce_fusion.1
  9.7 0.6 compare_select_fusion.token_owner_ref
  10.3 0.0 copy-done.5
  10.3 0.0 copy-start.3
  10.3 0.0 copy-start.2
  10.3 19.4 %shard_map.154 = f32[96,2304]{1,0:T(8,128)} custom-call(bf16[96,2304]{1,0:T(8,128)(2,1)} %query_ref.1, bf16[1024,2304]{1,0:T(8,128)(2,1)} %pool_key_ref.1, bf16[96,2304]{1,0:T(8,128)(2,1)} %new_key_ref.1, bf16[1024,2304]{1,0:T(8,128)(2,1)} %pool_value_ref.1, bf16[96,2304]{1,0:T(8,128)(2,1)} %new_value_ref.1, bf16[96,2304]{1,0:T(8,128)(2,1)} %hidden_ref.1, ...), custom_call_target="tpu_custom_call" | custom-call | tf_op jit(solution)/shard_map/pallas_call | solution.py:103
  29.7 0.0 copy-start.1
  29.7 1.4 multiply_reduce_fusion.1
  31.1 0.0 copy-done.3
  31.2 0.0 copy-done.2
  31.2 0.1 copy.34
  31.3 0.1 eq.89
  31.4 0.6 reduce-window.19
  32.0 0.2 slice_reduce_fusion
  32.3 0.1 add_bitcast_fusion
  32.4 0.1 reduce_sum.87
  32.5 0.1 copy.35
  32.6 0.1 iota_compare_fusion
  32.7 0.0 copy-done.1
  32.7 0.5 convolution_convert_fusion
  33.3 23.2 %all_to_all.10 = bf16[8,32,2304]{2,1,0:T(8,128)(2,1)} all-to-all(bf16[8,32,2304]{2,1,0:T(8,128)(2,1)S(1)} %bitcast.44), channel_id=1, replica_groups=mesh['ex'=8,'sh'=16] {'ex'}, dimensions={0} | all-to-all | bytes 2359296 | tf_op jit(solution)/shard_map/all_to_all | solution.py:212
  56.5 0.0 all-gather.2.cloned.1.call-update
  56.5 0.0 reduce-scatter.2.cloned.1.call-start
  56.6 121.4 %all-gather.2.cloned.1.call-done.rows_ref = bf16[4096,2304]{1,0:T(8,128)(2,1)} async-done(((bf16[256,2304]{1,0:T(8,128)(2,1)}), bf16[4096,2304]{1,0:T(8,128)(2,1)}) %all-gather.2.cloned.1.call-update) | async-done | bytes 18874384 | tf_op jit(solution)/shard_map/all_gather | solution.py:215
  178.0 36.1 %shard_map.155 = bf16[4096,2304]{1,0:T(8,128)(2,1)} custom-call(bf16[4096,2304]{1,0:T(8,128)(2,1)} %all-gather.2.cloned.1.call-done.rows_ref, bf16[360,2304]{1,0:T(8,128)(2,1)} %bitcast.45, bf16[360,2304]{1,0:T(8,128)(2,1)} %bitcast.46, bf16[360,2304]{1,0:T(8,128)(2,1)} %bitcast.47), custom_call_target="tpu_custom_call" | custom-call | tf_op jit(solution)/shard_map/pallas_call | solution.py:149
  214.2 0.0 reduce-scatter.2.cloned.1.call-update
  214.2 120.5 %reduce-scatter.2.cloned.1.call-done = bf16[256,2304]{1,0:T(8,128)(2,1)} async-done(((bf16[4096,2304]{1,0:T(8,128)(2,1)}), bf16[256,2304]{1,0:T(8,128)(2,1)}) %reduce-scatter.2.cloned.1.call-update) | async-done | bytes 1179664 | tf_op jit(solution)/shard_map/reduce_scatter | solution.py:217
  334.7 0.0 copy-start.4
  334.7 5.7 %all-to-all-start.1 = ((bf16[8,32,2304]{2,1,0:T(8,128)(2,1)}), bf16[8,32,2304]{2,1,0:T(8,128)(2,1)S(1)}, u32[]{:S(2)}, u32[]{:S(2)}) async-start(bf16[8,32,2304]{2,1,0:T(8,128)(2,1)} %bitcast.48), calls=%async_computation.2 | async-start | bytes 2359296 | tf_op jit(solution)/shard_map/all_to_all | solution.py:218
  340.4 0.0 copy-done.4
  340.4 0.0 copy-done
  340.4 0.3 fusion.12
  340.7 0.1 select_reduce_fusion.2
  340.8 16.0 %all-to-all-done.1 = bf16[8,32,2304]{2,1,0:T(8,128)(2,1)S(1)} async-done(((bf16[8,32,2304]{2,1,0:T(8,128)(2,1)}), bf16[8,32,2304]{2,1,0:T(8,128)(2,1)S(1)}, u32[]{:S(2)}, u32[]{:S(2)}) %all-to-all-start.1) | async-done | bytes 1179680 | tf_op jit(solution)/shard_map/all_to_all | solution.py:218
  356.8 0.3 convolution_multiply_fusion.1
  357.1 0.4 multiply_reduce_fusion
  357.6 0.9 multiply_convert_fusion
  (15 shorter events, 0.2 us)
Async XLA Ops:
  6.5 333.9 %copy-start = (bf16[2304,8]{0,1:T(8,128)(2,1)S(1)}, bf16[2304,8]{0,1:T(8,128)(2,1)}, u32[]{:S(2)}) copy-start(bf16[2304,8]{0,1:T(8,128)(2,1)} %param.27) | copy-start | bytes 110596
  6.5 171.5 %all-gather.2.cloned.1.call-start = ((), (), s32[]{:S(2)}) async-start(), calls=%async_computation.3 | async-start | bytes 20054016 | tf_op jit(solution)/shard_map/all_gather | solution.py:215
  8.2 2.1 copy-start.5
  10.3 20.8 %copy-start.3 = (bf16[2304]{0:T(1024)(128)(2,1)S(1)}, bf16[2304]{0:T(1024)(128)(2,1)}, u32[]{:S(2)}) copy-start(bf16[2304]{0:T(1024)(128)(2,1)} %param.26) | copy-start | bytes 13828
  10.3 20.8 %copy-start.2 = (s32[96,2]{0,1:T(2,128)S(1)}, s32[96,2]{0,1:T(2,128)}, u32[]{:S(2)}) copy-start(s32[96,2]{0,1:T(2,128)} %param.25) | copy-start | bytes 2308
  29.7 3.0 copy-start.1
  56.5 278.2 %reduce-scatter.2.cloned.1.call-start = ((), (), s32[]{:S(2)}) async-start(), calls=%async_computation.4 | async-start | bytes 20054016 | tf_op jit(solution)/shard_map/reduce_scatter | solution.py:217
  334.7 5.7 %copy-start.4 = (bf16[2304]{0:T(1024)(128)(2,1)S(1)}, bf16[2304]{0:T(1024)(128)(2,1)}, u32[]{:S(2)}) copy-start(bf16[2304]{0:T(1024)(128)(2,1)} %param.31) | copy-start | bytes 13828
  334.7 22.1 %all-to-all-start.1 = ((bf16[8,32,2304]{2,1,0:T(8,128)(2,1)}), bf16[8,32,2304]{2,1,0:T(8,128)(2,1)S(1)}, u32[]{:S(2)}, u32[]{:S(2)}) async-start(bf16[8,32,2304]{2,1,0:T(8,128)(2,1)} %bitcast.48), calls=%async_computation.2 | async-start | bytes 2359296 | tf_op jit(solution)/shard_map/all_to_all | solution.py:218
Sparse Core Ops, SparseCore 0:
  56.7 121.3 all-gather.1
  214.3 120.3 reduce-scatter.1

commit v11 on v10

--- a/solution.py
+++ b/solution.py
@@ -130,11 +130,14 @@
     )
 
 
-def ffn_kernel(rows_ref, gate_ref, up_ref, down_ref, out_ref):
-    rows = rows_ref[...]
+def ffn_kernel(rows_ref, both_ref, down_ref, out_ref):
     contract = (((1,), (1,)), ((), ()))
-    gate_value = lax.dot_general(rows, gate_ref[...], contract, preferred_element_type=jnp.float32)
-    up_value = lax.dot_general(rows, up_ref[...], contract, preferred_element_type=jnp.float32)
+    both = lax.dot_general(
+        rows_ref[...], both_ref[...], contract, preferred_element_type=jnp.float32
+    )
+    half = both.shape[1] // 2
+    gate_value = both[:, :half]
+    up_value = both[:, half:]
     hidden = (gate_value / (1.0 + jnp.exp(-gate_value)) * up_value).astype(jnp.bfloat16)
     out_ref[...] = jnp.dot(hidden, down_ref[...], preferred_element_type=jnp.float32).astype(
         out_ref.dtype
@@ -144,6 +147,10 @@
 def expert_ffn(rows, gate, up, down):
     count, width = rows.shape
     units = gate.shape[0]
+    padded = -(-units // 128) * 128
+    spare = ((0, padded - units), (0, 0))
+    both = jnp.concatenate([jnp.pad(gate, spare), jnp.pad(up, spare)], axis=0)
+    down = jnp.pad(down, spare)
     tile = 512
     fixed = lambda shape: pl.BlockSpec(shape, lambda i: (0, 0))
     return pl.pallas_call(
@@ -151,14 +158,13 @@
         grid=(count // tile,),
         in_specs=[
             pl.BlockSpec((tile, width), lambda i: (i, 0)),
-            fixed((units, width)),
-            fixed((units, width)),
-            fixed((units, width)),
+            fixed((2 * padded, width)),
+            fixed((padded, width)),
         ],
         out_specs=pl.BlockSpec((tile, width), lambda i: (i, 0)),
         out_shape=jax.ShapeDtypeStruct((count, width), jnp.bfloat16),
         interpret=INTERPRET,
-    )(rows, gate, up, down)
+    )(rows, both, down)
 
 
 def per_device(

time: 366 us -> 371 us (1.014)
  Pallas kernels: 55.5 us -> 60.9 us
  waiting for transfers between devices: 258 us -> 253 us
    pallas_call x1, Pallas kernels: 36.1 us -> 41.5 us  [expert_ffn(): pl.pallas_call(ffn_kernel, grid=(count // tile,), in_specs=[pl.BlockSpec(...]
    all_gather x1, waiting for transfers between devices: 121 us -> 117 us  [per_device(): arrived_rows = lax.all_gather(arrived, 'sh', axis=0, tiled=True)]
  transfers between devices with their start and end apart: 3 -> 3, of which waited for: 3 -> 3; matrix products, arithmetic and copies ran while one was open for 0% -> 1% of each run, Pallas kernels for 0% -> 0%
where the time goes in v11:
time: 371 us
  waiting for transfers between devices  253 us (68%)
  Pallas kernels  60.9 us (16%)
  blocking collectives  23.4 us (6%)
  between operations  13.6 us (4%)
  other arithmetic  8.28 us (2%)
  starting transfers between devices  5.56 us (1%)
  local copies, waits for them, and re-layouts  3.97 us (1%)
    reduce_scatter x1, waiting for transfers between devices, per_device(): summed = lax.psum_scatter(partial, 'sh', scatter_dimension=0, tiled=True)  121 us
    all_gather x1, waiting for transfers between devices, per_device(): arrived_rows = lax.all_gather(arrived, 'sh', axis=0, tiled=True)  117 us
    pallas_call x1, Pallas kernels, expert_ffn(): pl.pallas_call(ffn_kernel, grid=(count // tile,), in_specs=[pl.BlockSpec(...  41.5 us
    all_to_all x1, blocking collectives, per_device(): lax.all_to_all(outgoing, 'ex', split_axis=0, concat_axis=0, tiled=True)  23.4 us
    pallas_call x1, Pallas kernels, attend(): pl.pallas_call(attention_kernel, grid=(width // block,), in_specs=[column...  19.4 us
    all_to_all x1, waiting for transfers between devices, per_device(): lax.all_to_all(summed.reshape(EXPERTS, MOST, width), 'ex', split_axis=0,...  16 us
  transfers between devices with their start and end apart: 3, of which 3 were waited for; matrix products, arithmetic and copies ran while one was open for 1% of the time, Pallas kernels for 0%

profile of v11, /device:TPU:1, one launch (start us, length us, event | category | flops | bytes accessed | tf_op | source)
XLA Modules:
  0.0 370.7 jit_solution(3022616510397589929)
XLA Ops:
  6.5 0.0 copy-start
  6.5 0.0 all-gather.2.cloned.1.call-start
  6.5 0.8 select_reduce_fusion
  7.3 0.8 reduce-window.18
  8.2 0.1 convert_reduce_fusion
  8.2 0.0 copy-start.8
  8.2 0.7 copy.33.owner_ref
  9.0 0.7 select_reduce_fusion.1
  9.7 0.6 compare_select_fusion.token_owner_ref
  10.3 0.0 copy-done.8
  10.3 0.0 copy-start.6
  10.3 0.0 copy-start.5
  10.3 19.4 %shard_map.154 = f32[96,2304]{1,0:T(8,128)} custom-call(bf16[96,2304]{1,0:T(8,128)(2,1)} %query_ref.1, bf16[1024,2304]{1,0:T(8,128)(2,1)} %pool_key_ref.1, bf16[96,2304]{1,0:T(8,128)(2,1)} %new_key_ref.1, bf16[1024,2304]{1,0:T(8,128)(2,1)} %pool_value_ref.1, bf16[96,2304]{1,0:T(8,128)(2,1)} %new_value_ref.1, bf16[96,2304]{1,0:T(8,128)(2,1)} %hidden_ref.1, ...), custom_call_target="tpu_custom_call" | custom-call | tf_op jit(solution)/shard_map/pallas_call | solution.py:103
  29.7 0.0 copy-start.1
  29.7 1.4 multiply_reduce_fusion.1
  31.1 0.0 copy-done.6
  31.2 0.0 copy-done.5
  31.2 0.1 copy.34
  31.3 0.1 eq.89
  31.4 0.6 reduce-window.19
  32.0 0.2 slice_reduce_fusion
  32.3 0.1 add_bitcast_fusion
  32.4 0.1 reduce_sum.87
  32.5 0.1 copy.35
  32.6 0.1 iota_compare_fusion.2
  32.7 0.0 copy-done.1
  32.8 0.5 convolution_convert_fusion
  33.3 0.0 copy-start.2
  33.3 23.4 %all_to_all.10 = bf16[8,32,2304]{2,1,0:T(8,128)(2,1)} all-to-all(bf16[8,32,2304]{2,1,0:T(8,128)(2,1)S(1)} %bitcast.44), channel_id=1, replica_groups=mesh['ex'=8,'sh'=16] {'ex'}, dimensions={0} | all-to-all | bytes 2359296 | tf_op jit(solution)/shard_map/all_to_all | solution.py:218
  56.7 0.0 all-gather.2.cloned.1.call-update
  56.7 0.0 reduce-scatter.2.cloned.1.call-start
  56.7 0.0 copy-start.3
  56.8 0.0 copy-start.4
  56.8 0.0 copy-done.2
  56.8 1.4 pad.17.down_ref
  58.1 0.7 copy-done.3
  58.8 0.5 copy-done.4
  59.3 1.9 fusion.4.both_ref
  61.2 116.9 %all-gather.2.cloned.1.call-done.rows_ref = bf16[4096,2304]{1,0:T(8,128)(2,1)} async-done(((bf16[256,2304]{1,0:T(8,128)(2,1)}), bf16[4096,2304]{1,0:T(8,128)(2,1)}) %all-gather.2.cloned.1.call-update) | async-done | bytes 18874384 | tf_op jit(solution)/shard_map/all_gather | solution.py:221
  178.2 41.5 %shard_map.155 = bf16[4096,2304]{1,0:T(8,128)(2,1)} custom-call(bf16[4096,2304]{1,0:T(8,128)(2,1)} %all-gather.2.cloned.1.call-done.rows_ref, bf16[768,2304]{1,0:T(8,128)(2,1)} %fusion.4.both_ref, bf16[384,2304]{1,0:T(8,128)(2,1)} %pad.17.down_ref), custom_call_target="tpu_custom_call" | custom-call | tf_op jit(solution)/shard_map/pallas_call | solution.py:156
  219.7 0.0 reduce-scatter.2.cloned.1.call-update
  219.7 0.0 copy-start.7
  219.7 120.6 %reduce-scatter.2.cloned.1.call-done = bf16[256,2304]{1,0:T(8,128)(2,1)} async-done(((bf16[4096,2304]{1,0:T(8,128)(2,1)}), bf16[256,2304]{1,0:T(8,128)(2,1)}) %reduce-scatter.2.cloned.1.call-update) | async-done | bytes 1179664 | tf_op jit(solution)/shard_map/reduce_scatter | solution.py:223
  340.3 5.5 %all-to-all-start.1 = ((bf16[8,32,2304]{2,1,0:T(8,128)(2,1)}), bf16[8,32,2304]{2,1,0:T(8,128)(2,1)S(1)}, u32[]{:S(2)}, u32[]{:S(2)}) async-start(bf16[8,32,2304]{2,1,0:T(8,128)(2,1)} %bitcast.48), calls=%async_computation.2 | async-start | bytes 2359296 | tf_op jit(solution)/shard_map/all_to_all | solution.py:224
  345.8 0.0 copy-done.7
  345.8 0.0 copy-done
  345.8 0.3 fusion.15
  346.1 0.1 select_reduce_fusion.2
  346.2 16.0 %all-to-all-done.1 = bf16[8,32,2304]{2,1,0:T(8,128)(2,1)S(1)} async-done(((bf16[8,32,2304]{2,1,0:T(8,128)(2,1)}), bf16[8,32,2304]{2,1,0:T(8,128)(2,1)S(1)}, u32[]{:S(2)}, u32[]{:S(2)}) %all-to-all-start.1) | async-done | bytes 1179680 | tf_op jit(solution)/shard_map/all_to_all | solution.py:224
  362.2 0.3 convolution_multiply_fusion.1
  362.5 0.4 multiply_reduce_fusion
  363.0 0.9 multiply_convert_fusion
  (15 shorter events, 0.2 us)
Async XLA Ops:
  6.5 339.3 %copy-start = (bf16[2304,8]{0,1:T(8,128)(2,1)S(1)}, bf16[2304,8]{0,1:T(8,128)(2,1)}, u32[]{:S(2)}) copy-start(bf16[2304,8]{0,1:T(8,128)(2,1)} %param.27) | copy-start | bytes 110596
  6.5 171.6 %all-gather.2.cloned.1.call-start = ((), (), s32[]{:S(2)}) async-start(), calls=%async_computation.3 | async-start | bytes 20054016 | tf_op jit(solution)/shard_map/all_gather | solution.py:221
  8.2 2.1 copy-start.8
  10.3 20.8 %copy-start.6 = (bf16[2304]{0:T(1024)(128)(2,1)S(1)}, bf16[2304]{0:T(1024)(128)(2,1)}, u32[]{:S(2)}) copy-start(bf16[2304]{0:T(1024)(128)(2,1)} %param.26) | copy-start | bytes 13828
  10.3 20.8 %copy-start.5 = (s32[96,2]{0,1:T(2,128)S(1)}, s32[96,2]{0,1:T(2,128)}, u32[]{:S(2)}) copy-start(s32[96,2]{0,1:T(2,128)} %param.25) | copy-start | bytes 2308
  29.7 3.0 copy-start.1
  33.3 23.5 %copy-start.2 = (bf16[1,360,2304]{2,1,0:T(8,128)(2,1)S(1)}, bf16[1,360,2304]{2,1,0:T(8,128)(2,1)}, u32[]{:S(2)}) copy-start(bf16[1,360,2304]{2,1,0:T(8,128)(2,1)} %param.30) | copy-start | bytes 4976644
  56.7 283.6 %reduce-scatter.2.cloned.1.call-start = ((), (), s32[]{:S(2)}) async-start(), calls=%async_computation.4 | async-start | bytes 20054016 | tf_op jit(solution)/shard_map/reduce_scatter | solution.py:223
  56.7 2.1 copy-start.3
  56.8 2.6 copy-start.4
  219.7 126.1 %copy-start.7 = (bf16[2304]{0:T(1024)(128)(2,1)S(1)}, bf16[2304]{0:T(1024)(128)(2,1)}, u32[]{:S(2)}) copy-start(bf16[2304]{0:T(1024)(128)(2,1)} %param.31) | copy-start | bytes 13828
  340.3 21.9 %all-to-all-start.1 = ((bf16[8,32,2304]{2,1,0:T(8,128)(2,1)}), bf16[8,32,2304]{2,1,0:T(8,128)(2,1)S(1)}, u32[]{:S(2)}, u32[]{:S(2)}) async-start(bf16[8,32,2304]{2,1,0:T(8,128)(2,1)} %bitcast.48), calls=%async_computation.2 | async-start | bytes 2359296 | tf_op jit(solution)/shard_map/all_to_all | solution.py:224
Sparse Core Ops, SparseCore 0:
  56.8 121.3 all-gather.1
  219.8 120.4 reduce-scatter.1

commit v12 on v10

--- a/solution.py
+++ b/solution.py
@@ -80,16 +80,24 @@
     store_count = key_store.shape[0]
     requests = new_row_lengths.shape[0]
     per_request = page_row.shape[0] // requests
-    ends = jnp.cumsum(new_row_lengths)
+    request_index = jnp.arange(requests, dtype=jnp.int32)
+    ends = jnp.sum(
+        jnp.where(request_index[None, :] <= request_index[:, None], new_row_lengths[None, :], 0),
+        axis=1,
+    )
     row_index = jnp.arange(row_count, dtype=jnp.int32)
-    owner = jnp.sum((row_index[:, None] >= ends[None, :]).astype(jnp.int32), axis=1)
+    owner_column = jnp.sum(
+        (row_index[:, None] >= ends[None, :]).astype(jnp.int32), axis=1, keepdims=True
+    )
+    owner_row = jnp.sum(
+        (row_index[None, :] >= ends[:, None]).astype(jnp.int32), axis=0, keepdims=True
+    )
     entry = jnp.arange(page_row.shape[0], dtype=jnp.int32)
     token_index = jnp.arange(store_count, dtype=jnp.int32)
     hit = page_row[:, None] == (token_index // PAGE)[None, :]
     token_entry = jnp.sum(jnp.where(hit, entry[:, None], 0), axis=0)
     token_request = token_entry // per_request
     position = (token_entry % per_request) * PAGE + token_index % PAGE
-    request_index = jnp.arange(requests, dtype=jnp.int32)
     limit = jnp.sum(
         jnp.where(
             token_request[None, :] == request_index[:, None], context_row_lengths[:, None], 0
@@ -125,8 +133,8 @@
         value_rows,
         hidden_rows,
         token_owner.reshape(1, store_count),
-        owner.reshape(row_count, 1),
-        owner.reshape(1, row_count),
+        owner_column,
+        owner_row,
     )
 
 
@@ -200,8 +208,12 @@
     entries = route_ids.reshape(-1)
     expert_range = jnp.arange(EXPERTS, dtype=jnp.int32)
     onehot = (entries[:, None] == expert_range[None, :]).astype(jnp.int32)
-    before = jnp.cumsum(onehot, axis=0) - onehot
-    slot_index = jnp.sum(before * onehot, axis=1)
+    entry_index = jnp.arange(entries.shape[0], dtype=jnp.int32)
+    slot_index = jnp.sum(
+        (entry_index[None, :] < entry_index[:, None]) & (entries[None, :] == entries[:, None]),
+        axis=1,
+        dtype=jnp.int32,
+    )
     target = entries * MOST + slot_index
     slots = jnp.arange(EXPERTS * MOST, dtype=jnp.int32)
     pick = target.reshape(row_count, top_count)[:, :, None] == slots[None, None, :]

time: 366 us -> 366 us (level)
  no operation moved by 1% of the time
where the time goes in v12:
time: 366 us; the launch traced here: 365 us
  waiting for transfers between devices  258 us (70%)
  Pallas kernels  55.5 us (15%)
  blocking collectives  23.2 us (6%)
  between operations  13.5 us (4%)
  other arithmetic  6.41 us (2%)
  starting transfers between devices  5.7 us (2%)
    all_gather x1, waiting for transfers between devices, per_device(): arrived_rows = lax.all_gather(arrived, 'sh', axis=0, tiled=True)  121 us
    reduce_scatter x1, waiting for transfers between devices, per_device(): summed = lax.psum_scatter(partial, 'sh', scatter_dimension=0, tiled=True)  121 us
    pallas_call x1, Pallas kernels, expert_ffn(): pl.pallas_call(ffn_kernel, grid=(count // tile,), in_specs=[pl.BlockSpec(...  36.1 us
    all_to_all x1, blocking collectives, per_device(): lax.all_to_all(outgoing, 'ex', split_axis=0, concat_axis=0, tiled=True)  23.2 us
    pallas_call x1, Pallas kernels, attend(): pl.pallas_call(attention_kernel, grid=(width // block,), in_specs=[column...  19.4 us
    all_to_all x1, waiting for transfers between devices, per_device(): lax.all_to_all(summed.reshape(EXPERTS, MOST, width), 'ex', split_axis=0,...  16 us
  transfers between devices with their start and end apart: 3, of which 3 were waited for; matrix products, arithmetic and copies ran while one was open for 0% of the time, Pallas kernels for 0%

profile of v12, /device:TPU:1, one launch (start us, length us, event | category | flops | bytes accessed | tf_op | source)
XLA Modules:
  0.0 365.1 jit_solution(16356746781050488977)
XLA Ops:
  6.5 0.0 copy-start
  6.5 0.0 all-gather.2.cloned.1.call-start
  6.5 0.8 select_reduce_fusion.3
  7.3 0.1 convert_reduce_fusion.2
  7.4 0.7 convert_reduce_fusion.1
  8.1 0.8 select_reduce_fusion
  8.8 0.7 copy.33.owner_ref
  9.6 0.7 select_reduce_fusion.1
  10.3 0.6 compare_select_fusion.token_owner_ref
  10.9 0.0 copy-start.3
  10.9 0.0 copy-start.2
  10.9 19.4 %shard_map.154 = f32[96,2304]{1,0:T(8,128)} custom-call(bf16[96,2304]{1,0:T(8,128)(2,1)} %query_ref.1, bf16[1024,2304]{1,0:T(8,128)(2,1)} %pool_key_ref.1, bf16[96,2304]{1,0:T(8,128)(2,1)} %new_key_ref.1, bf16[1024,2304]{1,0:T(8,128)(2,1)} %pool_value_ref.1, bf16[96,2304]{1,0:T(8,128)(2,1)} %new_value_ref.1, bf16[96,2304]{1,0:T(8,128)(2,1)} %hidden_ref.1, ...), custom_call_target="tpu_custom_call" | custom-call | tf_op jit(solution)/shard_map/pallas_call | solution.py:111
  30.3 0.0 copy-start.1
  30.3 1.4 multiply_reduce_fusion.1
  31.7 0.0 copy-done.3
  31.7 0.0 copy-done.2
  31.8 0.1 copy.34
  31.9 0.1 eq.82
  32.0 0.2 convert_reduce_fusion
  32.2 0.1 reduce_sum.107
  32.3 0.1 copy.35
  32.4 0.1 iota_compare_fusion
  32.5 0.0 copy-done.1
  32.6 0.5 convolution_convert_fusion
  33.1 23.2 %all_to_all.10 = bf16[8,32,2304]{2,1,0:T(8,128)(2,1)} all-to-all(bf16[8,32,2304]{2,1,0:T(8,128)(2,1)S(1)} %bitcast.37), channel_id=1, replica_groups=mesh['ex'=8,'sh'=16] {'ex'}, dimensions={0} | all-to-all | bytes 2359296 | tf_op jit(solution)/shard_map/all_to_all | solution.py:224
  56.3 0.0 all-gather.2.cloned.1.call-update
  56.4 0.0 reduce-scatter.2.cloned.1.call-start
  56.4 121.4 %all-gather.2.cloned.1.call-done.rows_ref = bf16[4096,2304]{1,0:T(8,128)(2,1)} async-done(((bf16[256,2304]{1,0:T(8,128)(2,1)}), bf16[4096,2304]{1,0:T(8,128)(2,1)}) %all-gather.2.cloned.1.call-update) | async-done | bytes 18874384 | tf_op jit(solution)/shard_map/all_gather | solution.py:227
  177.8 36.1 %shard_map.155 = bf16[4096,2304]{1,0:T(8,128)(2,1)} custom-call(bf16[4096,2304]{1,0:T(8,128)(2,1)} %all-gather.2.cloned.1.call-done.rows_ref, bf16[360,2304]{1,0:T(8,128)(2,1)} %bitcast.38, bf16[360,2304]{1,0:T(8,128)(2,1)} %bitcast.39, bf16[360,2304]{1,0:T(8,128)(2,1)} %bitcast.40), custom_call_target="tpu_custom_call" | custom-call | tf_op jit(solution)/shard_map/pallas_call | solution.py:157
  214.0 0.0 reduce-scatter.2.cloned.1.call-update
  214.0 120.6 %reduce-scatter.2.cloned.1.call-done = bf16[256,2304]{1,0:T(8,128)(2,1)} async-done(((bf16[4096,2304]{1,0:T(8,128)(2,1)}), bf16[256,2304]{1,0:T(8,128)(2,1)}) %reduce-scatter.2.cloned.1.call-update) | async-done | bytes 1179664 | tf_op jit(solution)/shard_map/reduce_scatter | solution.py:229
  334.6 0.0 copy-start.4
  334.6 5.7 %all-to-all-start.1 = ((bf16[8,32,2304]{2,1,0:T(8,128)(2,1)}), bf16[8,32,2304]{2,1,0:T(8,128)(2,1)S(1)}, u32[]{:S(2)}, u32[]{:S(2)}) async-start(bf16[8,32,2304]{2,1,0:T(8,128)(2,1)} %bitcast.41), calls=%async_computation.2 | async-start | bytes 2359296 | tf_op jit(solution)/shard_map/all_to_all | solution.py:230
  340.2 0.0 copy-done.4
  340.2 0.0 copy-done
  340.2 0.3 fusion.11
  340.5 0.1 select_reduce_fusion.2
  340.6 16.0 %all-to-all-done.1 = bf16[8,32,2304]{2,1,0:T(8,128)(2,1)S(1)} async-done(((bf16[8,32,2304]{2,1,0:T(8,128)(2,1)}), bf16[8,32,2304]{2,1,0:T(8,128)(2,1)S(1)}, u32[]{:S(2)}, u32[]{:S(2)}) %all-to-all-start.1) | async-done | bytes 1179680 | tf_op jit(solution)/shard_map/all_to_all | solution.py:230
  356.6 0.3 convolution_multiply_fusion.1
  356.9 0.4 multiply_reduce_fusion
  357.4 0.9 multiply_convert_fusion
  (10 shorter events, 0.1 us)
Async XLA Ops:
  6.5 333.7 %copy-start = (bf16[2304,8]{0,1:T(8,128)(2,1)S(1)}, bf16[2304,8]{0,1:T(8,128)(2,1)}, u32[]{:S(2)}) copy-start(bf16[2304,8]{0,1:T(8,128)(2,1)} %param.27) | copy-start | bytes 110596
  6.5 171.3 %all-gather.2.cloned.1.call-start = ((), (), s32[]{:S(2)}) async-start(), calls=%async_computation.3 | async-start | bytes 20054016 | tf_op jit(solution)/shard_map/all_gather | solution.py:227
  10.9 20.8 %copy-start.3 = (bf16[2304]{0:T(1024)(128)(2,1)S(1)}, bf16[2304]{0:T(1024)(128)(2,1)}, u32[]{:S(2)}) copy-start(bf16[2304]{0:T(1024)(128)(2,1)} %param.26) | copy-start | bytes 13828
  10.9 20.8 %copy-start.2 = (s32[96,2]{0,1:T(2,128)S(1)}, s32[96,2]{0,1:T(2,128)}, u32[]{:S(2)}) copy-start(s32[96,2]{0,1:T(2,128)} %param.25) | copy-start | bytes 2308
  30.3 2.2 copy-start.1
  56.4 278.2 %reduce-scatter.2.cloned.1.call-start = ((), (), s32[]{:S(2)}) async-start(), calls=%async_computation.4 | async-start | bytes 20054016 | tf_op jit(solution)/shard_map/reduce_scatter | solution.py:229
  334.6 5.7 %copy-start.4 = (bf16[2304]{0:T(1024)(128)(2,1)S(1)}, bf16[2304]{0:T(1024)(128)(2,1)}, u32[]{:S(2)}) copy-start(bf16[2304]{0:T(1024)(128)(2,1)} %param.31) | copy-start | bytes 13828
  334.6 22.0 %all-to-all-start.1 = ((bf16[8,32,2304]{2,1,0:T(8,128)(2,1)}), bf16[8,32,2304]{2,1,0:T(8,128)(2,1)S(1)}, u32[]{:S(2)}, u32[]{:S(2)}) async-start(bf16[8,32,2304]{2,1,0:T(8,128)(2,1)} %bitcast.41), calls=%async_computation.2 | async-start | bytes 2359296 | tf_op jit(solution)/shard_map/all_to_all | solution.py:230
Sparse Core Ops, SparseCore 0:
  56.5 121.3 all-gather.1
  214.1 120.3 reduce-scatter.1

commit v13 on v12

--- a/solution.py
+++ b/solution.py
@@ -34,11 +34,23 @@
 ):
     query = query_ref[...]
     rows = query.shape[0]
-    owner = owner_ref[...]
+    ends_row = owner_ref[...]
+    ends_column = owner_row_ref[...]
+    requests = ends_row.shape[1]
+    owner = jnp.sum(
+        (lax.broadcasted_iota(jnp.int32, (rows, requests), 0) >= ends_row).astype(jnp.int32),
+        axis=1,
+        keepdims=True,
+    )
+    owner_row = jnp.sum(
+        (lax.broadcasted_iota(jnp.int32, (requests, rows), 1) >= ends_column).astype(jnp.int32),
+        axis=0,
+        keepdims=True,
+    )
     pool_ok = owner == token_owner_ref[...]
     row_at = lax.broadcasted_iota(jnp.int32, (rows, rows), 0)
     col_at = lax.broadcasted_iota(jnp.int32, (rows, rows), 1)
-    new_ok = (owner == owner_row_ref[...]) & (col_at <= row_at)
+    new_ok = (owner == owner_row) & (col_at <= row_at)
     lane = lax.broadcasted_iota(jnp.int32, (1, query.shape[1]), 1)
     contract = (((1,), (1,)), ((), ()))
     total = hidden_ref[...].astype(jnp.float32)
@@ -86,12 +98,6 @@
         axis=1,
     )
     row_index = jnp.arange(row_count, dtype=jnp.int32)
-    owner_column = jnp.sum(
-        (row_index[:, None] >= ends[None, :]).astype(jnp.int32), axis=1, keepdims=True
-    )
-    owner_row = jnp.sum(
-        (row_index[None, :] >= ends[:, None]).astype(jnp.int32), axis=0, keepdims=True
-    )
     entry = jnp.arange(page_row.shape[0], dtype=jnp.int32)
     token_index = jnp.arange(store_count, dtype=jnp.int32)
     hit = page_row[:, None] == (token_index // PAGE)[None, :]
@@ -119,8 +125,8 @@
             column(row_count),
             column(row_count),
             whole((1, store_count)),
-            whole((row_count, 1)),
-            whole((1, row_count)),
+            whole((1, requests)),
+            whole((requests, 1)),
         ],
         out_specs=column(row_count),
         out_shape=jax.ShapeDtypeStruct((row_count, width), jnp.float32),
@@ -133,8 +139,8 @@
         value_rows,
         hidden_rows,
         token_owner.reshape(1, store_count),
-        owner_column,
-        owner_row,
+        ends.reshape(1, requests),
+        ends.reshape(requests, 1),
     )
 
 

time: 366 us -> 365 us (level)
  no operation moved by 1% of the time
where the time goes in v13:
time: 365 us; the launch traced here: 364 us
  waiting for transfers between devices  258 us (71%)
  Pallas kernels  55.6 us (15%)
  blocking collectives  23.2 us (6%)
  between operations  13.5 us (4%)
  starting transfers between devices  5.74 us (2%)
  other arithmetic  5.67 us (2%)
    all_gather x1, waiting for transfers between devices, per_device(): arrived_rows = lax.all_gather(arrived, 'sh', axis=0, tiled=True)  121 us
    reduce_scatter x1, waiting for transfers between devices, per_device(): summed = lax.psum_scatter(partial, 'sh', scatter_dimension=0, tiled=True)  121 us
    pallas_call x1, Pallas kernels, expert_ffn(): pl.pallas_call(ffn_kernel, grid=(count // tile,), in_specs=[pl.BlockSpec(...  36.2 us
    all_to_all x1, blocking collectives, per_device(): lax.all_to_all(outgoing, 'ex', split_axis=0, concat_axis=0, tiled=True)  23.2 us
    pallas_call x1, Pallas kernels, attend(): pl.pallas_call(attention_kernel, grid=(width // block,), in_specs=[column...  19.4 us
    all_to_all x1, waiting for transfers between devices, per_device(): lax.all_to_all(summed.reshape(EXPERTS, MOST, width), 'ex', split_axis=0,...  16 us
  transfers between devices with their start and end apart: 3, of which 3 were waited for; matrix products, arithmetic and copies ran while one was open for 0% of the time, Pallas kernels for 0%

profile of v13, /device:TPU:1, one launch (start us, length us, event | category | flops | bytes accessed | tf_op | source)
XLA Modules:
  0.0 364.4 jit_solution(3151305372374948657)
XLA Ops:
  6.5 0.0 copy-start
  6.5 0.0 all-gather.2.cloned.1.call-start
  6.5 0.8 select_reduce_fusion
  7.3 0.8 select_reduce_fusion.3
  8.1 0.0 copy-start.5
  8.1 0.7 copy.33.owner_row_ref
  8.8 0.7 select_reduce_fusion.1
  9.5 0.6 compare_select_fusion.token_owner_ref
  10.2 0.0 copy-done.5
  10.2 0.0 copy-start.3
  10.2 0.0 copy-start.2
  10.2 19.4 %shard_map.154 = f32[96,2304]{1,0:T(8,128)} custom-call(bf16[96,2304]{1,0:T(8,128)(2,1)} %query_ref.1, bf16[1024,2304]{1,0:T(8,128)(2,1)} %pool_key_ref.1, bf16[96,2304]{1,0:T(8,128)(2,1)} %new_key_ref.1, bf16[1024,2304]{1,0:T(8,128)(2,1)} %pool_value_ref.1, bf16[96,2304]{1,0:T(8,128)(2,1)} %new_value_ref.1, bf16[96,2304]{1,0:T(8,128)(2,1)} %hidden_ref.1, ...), custom_call_target="tpu_custom_call" | custom-call | tf_op jit(solution)/shard_map/pallas_call | solution.py:117
  29.6 0.0 copy-start.1
  29.6 1.4 multiply_reduce_fusion.1
  31.0 0.0 copy-done.3
  31.0 0.0 copy-done.2
  31.0 0.1 copy.34
  31.1 0.1 eq.82
  31.3 0.2 convert_reduce_fusion
  31.5 0.1 reduce_sum.87
  31.6 0.1 copy.35
  31.7 0.1 iota_compare_fusion
  31.8 0.0 copy-done.1
  31.8 0.5 convolution_convert_fusion
  32.4 23.2 %all_to_all.10 = bf16[8,32,2304]{2,1,0:T(8,128)(2,1)} all-to-all(bf16[8,32,2304]{2,1,0:T(8,128)(2,1)S(1)} %bitcast.37), channel_id=1, replica_groups=mesh['ex'=8,'sh'=16] {'ex'}, dimensions={0} | all-to-all | bytes 2359296 | tf_op jit(solution)/shard_map/all_to_all | solution.py:230
  55.6 0.0 all-gather.2.cloned.1.call-update
  55.6 0.0 reduce-scatter.2.cloned.1.call-start
  55.7 121.4 %all-gather.2.cloned.1.call-done.rows_ref = bf16[4096,2304]{1,0:T(8,128)(2,1)} async-done(((bf16[256,2304]{1,0:T(8,128)(2,1)}), bf16[4096,2304]{1,0:T(8,128)(2,1)}) %all-gather.2.cloned.1.call-update) | async-done | bytes 18874384 | tf_op jit(solution)/shard_map/all_gather | solution.py:233
  177.1 36.2 %shard_map.155 = bf16[4096,2304]{1,0:T(8,128)(2,1)} custom-call(bf16[4096,2304]{1,0:T(8,128)(2,1)} %all-gather.2.cloned.1.call-done.rows_ref, bf16[360,2304]{1,0:T(8,128)(2,1)} %bitcast.38, bf16[360,2304]{1,0:T(8,128)(2,1)} %bitcast.39, bf16[360,2304]{1,0:T(8,128)(2,1)} %bitcast.40), custom_call_target="tpu_custom_call" | custom-call | tf_op jit(solution)/shard_map/pallas_call | solution.py:163
  213.2 0.0 reduce-scatter.2.cloned.1.call-update
  213.3 120.5 %reduce-scatter.2.cloned.1.call-done = bf16[256,2304]{1,0:T(8,128)(2,1)} async-done(((bf16[4096,2304]{1,0:T(8,128)(2,1)}), bf16[256,2304]{1,0:T(8,128)(2,1)}) %reduce-scatter.2.cloned.1.call-update) | async-done | bytes 1179664 | tf_op jit(solution)/shard_map/reduce_scatter | solution.py:235
  333.8 0.0 copy-start.4
  333.8 5.7 %all-to-all-start.1 = ((bf16[8,32,2304]{2,1,0:T(8,128)(2,1)}), bf16[8,32,2304]{2,1,0:T(8,128)(2,1)S(1)}, u32[]{:S(2)}, u32[]{:S(2)}) async-start(bf16[8,32,2304]{2,1,0:T(8,128)(2,1)} %bitcast.41), calls=%async_computation.2 | async-start | bytes 2359296 | tf_op jit(solution)/shard_map/all_to_all | solution.py:236
  339.5 0.0 copy-done.4
  339.5 0.0 copy-done
  339.5 0.3 fusion.11
  339.8 0.1 select_reduce_fusion.2
  339.9 16.0 %all-to-all-done.1 = bf16[8,32,2304]{2,1,0:T(8,128)(2,1)S(1)} async-done(((bf16[8,32,2304]{2,1,0:T(8,128)(2,1)}), bf16[8,32,2304]{2,1,0:T(8,128)(2,1)S(1)}, u32[]{:S(2)}, u32[]{:S(2)}) %all-to-all-start.1) | async-done | bytes 1179680 | tf_op jit(solution)/shard_map/all_to_all | solution.py:236
  355.9 0.3 convolution_multiply_fusion.1
  356.2 0.4 multiply_reduce_fusion
  356.6 0.9 multiply_convert_fusion
  (10 shorter events, 0.1 us)
Async XLA Ops:
  6.5 333.0 %copy-start = (bf16[2304,8]{0,1:T(8,128)(2,1)S(1)}, bf16[2304,8]{0,1:T(8,128)(2,1)}, u32[]{:S(2)}) copy-start(bf16[2304,8]{0,1:T(8,128)(2,1)} %param.27) | copy-start | bytes 110596
  6.5 170.6 %all-gather.2.cloned.1.call-start = ((), (), s32[]{:S(2)}) async-start(), calls=%async_computation.3 | async-start | bytes 20054016 | tf_op jit(solution)/shard_map/all_gather | solution.py:233
  8.1 2.1 copy-start.5
  10.2 20.8 %copy-start.3 = (bf16[2304]{0:T(1024)(128)(2,1)S(1)}, bf16[2304]{0:T(1024)(128)(2,1)}, u32[]{:S(2)}) copy-start(bf16[2304]{0:T(1024)(128)(2,1)} %param.26) | copy-start | bytes 13828
  10.2 20.9 %copy-start.2 = (s32[96,2]{0,1:T(2,128)S(1)}, s32[96,2]{0,1:T(2,128)}, u32[]{:S(2)}) copy-start(s32[96,2]{0,1:T(2,128)} %param.25) | copy-start | bytes 2308
  29.6 2.2 copy-start.1
  55.6 278.2 %reduce-scatter.2.cloned.1.call-start = ((), (), s32[]{:S(2)}) async-start(), calls=%async_computation.4 | async-start | bytes 20054016 | tf_op jit(solution)/shard_map/reduce_scatter | solution.py:235
  333.8 5.7 %copy-start.4 = (bf16[2304]{0:T(1024)(128)(2,1)S(1)}, bf16[2304]{0:T(1024)(128)(2,1)}, u32[]{:S(2)}) copy-start(bf16[2304]{0:T(1024)(128)(2,1)} %param.31) | copy-start | bytes 13828
  333.8 22.1 %all-to-all-start.1 = ((bf16[8,32,2304]{2,1,0:T(8,128)(2,1)}), bf16[8,32,2304]{2,1,0:T(8,128)(2,1)S(1)}, u32[]{:S(2)}, u32[]{:S(2)}) async-start(bf16[8,32,2304]{2,1,0:T(8,128)(2,1)} %bitcast.41), calls=%async_computation.2 | async-start | bytes 2359296 | tf_op jit(solution)/shard_map/all_to_all | solution.py:236
Sparse Core Ops, SparseCore 0:
  55.7 121.3 all-gather.1
  213.4 120.3 reduce-scatter.1
